TPU v7x, 32 devices: a whole 2x2x4 slice. The times are simulated.
32 devices in a mesh: wl: 2 (over y), row: 16 (over z, x, core).
Axes of the slice: x: 2, y: 2, z: 4, core: 2. Of those that a mesh axis runs over, the one named last changes fastest.
Arguments:
- scenes: float32 [2, 4096, 4096], P(None, 'row'), may hold values from -6 to 6
- optics: bfloat16 [4, 2, 4096, 4096], P('wl', None, 'row'), may hold values from -4 to 4
- weights: float32 [4, 2], replicated, may hold values from 0.1 to 2
Outputs:
- blurred: float32 [2, 4096, 4096], P(None, 'row', 'wl')
All inputs are finite; a program needn't handle non-finite values.
Results may differ from a plain program's by a relative error of at most 0.0003.
Values may be sent and summed in bfloat16 or wider, within the bound.
No kernel may reach another device: no remote copies, remote signals or barrier semaphores. Data moves between devices by JAX's collectives and lax.ppermute only.
A program may use at most 128 MiB of HBM per device.

v0:
```python
import math

import jax
import jax.numpy as jnp
from jax import lax
from jax.sharding import PartitionSpec as P

PRECISE = lax.Precision.HIGHEST
NARROW = 32


def phase(left_ids, right_ids, modulus, orient):
    turns = (left_ids * right_ids % modulus).astype(jnp.float32)
    angles = turns * (orient * 2.0 * math.pi / modulus)
    return (jnp.cos(angles), jnp.sin(angles))


def ids(count):
    return jnp.arange(count, dtype=jnp.int32)


def cblock(cos_part, sin_part):
    return jnp.stack([jnp.stack([cos_part, -sin_part]), jnp.stack([sin_part, cos_part])])


def small_tables(out_count, in_count, modulus, orients):
    tables = []
    for orient in orients:
        cos_part, sin_part = phase(ids(out_count)[:, None], ids(in_count)[None, :], modulus, orient)
        tables.append(cblock(cos_part, sin_part))
    return jnp.stack(tables)


def twist(values, axis_e, cos_part, sin_part):
    real = jnp.take(values, 0, axis=axis_e)
    imag = jnp.take(values, 1, axis=axis_e)
    return jnp.stack([real * cos_part - imag * sin_part, real * sin_part + imag * cos_part], axis_e)


def canon_to_groups(canon, group_count):
    mcount, span_c = canon.shape[0], canon.shape[-1] // 2
    mid = canon.shape[1:-1]
    if group_count == mcount:
        return canon
    span = mcount * span_c // group_count
    flat = jnp.moveaxis(canon.reshape((mcount,) + mid + (2, span_c)), 0, -2)
    flat = flat.reshape(mid + (2, group_count, span))
    return jnp.moveaxis(flat, -2, 0).reshape((group_count,) + mid + (2 * span,))


def groups_to_canon(grouped, mcount, axis_g):
    group_count = grouped.shape[axis_g]
    if group_count == mcount:
        return grouped
    moved = jnp.moveaxis(grouped, axis_g, 0)
    mid = moved.shape[1:-1]
    span = moved.shape[-1] // 2
    span_c = group_count * span // mcount
    flat = jnp.moveaxis(moved.reshape((group_count,) + mid + (2, span)), 0, -2)
    flat = flat.reshape(mid + (2, mcount, span_c))
    canon = jnp.moveaxis(flat, -2, 0).reshape((mcount,) + mid + (2 * span_c,))
    return jnp.moveaxis(canon, 0, axis_g)


def forward_rows(scenes):
    rows_here, length = scenes.shape[1], scenes.shape[2]
    across = length // NARROW
    half_k = across // 2
    grid = scenes.reshape((2, rows_here, NARROW, across))
    first_tab = jnp.transpose(small_tables(NARROW, NARROW, NARROW, (-1.0, 1.0)), (0, 3, 1, 2, 4))
    first = jnp.einsum("oaedb,drbn->oaern", first_tab, grid, precision=PRECISE)
    tw_cos, tw_sin = [], []
    for orient in (-1.0, 1.0):
        cos_part, sin_part = phase(ids(NARROW)[:, None], ids(across)[None, :], length, orient)
        tw_cos.append(cos_part)
        tw_sin.append(sin_part)
    tw_cos = jnp.stack(tw_cos)[:, :, None, :]
    tw_sin = jnp.stack(tw_sin)[:, :, None, :]
    turned = twist(first, 2, tw_cos, tw_sin)
    second_tab = jnp.transpose(small_tables(half_k, across, across, (-1.0, 1.0)), (0, 2, 4, 1, 3))
    second = jnp.einsum("oaern,oenfk->oarfk", turned, second_tab, precision=PRECISE)
    signs = 1.0 - 2.0 * (ids(across) % 2).astype(jnp.float32)
    nyquist = jnp.einsum("ern,n->er", first[0, 0], signs, precision=PRECISE)
    per_block = across // NARROW
    mcount = half_k // per_block
    blocks = second.reshape((2, NARROW, rows_here, 2, mcount, per_block))
    canon = jnp.transpose(blocks, (4, 3, 2, 0, 5, 1)).reshape((mcount, 2, rows_here, 2 * across))
    canon = canon.at[0, :, :, across].set(nyquist)
    return canon


def forward_cols(columns):
    length, width = columns.shape[1], columns.shape[2]
    across = length // NARROW
    grid = columns.reshape((2, NARROW, across, width))
    first_tab = jnp.transpose(small_tables(NARROW, NARROW, NARROW, (-1.0, 1.0)), (0, 3, 1, 2, 4))
    first = jnp.einsum("oafeb,ebnj->oafnj", first_tab, grid, precision=PRECISE)
    tw_cos, tw_sin = [], []
    for orient in (-1.0, 1.0):
        cos_part, sin_part = phase(ids(NARROW)[:, None], ids(across)[None, :], length, orient)
        tw_cos.append(cos_part)
        tw_sin.append(sin_part)
    tw_cos = jnp.stack(tw_cos)[:, :, :, None]
    tw_sin = jnp.stack(tw_sin)[:, :, :, None]
    turned = twist(first, 2, tw_cos, tw_sin)
    second_tab = small_tables(across, across, across, (-1.0, 1.0))
    second = jnp.einsum("ofekn,oaenj->ofkaj", second_tab, turned, precision=PRECISE)
    return second.reshape((2, 2, length, width))


def inverse_cols(combined):
    length, width = combined.shape[1], combined.shape[2]
    across = length // NARROW
    grid = combined.reshape((2, NARROW, across, width))
    first_tab = jnp.transpose(small_tables(NARROW, NARROW, NARROW, (1.0,))[0], (2, 0, 1, 3))
    first = jnp.einsum("afeb,ebnj->afnj", first_tab, grid, precision=PRECISE)
    cos_part, sin_part = phase(ids(NARROW)[:, None], ids(across)[None, :], length, 1.0)
    turned = twist(first, 1, cos_part[:, :, None], sin_part[:, :, None])
    second_tab = jnp.transpose(small_tables(across, across, across, (1.0,))[0], (0, 2, 1, 3))
    second = jnp.einsum("fken,aenj->fkaj", second_tab, turned, precision=PRECISE)
    return second.reshape((2, length, width))


def inverse_rows(canon, length, scale):
    mcount, rows_here, width = canon.shape[1], canon.shape[2], canon.shape[3]
    across = width // 2
    first_tab = jnp.transpose(small_tables(NARROW, mcount, NARROW, (1.0, -1.0)), (0, 3, 1, 2, 4))
    first = jnp.einsum("oafem,emRj->oafRj", first_tab, canon, precision=PRECISE)
    lower = first[0, :, :, :, :across]
    upper = first[1, :, :, :, across:]
    flip_gain = -2.0 * (ids(NARROW) % 2).astype(jnp.float32)
    fix = flip_gain[:, None, None] * canon[:, 0, :, across][None]
    lane0 = (ids(across) == 0)[None, None, None, :]
    upper = jnp.where(lane0, upper + fix[..., None], upper)
    cos_up, sin_up = phase(ids(NARROW)[:, None], ids(across)[None, :], length, 1.0)
    cos_dn, sin_dn = phase(ids(NARROW)[:, None], ids(across)[None, :], length, -1.0)
    lower = twist(lower, 1, cos_up[:, None, :], sin_up[:, None, :])
    upper = twist(upper, 1, cos_dn[:, None, :], sin_dn[:, None, :])
    tabs = small_tables(across, across, across, (1.0, -1.0)) * scale
    tabs = jnp.transpose(tabs, (0, 2, 4, 1, 3))
    out = jnp.einsum("aeRu,eufk->aRfk", lower, tabs[0], precision=PRECISE)
    out = out + jnp.einsum("aeRu,eufk->aRfk", upper, tabs[1], precision=PRECISE)
    return jnp.transpose(out, (2, 1, 3, 0)).reshape((2, rows_here, length))


def pair_optics(optics):
    length = optics.shape[-1]
    across = length // NARROW
    half = length // 2
    mcount = half // across
    block = [lax.slice_in_dim(optics, across * i, across * (i + 1), axis=3) for i in range(NARROW)]
    windows = []
    for m in range(mcount):
        second = block[(half // across) if m == 0 else (NARROW - m)]
        windows.append(jnp.concatenate([block[NARROW - 1 - m], second], -1))
    windows = jnp.stack(windows)
    src = ids(2 * across)[:, None]
    dst = ids(across)[None, :]
    picker = jnp.logical_or(
        jnp.logical_and(src == across - dst, dst > 0), jnp.logical_and(src == across, dst == 0)
    ).astype(optics.dtype)
    mirrored = jnp.einsum("mwcpv,vu->mwcpu", windows, picker, preferred_element_type=jnp.float32)
    lower = jnp.stack(block[:mcount])
    return jnp.concatenate([lower, mirrored.astype(optics.dtype)], -1)


def local(scenes, optics, weights):
    row_count = lax.axis_size("row")
    length = scenes.shape[2]
    across = length // NARROW
    norm_factor = 1.0 / (float(length) * float(length))
    wl_index = lax.axis_index("wl")
    local_waves = optics.shape[0]
    weight_rows = lax.dynamic_slice_in_dim(weights, wl_index * local_waves, local_waves, 0)
    first_row = lax.axis_index("row") == 0

    canon = forward_rows(scenes)
    mcount = canon.shape[0]
    sent = canon_to_groups(canon, row_count)
    got = lax.all_to_all(sent, "row", split_axis=0, concat_axis=2, tiled=True)[0]
    spec = forward_cols(got)

    optic_canon = pair_optics(optics)
    optic_sent = canon_to_groups(optic_canon, row_count)
    optic_got = lax.all_to_all(optic_sent, "row", split_axis=0, concat_axis=3, tiled=True)[0]

    width = spec.shape[-1]
    span = width // 2
    lane_ids = ids(width)
    itself = jnp.logical_and(first_row, lane_ids % span == 0)
    direct = spec[0]
    flipped = spec[1]
    swapped = jnp.concatenate([flipped[..., span:], flipped[..., :span]], -1)
    partner = jnp.where(itself, flipped, swapped)
    mirror_real = partner[0]
    mirror_imag = -partner[1]
    even_real = 0.5 * (direct[0] + mirror_real)
    even_imag = 0.5 * (direct[1] + mirror_imag)
    odd_real = 0.5 * (direct[0] - mirror_real)
    odd_imag = 0.5 * (direct[1] - mirror_imag)
    combined_real = jnp.zeros_like(even_real)
    combined_imag = jnp.zeros_like(even_imag)
    for colour in range(local_waves):
        mixed_real = weight_rows[colour, 0] * even_real + weight_rows[colour, 1] * odd_real
        mixed_imag = weight_rows[colour, 0] * even_imag + weight_rows[colour, 1] * odd_imag
        resp_real = optic_got[colour, 0].astype(jnp.float32)
        resp_imag = optic_got[colour, 1].astype(jnp.float32)
        combined_real = combined_real + resp_real * mixed_real - resp_imag * mixed_imag
        combined_imag = combined_imag + resp_real * mixed_imag + resp_imag * mixed_real

    back = inverse_cols(jnp.stack([combined_real, combined_imag]))
    rows_here = length // row_count
    back = back.reshape((2, row_count, rows_here, width))
    returned = lax.all_to_all(back, "row", split_axis=1, concat_axis=1, tiled=True)
    returned = groups_to_canon(returned, mcount, 1)
    result_image = inverse_rows(returned, length, norm_factor)
    return lax.psum_scatter(result_image, "wl", scatter_dimension=2, tiled=True)


def solution(mesh):
    in_specs = (P(None, "row", None), P("wl", None, "row", None), P())
    out_specs = P(None, "row", "wl")
    return jax.shard_map(local, mesh=mesh, in_specs=in_specs, out_specs=out_specs, check_vma=False)
```

profile of v0, /device:TPU:10, one launch (start us, length us, event | category | flops | bytes accessed | tf_op | source)
XLA Modules:
  0.0 970.3 jit_solution(3809347830896810424)
XLA Ops:
  13.8 16.4 %fusion.22 = f32[2,32,2,256,128]{4,1,3,2,0:T(8,128)} fusion(f32[1,2,2,32,32]{4,3,2,1,0:T(8,128)S(1)} %fusion.68, f32[1,2,2,32,32]{4,3,2,1,0:T(8,128)S(1)} %maximum_bitcast_fusion.22, f32[2,256,32,128]{3,2,1,0:T(8,128)S(1)} %bitcast.441), kind=kOutput, calls=%fused_computation.42 | convolution fusion | flops 3221233664 | bytes 25198592 | tf_op jit(solution)/shard_map/oaedb,drbn->oaern/dot_general | solution.py:71
  32.0 10.6 %subtract_bitcast_fusion.1 = (f32[2,32,1,256,128]{4,1,3,0,2:T(8,128)}, f32[2,32,1,256,128]{4,1,3,0,2:T(8,128)}) fusion(f32[2,32,2,256,128]{4,1,3,2,0:T(8,128)} %fusion.22, f32[2,32,128]{2,1,0:T(8,128)S(1)} %pad_maximum_fusion.10, f32[2,32,128]{2,1,0:T(8,128)S(1)} %pad_maximum_fusion.9), kind=kLoop, calls=%fused_computation.40 | loop fusion | flops 12582912 | bytes 33619968 | tf_op jit(solution)/shard_map/stack | solution.py:37
  42.6 6.8 maximum_bitcast_fusion
  49.4 26.0 %fusion.38 = f32[2,32,256,2,64]{2,4,3,1,0:T(8,128)} fusion(f32[2,32,2,256,128,1]{4,1,3,0,2,5:T(8,128)S(1)} %maximum_bitcast_fusion, f32[1,2,2,64,128]{4,3,2,1,0:T(8,128)S(1)} %maximum_bitcast_fusion.19, f32[1,2,2,64,128]{4,3,2,1,0:T(8,128)S(1)} %maximum_bitcast_fusion.18), kind=kOutput, calls=%fused_computation.81 | convolution fusion | flops 6442516480 | bytes 25427968 | tf_op jit(solution)/shard_map/oaern,oenfk->oarfk/dot_general | solution.py:81
  75.4 10.1 %reshape.810 = f32[2,32,256,2,16,4]{2,5,4,3,1,0:T(4,128)} reshape(f32[2,32,256,2,64]{2,4,3,1,0:T(8,128)} %fusion.38) | data formatting | bytes 16777216 | tf_op jit(solution)/shard_map/reshape | solution.py:86
  85.6 8.2 copy.146
  101.8 6.2 all-to-all-start.1
  145.2 7.8 pad_maximum_fusion
  153.1 137.2 %all-to-all-done.1 = f32[16,2,256,256]{2,3,1,0:T(8,128)} async-done(((f32[16,2,256,256]{2,3,1,0:T(8,128)}), f32[16,2,256,256]{2,3,1,0:T(8,128)}, u32[]{:S(2)}, u32[]{:S(2)}) %all-to-all-start.1) | async-done | bytes 8388640 | tf_op jit(solution)/shard_map/all_to_all | solution.py:180
  290.2 5.4 all-to-all-start
  304.0 8.7 copy.148
  312.8 21.8 %fusion.19 = f32[2,32,2,128,256]{4,1,3,2,0:T(8,128)S(1)} fusion(f32[2,32,128,256,1,1]{3,2,1,0,5,4:T(8,128)} %bitcast.444, f32[1,2,2,32,32]{4,3,2,1,0:T(8,128)S(1)} %copy-done.19, f32[1,2,2,32,32]{4,3,2,1,0:T(8,128)S(1)} %copy-done.17), kind=kOutput, calls=%fused_computation.41 | convolution fusion | flops 3221233664 | bytes 25198592 | tf_op jit(solution)/shard_map/oafeb,ebnj->oafnj/dot_general | solution.py:97
  334.6 5.6 subtract_bitcast_fusion
  340.2 5.5 maximum_bitcast_fusion.1
  345.7 24.8 %fusion.23 = f32[2,2,128,32,256]{4,2,3,1,0:T(8,128)S(1)} fusion(f32[2,32,2,128,256,1]{4,1,3,0,2,5:T(8,128)S(1)} %maximum_bitcast_fusion.1, f32[1,2,2,128,128]{4,3,2,1,0:T(8,128)} %fusion.48, f32[1,2,2,128,128]{4,3,2,1,0:T(8,128)} %maximum_bitcast_fusion.11), kind=kOutput, calls=%fused_computation.43 | convolution fusion | flops 12885032960 | bytes 34078720 | tf_op jit(solution)/shard_map/ofekn,oaenj->ofkaj/dot_general | solution.py:107
  370.6 5.8 copy-done.2
  380.8 96.9 %all-to-all-done = bf16[16,2,2,256,256]{3,4,2,1,0:T(8,128)(2,1)} async-done(((bf16[16,2,2,256,256]{3,4,2,1,0:T(8,128)(2,1)}), bf16[16,2,2,256,256]{3,4,2,1,0:T(8,128)(2,1)}, u32[]{:S(2)}, u32[]{:S(2)}) %all-to-all-start) | async-done | bytes 8388640 | tf_op jit(solution)/shard_map/all_to_all | solution.py:185
  477.7 11.6 %copy.142 = bf16[1,2,2,16,256,256]{5,4,3,2,1,0:T(8,128)(2,1)} copy(bf16[1,2,2,16,256,256]{4,5,2,1,3,0:T(8,128)(2,1)} %bitcast.54) | data formatting | bytes 16777216 | tf_op jit(solution)/shard_map/all_to_all | solution.py:185
  498.9 6.7 copy.154
  509.7 6.6 maximum_select_fusion
  516.6 8.0 fusion.28
  529.5 7.7 fusion.37
  540.4 11.9 %fusion.32 = f32[2,128,32,256]{3,1,2,0:T(8,128)S(1)} fusion(f32[32,2,128,256]{3,0,2,1:T(8,128)S(1)} %pad_maximum_fusion.1, f32[1,2,128,128]{3,2,1,0:T(8,128)S(1)} %copy-done.8, f32[1,2,128,128]{3,2,1,0:T(8,128)S(1)} %get-tuple-element.149), kind=kOutput, calls=%fused_computation.79 | convolution fusion | flops 6442516480 | bytes 17039360 | tf_op jit(solution)/shard_map/fken,aenj->fkaj/dot_general | solution.py:120
  557.1 8.1 copy.163
  571.0 181.7 %all-to-all-done.2 = f32[2,16,256,256]{3,0,2,1:T(2,128)} async-done(((f32[2,16,256,256]{3,0,2,1:T(2,128)}), f32[2,16,256,256]{3,0,2,1:T(2,128)}, u32[]{:S(2)}, u32[]{:S(2)}) %all-to-all-start.2) | async-done | bytes 8388640 | tf_op jit(solution)/shard_map/all_to_all | solution.py:214
  753.7 36.2 %convolution_bitcast_fusion = f32[2,32,2,256,256]{4,1,3,2,0:T(8,128)} fusion(f32[2,16,256,256,1,1]{3,0,2,1,5,4:T(2,128)} %bitcast.140, f32[2,32,2,2,16,1]{1,4,3,5,2,0:T(8,128)S(1)} %maximum_bitcast_fusion.39), kind=kOutput, calls=%fused_computation.6 | convolution fusion | flops 3221225472 | bytes 41959424 | tf_op jit(solution)/shard_map/oafem,emRj->oafRj/dot_general | solution.py:128
  794.5 6.8 add_select_fusion
  813.5 12.5 %fusion.9 = f32[32,256,2,128,1]{1,3,4,2,0:T(8,128)S(1)} fusion(f32[32,2,256,128,1]{3,0,2,1,4:T(8,128)S(1)} %maximum_bitcast_fusion.5, f32[2,2,128,2,128]{2,4,1,3,0:T(8,128)S(1)} %fusion.44), kind=kOutput, calls=%fused_computation.27 | convolution fusion | flops 6442450944 | bytes 17039360 | tf_op jit(solution)/shard_map/aeRu,eufk->aRfk/dot_general | solution.py:142
  829.8 16.9 %fusion.8 = f32[2,256,128,32]{1,2,0,3:T(8,128)} fusion(f32[32,256,2,128,1]{1,3,4,2,0:T(8,128)S(1)} %fusion.9, f32[32,2,256,128,1]{3,0,2,1,4:T(8,128)S(1)} %maximum_bitcast_fusion.4, f32[2,2,128,2,128]{2,4,1,3,0:T(8,128)S(1)} %fusion.44), kind=kOutput, calls=%fused_computation.26 | convolution fusion | flops 6444548096 | bytes 25427968 | tf_op jit(solution)/shard_map/aeRu,eufk->aRfk/dot_general | solution.py:141
  846.7 11.6 %copy.168 = f32[2,256,128,32]{1,3,2,0:T(8,128)} copy(f32[2,256,128,32]{1,2,0,3:T(8,128)} %fusion.8) | data formatting | bytes 16777216 | tf_op jit(solution)/shard_map/add | solution.py:142
  858.3 99.4 %reduce-scatter.2.cloned.1.call-done = f32[2,256,2048]{1,2,0:T(8,128)} async-done(((f32[2,256,4096]{1,2,0:T(8,128)}), f32[2,256,2048]{1,2,0:T(8,128)}) %reduce-scatter.2.cloned.1.call-update) | async-done | bytes 4194320 | tf_op jit(solution)/shard_map/reduce_scatter | solution.py:217
  957.7 5.3 copy.169
  (207 shorter events, 117.8 us)
Async XLA Ops:
  6.5 289.3 %copy-start = (f32[4,2]{0,1:T(2,128)S(1)}, f32[4,2]{0,1:T(2,128)}, u32[]{:S(2)}) copy-start(f32[4,2]{0,1:T(2,128)} %param.23) | copy-start | bytes 100
  13.7 16.4 %copy-start.16 = (f32[1,2,2,32,32]{4,3,2,1,0:T(8,128)}, f32[1,2,2,32,32]{4,3,2,1,0:T(8,128)S(1)}, u32[]{:S(2)}) copy-start(f32[1,2,2,32,32]{4,3,2,1,0:T(8,128)S(1)} %maximum_bitcast_fusion.22) | copy-start | bytes 49156
  13.7 16.4 %copy-start.20 = (f32[1,2,32,32]{3,2,1,0:T(8,128)}, f32[1,2,32,32]{3,2,1,0:T(8,128)S(1)}, u32[]{:S(2)}) copy-start(f32[1,2,32,32]{3,2,1,0:T(8,128)S(1)} %get-tuple-element.157) | copy-start | bytes 24580
  13.7 16.4 %copy-start.22 = (f32[1,2,32,32]{3,2,1,0:T(8,128)}, f32[1,2,32,32]{3,2,1,0:T(8,128)S(1)}, u32[]{:S(2)}) copy-start(f32[1,2,32,32]{3,2,1,0:T(8,128)S(1)} %get-tuple-element.158) | copy-start | bytes 24580
  13.7 16.4 %copy-start.18 = (f32[1,2,2,32,32]{4,3,2,1,0:T(8,128)}, f32[1,2,2,32,32]{4,3,2,1,0:T(8,128)S(1)}, u32[]{:S(2)}) copy-start(f32[1,2,2,32,32]{4,3,2,1,0:T(8,128)S(1)} %fusion.68) | copy-start | bytes 49156
  85.6 8.6 copy-start.32
  101.8 188.4 %all-to-all-start.1 = ((f32[16,2,256,256]{2,3,1,0:T(8,128)}), f32[16,2,256,256]{2,3,1,0:T(8,128)}, u32[]{:S(2)}, u32[]{:S(2)}) async-start(f32[16,2,256,256]{2,3,1,0:T(8,128)} %scatter.4), calls=%async_computation.1 | async-start | bytes 16777216 | tf_op jit(solution)/shard_map/all_to_all | solution.py:180
  118.0 12.4 %copy-start.9 = (bf16[2,2,256,128]{2,3,1,0:T(8,128)(2,1)S(1)}, bf16[2,2,256,128]{2,3,1,0:T(8,128)(2,1)}, u32[]{:S(2)}) copy-start(bf16[2,2,256,128]{2,3,1,0:T(8,128)(2,1)} %copy.223) | copy-start | bytes 786436
  118.9 11.5 %copy-start.10 = (bf16[2,2,256,128]{2,3,1,0:T(8,128)(2,1)S(1)}, bf16[2,2,256,128]{2,3,1,0:T(8,128)(2,1)}, u32[]{:S(2)}) copy-start(bf16[2,2,256,128]{2,3,1,0:T(8,128)(2,1)} %copy.222) | copy-start | bytes 786436
  119.7 10.6 %copy-start.11 = (bf16[2,2,256,128]{2,3,1,0:T(8,128)(2,1)S(1)}, bf16[2,2,256,128]{2,3,1,0:T(8,128)(2,1)}, u32[]{:S(2)}) copy-start(bf16[2,2,256,128]{2,3,1,0:T(8,128)(2,1)} %copy.221) | copy-start | bytes 786436
  120.6 9.7 copy-start.12
  121.5 8.8 copy-start.13
  122.3 7.9 copy-start.14
  123.2 7.0 copy-start.15
  124.8 15.6 %copy-start.30 = (pred[128]{0:T(512)(128)(4,1)}, pred[128]{0:T(512)(128)(4,1)S(1)}, u32[]{:S(2)}) copy-start(pred[128]{0:T(512)(128)(4,1)S(1)} %get-tuple-element.169) | copy-start | bytes 388
  124.8 14.9 %slice-start.3 = ((s8[8388608]{0:T(1024)(128)(4,1)}), s8[4194304]{0:T(1024)(128)(4,1)S(1)}, s32[]{:S(2)}) async-start(s8[8388608]{0:T(1024)(128)(4,1)} %bitcast.452), calls=%async_computation.8 | async-start | bytes 8388608
  130.4 9.4 slice-start.4
  130.4 9.9 %copy-start.4 = (bf16[16,2,2,256,128]{3,4,2,1,0:T(8,128)(2,1)}, bf16[16,2,2,256,128]{3,4,2,1,0:T(8,128)(2,1)S(1)}, u32[]{:S(2)}) copy-start(bf16[16,2,2,256,128]{3,4,2,1,0:T(8,128)(2,1)S(1)} %bitcast_dynamic-update-slice_fusion.15) | copy-start | bytes 12582916
  290.2 187.4 %all-to-all-start = ((bf16[16,2,2,256,256]{3,4,2,1,0:T(8,128)(2,1)}), bf16[16,2,2,256,256]{3,4,2,1,0:T(8,128)(2,1)}, u32[]{:S(2)}, u32[]{:S(2)}) async-start(bf16[16,2,2,256,256]{3,4,2,1,0:T(8,128)(2,1)} %pad_maximum_fusion), calls=%async_computation | async-start | bytes 16777216 | tf_op jit(solution)/shard_map/all_to_all | solution.py:185
  304.0 8.7 copy-start.17
  304.0 8.7 copy-start.19
  370.5 5.8 copy-start.2
  505.7 10.6 %slice-start.1 = ((s8[8388608]{0:T(1024)(128)(4,1)}), s8[4194304]{0:T(1024)(128)(4,1)S(1)}, s32[]{:S(2)}) async-start(s8[8388608]{0:T(1024)(128)(4,1)} %bitcast.449), calls=%async_computation.6 | async-start | bytes 8388608
  509.7 6.9 slice-start.2
  529.5 7.7 copy-start.24
  529.5 7.7 copy-start.25
  565.3 5.7 copy-start.6
  565.3 187.4 %all-to-all-start.2 = ((f32[2,16,256,256]{3,0,2,1:T(2,128)}), f32[2,16,256,256]{3,0,2,1:T(2,128)}, u32[]{:S(2)}, u32[]{:S(2)}) async-start(f32[2,16,256,256]{3,0,2,1:T(2,128)} %copy.163), calls=%async_computation.2 | async-start | bytes 16777216 | tf_op jit(solution)/shard_map/all_to_all | solution.py:214
  570.4 387.3 %reduce-scatter.2.cloned.1.call-start = ((), (), s32[]{:S(2)}) async-start(), calls=%async_computation.4 | async-start | bytes 12582912 | tf_op jit(solution)/shard_map/reduce_scatter | solution.py:217
  794.5 6.9 copy-start.27
  794.5 6.9 copy-start.29
  858.3 104.7 %copy-start.1 = (f32[4,2]{0,1:T(2,128)S(1)}, f32[4,2]{0,1:T(2,128)}, u32[]{:S(2)}) copy-start(f32[4,2]{0,1:T(2,128)} %param.23) | copy-start | bytes 100
  (10 other events, 39.9 us)
Sparse Core Ops, SparseCore 0:
  858.5 99.2 reduce-scatter.1
where the time goes:
time: 981 us; the launch traced here: 970 us
  waiting for transfers between devices  515 us (52%)
  matrix products  179 us (18%)
  local copies, waits for them, and re-layouts  154 us (16%)
  other arithmetic  87.1 us (9%)
  between operations  17.5 us (2%)
  starting transfers between devices  16.8 us (2%)
    all_to_all x1, waiting for transfers between devices, local(): lax.all_to_all(back, 'row', split_axis=1, concat_axis=1, tiled=True)  182 us
    all_to_all x1, waiting for transfers between devices, local(): lax.all_to_all(sent, 'row', split_axis=0, concat_axis=2, tiled=True)[0]  137 us
    reduce_scatter x1, waiting for transfers between devices, local(): return lax.psum_scatter(result_image, 'wl', scatter_dimension=2, tiled=True)  99.4 us
    all_to_all x1, waiting for transfers between devices, local(): lax.all_to_all(optic_sent, 'row', split_axis=0, concat_axis=3, tiled=True)  96.9 us
    another operation x10, other arithmetic, twist(): jnp.stack([real * cos_part - imag * sin_part, real * sin_part + imag * co...  47.6 us
    unnamed x120, local copies, waits for them, and re-layouts  39.3 us
    dot_general x1, matrix products, inverse_rows(): first = jnp.einsum('oafem,emRj->oafRj', first_tab, canon, precision=PRECISE)  36.2 us
    dot_general x1, matrix products, forward_rows(): jnp.einsum('oaern,oenfk->oarfk', turned, second_tab, precision=PRECISE)  26 us
  transfers between devices with their start and end apart: 4, of which 4 were waited for; matrix products, arithmetic and copies ran while one was open for 12% of the time, Pallas kernels for 0%

commit v1 on v0

--- a/solution.py
+++ b/solution.py
@@ -174,15 +174,16 @@
     weight_rows = lax.dynamic_slice_in_dim(weights, wl_index * local_waves, local_waves, 0)
     first_row = lax.axis_index("row") == 0
 
+    optic_canon = pair_optics(optics)
+    optic_sent = canon_to_groups(optic_canon, row_count)
+    optic_got = lax.all_to_all(optic_sent, "row", split_axis=0, concat_axis=3, tiled=True)[0]
+
     canon = forward_rows(scenes)
     mcount = canon.shape[0]
     sent = canon_to_groups(canon, row_count)
+    optic_got, sent = lax.optimization_barrier((optic_got, sent))
     got = lax.all_to_all(sent, "row", split_axis=0, concat_axis=2, tiled=True)[0]
     spec = forward_cols(got)
-
-    optic_canon = pair_optics(optics)
-    optic_sent = canon_to_groups(optic_canon, row_count)
-    optic_got = lax.all_to_all(optic_sent, "row", split_axis=0, concat_axis=3, tiled=True)[0]
 
     width = spec.shape[-1]
     span = width // 2
@@ -214,7 +215,14 @@
     returned = lax.all_to_all(back, "row", split_axis=1, concat_axis=1, tiled=True)
     returned = groups_to_canon(returned, mcount, 1)
     result_image = inverse_rows(returned, length, norm_factor)
-    return lax.psum_scatter(result_image, "wl", scatter_dimension=2, tiled=True)
+    wl_count = lax.axis_size("wl")
+    if wl_count != 2:
+        return lax.psum_scatter(result_image, "wl", scatter_dimension=2, tiled=True)
+    half = length // 2
+    kept = lax.dynamic_slice_in_dim(result_image, wl_index * half, half, 2)
+    given = lax.dynamic_slice_in_dim(result_image, (1 - wl_index) * half, half, 2)
+    taken = lax.ppermute(given, "wl", perm=[(0, 1), (1, 0)])
+    return kept + taken
 
 
 def solution(mesh):

time: 981 us -> 998 us (1.017)
  waiting for transfers between devices: 515 us -> 535 us
  between operations: 17.5 us -> 3.92 us
    reduce_scatter x1 -> x0, waiting for transfers between devices: 99.4 us -> none  [local(): return lax.psum_scatter(result_image, 'wl', scatter_dimension=2, tiled=True)]
    ppermute x0 -> x1, waiting for transfers between devices: none -> 91.5 us  [local(): taken = lax.ppermute(given, 'wl', perm=[(0, 1), (1, 0)])]
    all_to_all x1, waiting for transfers between devices: 137 us -> 174 us  [local(): lax.all_to_all(sent, 'row', split_axis=0, concat_axis=2, tiled=True)[0]]
    unnamed x120 -> x98, local copies, waits for them, and re-layouts: 39.3 us -> 49.5 us
  transfers between devices with their start and end apart: 4 -> 4, of which waited for: 4 -> 4; matrix products, arithmetic and copies ran while one was open for 12% -> 10% of each run, Pallas kernels for 0% -> 0%
where the time goes in v1:
time: 998 us; the launch traced here: 991 us
  waiting for transfers between devices  535 us (54%)
  matrix products  179 us (18%)
  local copies, waits for them, and re-layouts  162 us (16%)
  other arithmetic  92 us (9%)
  starting transfers between devices  19.2 us (2%)
    all_to_all x1, waiting for transfers between devices, local(): lax.all_to_all(back, 'row', split_axis=1, concat_axis=1, tiled=True)  182 us
    all_to_all x1, waiting for transfers between devices, local(): lax.all_to_all(sent, 'row', split_axis=0, concat_axis=2, tiled=True)[0]  174 us
    ppermute x1, waiting for transfers between devices, local(): taken = lax.ppermute(given, 'wl', perm=[(0, 1), (1, 0)])  91.5 us
    all_to_all x1, waiting for transfers between devices, local(): lax.all_to_all(optic_sent, 'row', split_axis=0, concat_axis=3, tiled=True)  87.9 us
    unnamed x98, local copies, waits for them, and re-layouts  49.5 us
    another operation x10, other arithmetic, twist(): jnp.stack([real * cos_part - imag * sin_part, real * sin_part + imag * co...  47.4 us
    dot_general x1, matrix products, inverse_rows(): first = jnp.einsum('oafem,emRj->oafRj', first_tab, canon, precision=PRECISE)  35.8 us
    dot_general x1, matrix products, forward_rows(): jnp.einsum('oaern,oenfk->oarfk', turned, second_tab, precision=PRECISE)  26.2 us
  transfers between devices with their start and end apart: 4, of which 4 were waited for; matrix products, arithmetic and copies ran while one was open for 10% of the time, Pallas kernels for 0%

profile of v1, /device:TPU:10, one launch (start us, length us, event | category | flops | bytes accessed | tf_op | source)
XLA Modules:
  0.0 990.8 jit_solution(10931770117892721268)
XLA Ops:
  45.8 7.8 pad_maximum_fusion
  53.6 6.6 all-to-all-start
  65.8 16.3 %fusion.22 = f32[2,32,2,256,128]{4,1,3,2,0:T(8,128)} fusion(f32[1,2,2,32,32]{4,3,2,1,0:T(8,128)S(1)} %fusion.68, f32[1,2,2,32,32]{4,3,2,1,0:T(8,128)S(1)} %maximum_bitcast_fusion.22, f32[2,256,32,128]{3,2,1,0:T(8,128)S(1)} %bitcast.429), kind=kOutput, calls=%fused_computation.42 | convolution fusion | flops 3221233664 | bytes 25198592 | tf_op jit(solution)/shard_map/oaedb,drbn->oaern/dot_general | solution.py:71
  84.9 10.6 %subtract_bitcast_fusion.1 = (f32[2,32,1,256,128]{4,1,3,0,2:T(8,128)}, f32[2,32,1,256,128]{4,1,3,0,2:T(8,128)}) fusion(f32[2,32,2,256,128]{4,1,3,2,0:T(8,128)} %fusion.22, f32[2,32,128]{2,1,0:T(8,128)S(1)} %pad_maximum_fusion.10, f32[2,32,128]{2,1,0:T(8,128)S(1)} %pad_maximum_fusion.9), kind=kLoop, calls=%fused_computation.40 | loop fusion | flops 12582912 | bytes 33619968 | tf_op jit(solution)/shard_map/stack | solution.py:37
  95.4 6.8 maximum_bitcast_fusion
  102.3 26.2 %fusion.38 = f32[2,32,256,2,64]{2,4,3,1,0:T(8,128)} fusion(f32[2,32,2,256,128,1]{4,1,3,0,2,5:T(8,128)S(1)} %maximum_bitcast_fusion, f32[1,2,2,64,128]{4,3,2,1,0:T(8,128)S(1)} %maximum_bitcast_fusion.17, f32[1,2,2,64,128]{4,3,2,1,0:T(8,128)S(1)} %maximum_bitcast_fusion.16), kind=kOutput, calls=%fused_computation.82 | convolution fusion | flops 6442516480 | bytes 25427968 | tf_op jit(solution)/shard_map/oaern,oenfk->oarfk/dot_general | solution.py:81
  128.5 9.8 reshape.810
  138.3 8.2 copy.146
  154.3 87.9 %all-to-all-done = bf16[16,2,2,256,256]{3,4,2,1,0:T(8,128)(2,1)} async-done(((bf16[16,2,2,256,256]{3,4,2,1,0:T(8,128)(2,1)}), bf16[16,2,2,256,256]{3,4,2,1,0:T(8,128)(2,1)}, u32[]{:S(2)}, u32[]{:S(2)}) %all-to-all-start) | async-done | bytes 8388640 | tf_op jit(solution)/shard_map/all_to_all | solution.py:179
  242.2 11.4 %copy.142 = bf16[1,2,2,16,256,256]{5,4,3,2,1,0:T(8,128)(2,1)} copy(bf16[1,2,2,16,256,256]{4,5,2,1,3,0:T(8,128)(2,1)} %bitcast.54) | data formatting | bytes 16777216 | tf_op jit(solution)/shard_map/all_to_all | solution.py:179
  267.4 173.6 %all-to-all-done.1 = f32[16,2,256,256]{2,3,1,0:T(8,128)} async-done(((f32[16,2,256,256]{2,3,1,0:T(8,128)}), f32[16,2,256,256]{2,3,1,0:T(8,128)}, u32[]{:S(2)}, u32[]{:S(2)}) %all-to-all-start.1) | async-done | bytes 8388640 | tf_op jit(solution)/shard_map/all_to_all | solution.py:185
  441.1 8.7 copy.148
  449.8 21.8 %fusion.19 = f32[2,32,2,128,256]{4,1,3,2,0:T(8,128)S(1)} fusion(f32[2,32,128,256,1,1]{3,2,1,0,5,4:T(8,128)} %bitcast.432, f32[1,2,2,32,32]{4,3,2,1,0:T(8,128)S(1)} %fusion.68, f32[1,2,2,32,32]{4,3,2,1,0:T(8,128)S(1)} %maximum_bitcast_fusion.22), kind=kOutput, calls=%fused_computation.41 | convolution fusion | flops 3221233664 | bytes 25198592 | tf_op jit(solution)/shard_map/oafeb,ebnj->oafnj/dot_general | solution.py:97
  471.6 5.6 subtract_bitcast_fusion
  477.2 5.5 maximum_bitcast_fusion.1
  482.7 25.0 %fusion.23 = f32[2,2,128,32,256]{4,2,3,1,0:T(8,128)S(1)} fusion(f32[2,32,2,128,256,1]{4,1,3,0,2,5:T(8,128)S(1)} %maximum_bitcast_fusion.1, f32[1,2,2,128,128]{4,3,2,1,0:T(8,128)} %fusion.48, f32[1,2,2,128,128]{4,3,2,1,0:T(8,128)} %maximum_bitcast_fusion.13), kind=kOutput, calls=%fused_computation.43 | convolution fusion | flops 12885032960 | bytes 34078720 | tf_op jit(solution)/shard_map/ofekn,oaenj->ofkaj/dot_general | solution.py:107
  507.7 5.8 copy-done.2
  524.4 6.7 copy.154
  535.2 6.6 maximum_select_fusion
  542.0 8.0 fusion.28
  555.0 7.7 fusion.37
  565.8 11.9 %fusion.32 = f32[2,128,32,256]{3,1,2,0:T(8,128)S(1)} fusion(f32[32,2,128,256]{3,0,2,1:T(8,128)S(1)} %pad_maximum_fusion.1, f32[1,2,128,128]{3,2,1,0:T(8,128)S(1)} %copy-done.8, f32[1,2,128,128]{3,2,1,0:T(8,128)S(1)} %get-tuple-element.153), kind=kOutput, calls=%fused_computation.80 | convolution fusion | flops 6442516480 | bytes 17039360 | tf_op jit(solution)/shard_map/fken,aenj->fkaj/dot_general | solution.py:120
  582.6 8.1 copy.163
  590.7 5.7 all-to-all-start.2
  596.9 181.5 %all-to-all-done.2 = f32[2,16,256,256]{3,0,2,1:T(2,128)} async-done(((f32[2,16,256,256]{3,0,2,1:T(2,128)}), f32[2,16,256,256]{3,0,2,1:T(2,128)}, u32[]{:S(2)}, u32[]{:S(2)}) %all-to-all-start.2) | async-done | bytes 8388640 | tf_op jit(solution)/shard_map/all_to_all | solution.py:215
  779.5 35.8 %convolution_bitcast_fusion = f32[2,32,2,256,256]{4,1,3,2,0:T(8,128)} fusion(f32[2,16,256,256,1,1]{3,0,2,1,5,4:T(2,128)} %bitcast.140, f32[2,32,2,2,16,1]{1,4,3,5,2,0:T(8,128)S(1)} %maximum_bitcast_fusion.39), kind=kOutput, calls=%fused_computation.6 | convolution fusion | flops 3221225472 | bytes 41959424 | tf_op jit(solution)/shard_map/oafem,emRj->oafRj/dot_general | solution.py:128
  819.9 6.8 add_select_fusion
  838.9 12.5 %fusion.9 = f32[32,256,2,128,1]{1,3,4,2,0:T(8,128)S(1)} fusion(f32[32,2,256,128,1]{3,0,2,1,4:T(8,128)S(1)} %maximum_bitcast_fusion.5, f32[2,2,128,2,128]{2,4,1,3,0:T(8,128)S(1)} %fusion.44), kind=kOutput, calls=%fused_computation.27 | convolution fusion | flops 6442450944 | bytes 17039360 | tf_op jit(solution)/shard_map/aeRu,eufk->aRfk/dot_general | solution.py:142
  855.2 17.0 %fusion.8 = f32[2,256,128,32]{1,2,0,3:T(8,128)} fusion(f32[32,256,2,128,1]{1,3,4,2,0:T(8,128)S(1)} %fusion.9, f32[32,2,256,128,1]{3,0,2,1,4:T(8,128)S(1)} %maximum_bitcast_fusion.4, f32[2,2,128,2,128]{2,4,1,3,0:T(8,128)S(1)} %fusion.44), kind=kOutput, calls=%fused_computation.26 | convolution fusion | flops 6444548096 | bytes 25427968 | tf_op jit(solution)/shard_map/aeRu,eufk->aRfk/dot_general | solution.py:141
  872.2 8.2 copy.168
  887.5 91.5 %collective-permute-done = f32[2,256,2048]{1,2,0:T(8,128)} collective-permute-done((f32[2,256,2048]{1,2,0:T(8,128)}, f32[2,256,2048]{1,2,0:T(8,128)}, u32[]{:S(2)}, u32[]{:S(2)}) %collective-permute-start) | collective-permute-done | bytes 4194336 | tf_op jit(solution)/shard_map/ppermute | solution.py:224
  979.1 6.0 dynamic-slice_add_fusion
  (185 shorter events, 135.2 us)
Async XLA Ops:
  0.0 259.3 %copy-start = (f32[4,2]{0,1:T(2,128)S(1)}, f32[4,2]{0,1:T(2,128)}, u32[]{:S(2)}) copy-start(f32[4,2]{0,1:T(2,128)} %param.23) | copy-start | bytes 100
  0.0 40.9 %copy-start.21 = (pred[128]{0:T(512)(128)(4,1)}, pred[128]{0:T(512)(128)(4,1)S(1)}, u32[]{:S(2)}) copy-start(pred[128]{0:T(512)(128)(4,1)S(1)} %get-tuple-element.173) | copy-start | bytes 388
  19.1 19.0 %copy-start.12 = (bf16[2,2,256,128]{2,3,1,0:T(8,128)(2,1)S(1)}, bf16[2,2,256,128]{2,3,1,0:T(8,128)(2,1)}, u32[]{:S(2)}) copy-start(bf16[2,2,256,128]{2,3,1,0:T(8,128)(2,1)} %copy.220) | copy-start | bytes 786436
  19.1 19.7 %copy-start.11 = (bf16[2,2,256,128]{2,3,1,0:T(8,128)(2,1)S(1)}, bf16[2,2,256,128]{2,3,1,0:T(8,128)(2,1)}, u32[]{:S(2)}) copy-start(bf16[2,2,256,128]{2,3,1,0:T(8,128)(2,1)} %copy.221) | copy-start | bytes 786436
  20.3 19.2 %copy-start.10 = (bf16[2,2,256,128]{2,3,1,0:T(8,128)(2,1)S(1)}, bf16[2,2,256,128]{2,3,1,0:T(8,128)(2,1)}, u32[]{:S(2)}) copy-start(bf16[2,2,256,128]{2,3,1,0:T(8,128)(2,1)} %copy.222) | copy-start | bytes 786436
  20.3 19.9 %copy-start.9 = (bf16[2,2,256,128]{2,3,1,0:T(8,128)(2,1)S(1)}, bf16[2,2,256,128]{2,3,1,0:T(8,128)(2,1)}, u32[]{:S(2)}) copy-start(bf16[2,2,256,128]{2,3,1,0:T(8,128)(2,1)} %copy.223) | copy-start | bytes 786436
  53.6 188.7 %all-to-all-start = ((bf16[16,2,2,256,256]{3,4,2,1,0:T(8,128)(2,1)}), bf16[16,2,2,256,256]{3,4,2,1,0:T(8,128)(2,1)}, u32[]{:S(2)}, u32[]{:S(2)}) async-start(bf16[16,2,2,256,256]{3,4,2,1,0:T(8,128)(2,1)} %pad_maximum_fusion), calls=%async_computation | async-start | bytes 16777216 | tf_op jit(solution)/shard_map/all_to_all | solution.py:179
  65.8 16.3 %copy-start.13 = (f32[1,2,32,32]{3,2,1,0:T(8,128)}, f32[1,2,32,32]{3,2,1,0:T(8,128)S(1)}, u32[]{:S(2)}) copy-start(f32[1,2,32,32]{3,2,1,0:T(8,128)S(1)} %get-tuple-element.161) | copy-start | bytes 24580
  65.8 16.3 %copy-start.15 = (f32[1,2,32,32]{3,2,1,0:T(8,128)}, f32[1,2,32,32]{3,2,1,0:T(8,128)S(1)}, u32[]{:S(2)}) copy-start(f32[1,2,32,32]{3,2,1,0:T(8,128)S(1)} %get-tuple-element.162) | copy-start | bytes 24580
  138.3 9.6 copy-start.23
  146.5 3.3 copy-start.3
  253.7 187.4 %all-to-all-start.1 = ((f32[16,2,256,256]{2,3,1,0:T(8,128)}), f32[16,2,256,256]{2,3,1,0:T(8,128)}, u32[]{:S(2)}, u32[]{:S(2)}) async-start(f32[16,2,256,256]{2,3,1,0:T(8,128)} %scatter.4), calls=%async_computation.1 | async-start | bytes 16777216 | tf_op jit(solution)/shard_map/all_to_all | solution.py:185
  262.7 1.5 copy-start.19
  266.1 0.7 copy-start.7
  507.7 5.8 copy-start.2
  516.2 3.4 slice-start
  531.1 10.6 %slice-start.1 = ((s8[8388608]{0:T(1024)(128)(4,1)}), s8[4194304]{0:T(1024)(128)(4,1)S(1)}, s32[]{:S(2)}) async-start(s8[8388608]{0:T(1024)(128)(4,1)} %bitcast.438), calls=%async_computation.4 | async-start | bytes 8388608
  535.2 6.9 slice-start.2
  550.0 4.9 copy-start.14
  550.0 4.9 copy-start.16
  555.0 7.7 copy-start.17
  555.0 7.7 copy-start.18
  564.1 1.7 copy-start.8
  590.7 6.2 copy-start.5
  590.7 6.2 copy-start.6
  590.7 187.8 %all-to-all-start.2 = ((f32[2,16,256,256]{3,0,2,1:T(2,128)}), f32[2,16,256,256]{3,0,2,1:T(2,128)}, u32[]{:S(2)}, u32[]{:S(2)}) async-start(f32[2,16,256,256]{3,0,2,1:T(2,128)} %copy.163), calls=%async_computation.2 | async-start | bytes 16777216 | tf_op jit(solution)/shard_map/all_to_all | solution.py:215
  815.3 4.6 copy-start.22
  819.9 6.8 copy-start.20
  880.4 3.3 copy-start.4
  886.0 93.1 %collective-permute-start = (f32[2,256,2048]{1,2,0:T(8,128)}, f32[2,256,2048]{1,2,0:T(8,128)}, u32[]{:S(2)}, u32[]{:S(2)}) collective-permute-start(f32[2,256,2048]{1,2,0:T(8,128)} %constant_dynamic-slice_fusion.1), channel_id=1, source_target_pairs={{0,16},{16,0},{1,17},{17,1},{2,18},{18,2},{3,19},{19,3},{4,20},{20... | collective-permute-start | bytes 12582920 | tf_op jit(solution)/shard_map/ppermute | solution.py:224
  887.5 102.8 %copy-start.1 = (f32[4,2]{0,1:T(2,128)S(1)}, f32[4,2]{0,1:T(2,128)}, u32[]{:S(2)}) copy-start(f32[4,2]{0,1:T(2,128)} %param.23) | copy-start | bytes 100

commit v2 on v1

--- a/solution.py
+++ b/solution.py
@@ -174,16 +174,31 @@
     weight_rows = lax.dynamic_slice_in_dim(weights, wl_index * local_waves, local_waves, 0)
     first_row = lax.axis_index("row") == 0
 
+    wl_count = lax.axis_size("wl")
+    rows_here = scenes.shape[1]
+    own_rows = rows_here // wl_count
+    if wl_count == 2 and own_rows * wl_count == rows_here:
+        mine = lax.dynamic_slice_in_dim(scenes, wl_index * own_rows, own_rows, 1)
+        canon = forward_rows(mine)
+        mcount = canon.shape[0]
+        sent = canon_to_groups(canon, row_count)
+        got = lax.all_to_all(sent, "row", split_axis=0, concat_axis=2, tiled=True)[0]
+        other = lax.ppermute(got, "wl", perm=[(0, 1), (1, 0)])
+        got = got.reshape((2, row_count, own_rows, got.shape[-1]))
+        other = other.reshape(got.shape)
+        first_half = jnp.where(wl_index == 0, got, other)
+        second_half = jnp.where(wl_index == 0, other, got)
+        got = jnp.stack([first_half, second_half], 2).reshape((2, length, got.shape[-1]))
+    else:
+        canon = forward_rows(scenes)
+        mcount = canon.shape[0]
+        sent = canon_to_groups(canon, row_count)
+        got = lax.all_to_all(sent, "row", split_axis=0, concat_axis=2, tiled=True)[0]
+    spec = forward_cols(got)
+
     optic_canon = pair_optics(optics)
     optic_sent = canon_to_groups(optic_canon, row_count)
     optic_got = lax.all_to_all(optic_sent, "row", split_axis=0, concat_axis=3, tiled=True)[0]
-
-    canon = forward_rows(scenes)
-    mcount = canon.shape[0]
-    sent = canon_to_groups(canon, row_count)
-    optic_got, sent = lax.optimization_barrier((optic_got, sent))
-    got = lax.all_to_all(sent, "row", split_axis=0, concat_axis=2, tiled=True)[0]
-    spec = forward_cols(got)
 
     width = spec.shape[-1]
     span = width // 2
@@ -210,12 +225,10 @@
         combined_imag = combined_imag + resp_real * mixed_imag + resp_imag * mixed_real
 
     back = inverse_cols(jnp.stack([combined_real, combined_imag]))
-    rows_here = length // row_count
     back = back.reshape((2, row_count, rows_here, width))
     returned = lax.all_to_all(back, "row", split_axis=1, concat_axis=1, tiled=True)
     returned = groups_to_canon(returned, mcount, 1)
     result_image = inverse_rows(returned, length, norm_factor)
-    wl_count = lax.axis_size("wl")
     if wl_count != 2:
         return lax.psum_scatter(result_image, "wl", scatter_dimension=2, tiled=True)
     half = length // 2

time: 998 us -> 832 us (0.83)
  waiting for transfers between devices: 535 us -> 385 us
  matrix products: 179 us -> 154 us
  local copies, waits for them, and re-layouts: 162 us -> 174 us
    all_to_all x1, waiting for transfers between devices: 174 us -> 29.2 us  [local(): lax.all_to_all(sent, 'row', split_axis=0, concat_axis=2, tiled=True)[0]]
    all_to_all x1, waiting for transfers between devices: 87.9 us -> 0.01 us  [local(): lax.all_to_all(optic_sent, 'row', split_axis=0, concat_axis=3, tiled=True)]
    ppermute x0 -> x1, waiting for transfers between devices: none -> 83.1 us  [local(): other = lax.ppermute(got, 'wl', perm=[(0, 1), (1, 0)])]
    another operation x1 -> x3, local copies, waits for them, and re-layouts: 0.95 us -> 24.9 us  [the longest x1 13.3 us: local(): jnp.stack([first_half, second_half], 2).reshape((2, length, got.shape[-1]))]
    reshape x2 -> x1, local copies, waits for them, and re-layouts: 18 us -> 2.84 us  [forward_rows(): blocks = second.reshape((2, NARROW, rows_here, 2, mcount, per_block))]
    another operation x10, other arithmetic: 47.4 us -> 32.9 us  [twist(): jnp.stack([real * cos_part - imag * sin_part, real * sin_part + imag * co...]
    dot_general x1, matrix products: 26.2 us -> 13.9 us  [forward_rows(): jnp.einsum('oaern,oenfk->oarfk', turned, second_tab, precision=PRECISE)]
    unnamed x98 -> x114, local copies, waits for them, and re-layouts: 49.5 us -> 54.1 us
  transfers between devices with their start and end apart: 4 -> 5, of which waited for: 4 -> 4; matrix products, arithmetic and copies ran while one was open for 10% -> 23% of each run, Pallas kernels for 0% -> 0%
where the time goes in v2:
time: 832 us; the launch traced here: 821 us
  waiting for transfers between devices  385 us (46%)
  local copies, waits for them, and re-layouts  174 us (21%)
  matrix products  154 us (19%)
  other arithmetic  82.9 us (10%)
  starting transfers between devices  21.4 us (3%)
    all_to_all x1, waiting for transfers between devices, local(): lax.all_to_all(back, 'row', split_axis=1, concat_axis=1, tiled=True)  182 us
    ppermute x1, waiting for transfers between devices, local(): taken = lax.ppermute(given, 'wl', perm=[(0, 1), (1, 0)])  91.6 us
    ppermute x1, waiting for transfers between devices, local(): other = lax.ppermute(got, 'wl', perm=[(0, 1), (1, 0)])  83.1 us
    unnamed x114, local copies, waits for them, and re-layouts  54.1 us
    dot_general x1, matrix products, inverse_rows(): first = jnp.einsum('oafem,emRj->oafRj', first_tab, canon, precision=PRECISE)  35.8 us
    another operation x10, other arithmetic, twist(): jnp.stack([real * cos_part - imag * sin_part, real * sin_part + imag * co...  32.9 us
    all_to_all x1, waiting for transfers between devices, local(): lax.all_to_all(sent, 'row', split_axis=0, concat_axis=2, tiled=True)[0]  29.2 us
    dot_general x1, matrix products, forward_cols(): jnp.einsum('ofekn,oaenj->ofkaj', second_tab, turned, precision=PRECISE)  25 us
  transfers between devices with their start and end apart: 5, of which 4 were waited for; matrix products, arithmetic and copies ran while one was open for 23% of the time, Pallas kernels for 0%

profile of v2, /device:TPU:10, one launch (start us, length us, event | category | flops | bytes accessed | tf_op | source)
XLA Modules:
  0.0 821.2 jit_solution(16458092487448833604)
XLA Ops:
  5.2 6.8 fusion.36
  15.1 13.9 %fusion.15 = f32[2,32,128,2,64,1]{2,4,5,3,1,0:T(8,128)S(1)} fusion(f32[2,32,2,128,128,1]{4,1,3,0,2,5:T(8,128)S(1)} %maximum_bitcast_fusion.1, f32[1,2,2,64,128]{4,3,2,1,0:T(8,128)S(1)} %maximum_bitcast_fusion.19, f32[1,2,2,64,128]{4,3,2,1,0:T(8,128)S(1)} %maximum_bitcast_fusion.18), kind=kOutput, calls=%fused_computation.31 | convolution fusion | flops 3221291008 | bytes 12845056 | tf_op jit(solution)/shard_map/oaern,oenfk->oarfk/dot_general | solution.py:81
  38.6 6.3 all-to-all-start.1
  100.2 7.8 pad_maximum_fusion
  108.0 29.2 %all-to-all-done.1 = f32[16,2,128,256]{2,3,1,0:T(8,128)} async-done(((f32[16,2,128,256]{2,3,1,0:T(8,128)}), f32[16,2,128,256]{2,3,1,0:T(8,128)}, u32[]{:S(2)}, u32[]{:S(2)}) %all-to-all-start.1) | async-done | bytes 4194336 | tf_op jit(solution)/shard_map/all_to_all | solution.py:185
  137.2 5.4 all-to-all-start
  142.6 5.3 copy.152
  157.7 83.1 %collective-permute-done = f32[2,2048,256]{2,1,0:T(8,128)} collective-permute-done((f32[2,2048,256]{2,1,0:T(8,128)}, f32[2,2048,256]{2,1,0:T(8,128)}, u32[]{:S(2)}, u32[]{:S(2)}) %collective-permute-start) | collective-permute-done | bytes 4194336 | tf_op jit(solution)/shard_map/ppermute | solution.py:186
  240.9 5.3 copy.153
  254.2 13.3 %copy.155 = f32[2,16,2,128,256]{4,2,1,0,3:T(2,128)} copy(f32[2,16,2,128,256]{3,4,0,1,2:T(8,128)} %pad_maximum_fusion.1) | data formatting | bytes 16777216 | tf_op jit(solution)/shard_map/stack | solution.py:191
  267.4 11.0 %reshape.1096 = f32[2,32,128,256,1,1]{3,1,0,2,4,5:T(8,128)} reshape(f32[2,16,2,128,256]{4,2,1,0,3:T(2,128)} %copy.155) | data formatting | bytes 16777216 | tf_op jit(solution)/shard_map/reshape;reshape | solution.py:95
  278.4 16.7 %fusion.18 = f32[2,32,2,128,256]{4,1,3,2,0:T(8,128)S(1)} fusion(f32[2,32,128,256,1,1]{3,1,0,2,4,5:T(8,128)} %reshape.1096, f32[1,2,2,32,32]{4,3,2,1,0:T(8,128)S(1)} %copy-done.20, f32[1,2,2,32,32]{4,3,2,1,0:T(8,128)S(1)} %copy-done.18), kind=kOutput, calls=%fused_computation.36 | convolution fusion | flops 3221233664 | bytes 25198592 | tf_op jit(solution)/shard_map/oafeb,ebnj->oafnj/dot_general | solution.py:97
  295.1 6.1 subtract_bitcast_fusion
  301.2 5.1 maximum_bitcast_fusion
  306.3 25.0 %fusion.21 = f32[2,2,128,32,256]{4,2,3,1,0:T(8,128)S(1)} fusion(f32[2,32,2,128,256,1]{4,1,3,0,2,5:T(8,128)S(1)} %maximum_bitcast_fusion, f32[1,2,2,128,128]{4,3,2,1,0:T(8,128)} %fusion.46, f32[1,2,2,128,128]{4,3,2,1,0:T(8,128)} %maximum_bitcast_fusion.11), kind=kOutput, calls=%fused_computation.37 | convolution fusion | flops 12885032960 | bytes 34078720 | tf_op jit(solution)/shard_map/ofekn,oaenj->ofkaj/dot_general | solution.py:107
  331.3 5.8 copy-done.2
  357.9 11.4 %copy.146 = bf16[1,2,2,16,256,256]{5,4,3,2,1,0:T(8,128)(2,1)} copy(bf16[1,2,2,16,256,256]{4,5,2,1,3,0:T(8,128)(2,1)} %bitcast.54) | data formatting | bytes 16777216 | tf_op jit(solution)/shard_map/all_to_all | solution.py:201
  369.3 11.1 %fusion.26 = (f32[1,4096,256]{2,1,0:T(8,128)S(1)}, f32[1,4096,256]{2,1,0:T(8,128)S(1)}) fusion(bf16[2,2,4096,256]{3,2,1,0:T(8,128)(2,1)} %bitcast.457, f32[]{:T(128)} %bitcast.123, f32[]{:T(128)} %bitcast.122, f32[2,4096,256]{2,1,0:T(8,128)} %maximum_select_fusion, f32[1,1,128,32,256]{4,3,2,1,0:T(8,128)} %copy.160, f32[]{:T(128)} %bitcast.128, f32[]{:T(128)} %bitcast.127, ...), kind=kLoop, calls=%fused_computation.48 | loop fusion | flops 36700160 | bytes 33554448 | tf_op jit(solution)/shard_map/sub | solution.py:224
  385.3 7.7 fusion.37
  396.2 11.9 %fusion.31 = f32[2,128,32,256]{3,1,2,0:T(8,128)S(1)} fusion(f32[32,2,128,256]{3,0,2,1:T(8,128)S(1)} %pad_maximum_fusion.2, f32[1,2,128,128]{3,2,1,0:T(8,128)S(1)} %copy-done.9, f32[1,2,128,128]{3,2,1,0:T(8,128)S(1)} %get-tuple-element.151), kind=kOutput, calls=%fused_computation.82 | convolution fusion | flops 6442516480 | bytes 17039360 | tf_op jit(solution)/shard_map/fken,aenj->fkaj/dot_general | solution.py:120
  408.0 4.9 copy.168
  412.9 8.2 copy.169
  421.1 6.7 all-to-all-start.2
  428.3 181.5 %all-to-all-done.2 = f32[2,16,256,256]{3,0,2,1:T(2,128)} async-done(((f32[2,16,256,256]{3,0,2,1:T(2,128)}), f32[2,16,256,256]{3,0,2,1:T(2,128)}, u32[]{:S(2)}, u32[]{:S(2)}) %all-to-all-start.2) | async-done | bytes 8388640 | tf_op jit(solution)/shard_map/all_to_all | solution.py:229
  610.9 35.8 %convolution_bitcast_fusion = f32[2,32,2,256,256]{4,1,3,2,0:T(8,128)} fusion(f32[2,16,256,256,1,1]{3,0,2,1,5,4:T(2,128)} %bitcast.147, f32[2,32,2,2,16,1]{1,4,3,5,2,0:T(8,128)S(1)} %maximum_bitcast_fusion.39), kind=kOutput, calls=%fused_computation.3 | convolution fusion | flops 3221225472 | bytes 41959424 | tf_op jit(solution)/shard_map/oafem,emRj->oafRj/dot_general | solution.py:128
  651.3 6.8 add_select_fusion
  670.3 12.5 %fusion.6 = f32[32,256,2,128,1]{1,3,4,2,0:T(8,128)S(1)} fusion(f32[32,2,256,128,1]{3,0,2,1,4:T(8,128)S(1)} %maximum_bitcast_fusion.5, f32[2,2,128,2,128]{2,4,1,3,0:T(8,128)S(1)} %fusion.42), kind=kOutput, calls=%fused_computation.22 | convolution fusion | flops 6442450944 | bytes 17039360 | tf_op jit(solution)/shard_map/aeRu,eufk->aRfk/dot_general | solution.py:142
  686.6 17.0 %fusion.5 = f32[2,256,128,32]{1,2,0,3:T(8,128)} fusion(f32[32,256,2,128,1]{1,3,4,2,0:T(8,128)S(1)} %fusion.6, f32[32,2,256,128,1]{3,0,2,1,4:T(8,128)S(1)} %maximum_bitcast_fusion.4, f32[2,2,128,2,128]{2,4,1,3,0:T(8,128)S(1)} %fusion.42), kind=kOutput, calls=%fused_computation.21 | convolution fusion | flops 6444548096 | bytes 25427968 | tf_op jit(solution)/shard_map/aeRu,eufk->aRfk/dot_general | solution.py:141
  703.6 8.2 %copy.174 = f32[2,256,128,32]{1,3,2,0:T(8,128)S(1)} copy(f32[2,256,128,32]{1,2,0,3:T(8,128)} %fusion.5) | data formatting | bytes 16777216 | tf_op jit(solution)/shard_map/add | solution.py:142
  717.9 91.6 %collective-permute-done.1 = f32[2,256,2048]{1,2,0:T(8,128)} collective-permute-done((f32[2,256,2048]{1,2,0:T(8,128)}, f32[2,256,2048]{1,2,0:T(8,128)}, u32[]{:S(2)}, u32[]{:S(2)}) %collective-permute-start.1) | collective-permute-done | bytes 4194336 | tf_op jit(solution)/shard_map/ppermute | solution.py:237
  809.5 5.9 dynamic-slice_add_fusion
  815.4 5.3 copy.175
  (205 shorter events, 144.9 us)
Async XLA Ops:
  0.0 149.7 %copy-start = (f32[4,2]{0,1:T(2,128)S(1)}, f32[4,2]{0,1:T(2,128)}, u32[]{:S(2)}) copy-start(f32[4,2]{0,1:T(2,128)} %param.23) | copy-start | bytes 100
  5.2 6.9 copy-start.17
  5.2 6.8 copy-start.21
  5.2 6.8 copy-start.23
  5.2 6.8 copy-start.19
  38.6 98.6 %all-to-all-start.1 = ((f32[16,2,128,256]{2,3,1,0:T(8,128)}), f32[16,2,128,256]{2,3,1,0:T(8,128)}, u32[]{:S(2)}, u32[]{:S(2)}) async-start(f32[16,2,128,256]{2,3,1,0:T(8,128)} %scatter.4), calls=%async_computation.1 | async-start | bytes 8388608 | tf_op jit(solution)/shard_map/all_to_all | solution.py:185
  44.9 50.4 %copy-start.31 = (pred[128]{0:T(512)(128)(4,1)}, pred[128]{0:T(512)(128)(4,1)S(1)}, u32[]{:S(2)}) copy-start(pred[128]{0:T(512)(128)(4,1)S(1)} %get-tuple-element.171) | copy-start | bytes 388
  62.0 6.4 copy-start.10
  62.9 5.5 copy-start.11
  63.8 11.7 %copy-start.13 = (bf16[2,2,256,128]{2,3,1,0:T(8,128)(2,1)S(1)}, bf16[2,2,256,128]{2,3,1,0:T(8,128)(2,1)}, u32[]{:S(2)}) copy-start(bf16[2,2,256,128]{2,3,1,0:T(8,128)(2,1)} %copy.224) | copy-start | bytes 786436
  64.6 11.5 %copy-start.12 = (bf16[2,2,256,128]{2,3,1,0:T(8,128)(2,1)S(1)}, bf16[2,2,256,128]{2,3,1,0:T(8,128)(2,1)}, u32[]{:S(2)}) copy-start(bf16[2,2,256,128]{2,3,1,0:T(8,128)(2,1)} %copy.225) | copy-start | bytes 786436
  65.5 9.2 %copy-start.14 = (bf16[2,2,256,128]{2,3,1,0:T(8,128)(2,1)S(1)}, bf16[2,2,256,128]{2,3,1,0:T(8,128)(2,1)}, u32[]{:S(2)}) copy-start(bf16[2,2,256,128]{2,3,1,0:T(8,128)(2,1)} %copy.223) | copy-start | bytes 786436
  66.4 7.6 copy-start.15
  67.2 6.1 copy-start.16
  137.2 220.8 %all-to-all-start = ((bf16[16,2,2,256,256]{3,4,2,1,0:T(8,128)(2,1)}), bf16[16,2,2,256,256]{3,4,2,1,0:T(8,128)(2,1)}, u32[]{:S(2)}, u32[]{:S(2)}) async-start(bf16[16,2,2,256,256]{3,4,2,1,0:T(8,128)(2,1)} %pad_maximum_fusion), calls=%async_computation | async-start | bytes 16777216 | tf_op jit(solution)/shard_map/all_to_all | solution.py:201
  147.9 92.9 %collective-permute-start = (f32[2,2048,256]{2,1,0:T(8,128)}, f32[2,2048,256]{2,1,0:T(8,128)}, u32[]{:S(2)}, u32[]{:S(2)}) collective-permute-start(f32[2,2048,256]{2,1,0:T(8,128)} %bitcast.465), channel_id=1, source_target_pairs={{0,16},{16,0},{1,17},{17,1},{2,18},{18,2},{3,19},{19,3},{4,20},{20... | collective-permute-start | bytes 12582920 | tf_op jit(solution)/shard_map/ppermute | solution.py:186
  153.0 93.2 %copy-start.27 = (f32[32,128]{1,0:T(8,128)}, f32[32,128]{1,0:T(8,128)S(1)}, u32[]{:S(2)}) copy-start(f32[32,128]{1,0:T(8,128)S(1)} %get-tuple-element.195) | copy-start | bytes 49156
  153.0 93.2 %copy-start.29 = (f32[32,128]{1,0:T(8,128)}, f32[32,128]{1,0:T(8,128)S(1)}, u32[]{:S(2)}) copy-start(f32[32,128]{1,0:T(8,128)S(1)} %get-tuple-element.196) | copy-start | bytes 49156
  267.4 11.0 %copy-start.18 = (f32[1,2,2,32,32]{4,3,2,1,0:T(8,128)S(1)}, f32[1,2,2,32,32]{4,3,2,1,0:T(8,128)}, u32[]{:S(2)}) copy-start(f32[1,2,2,32,32]{4,3,2,1,0:T(8,128)} %copy-done.17) | copy-start | bytes 49156
  267.4 11.0 %copy-start.20 = (f32[1,2,2,32,32]{4,3,2,1,0:T(8,128)S(1)}, f32[1,2,2,32,32]{4,3,2,1,0:T(8,128)}, u32[]{:S(2)}) copy-start(f32[1,2,2,32,32]{4,3,2,1,0:T(8,128)} %copy-done.19) | copy-start | bytes 49156
  331.3 5.8 copy-start.2
  344.3 4.9 copy-start.5
  385.3 7.7 copy-start.25
  385.3 7.7 copy-start.26
  421.1 7.2 copy-start.6
  421.1 7.2 copy-start.7
  421.1 188.8 %all-to-all-start.2 = ((f32[2,16,256,256]{3,0,2,1:T(2,128)}), f32[2,16,256,256]{3,0,2,1:T(2,128)}, u32[]{:S(2)}, u32[]{:S(2)}) async-start(f32[2,16,256,256]{3,0,2,1:T(2,128)} %copy.169), calls=%async_computation.2 | async-start | bytes 16777216 | tf_op jit(solution)/shard_map/all_to_all | solution.py:229
  646.7 4.6 copy-start.32
  651.3 6.9 copy-start.28
  651.3 6.9 copy-start.30
  716.4 93.1 %collective-permute-start.1 = (f32[2,256,2048]{1,2,0:T(8,128)}, f32[2,256,2048]{1,2,0:T(8,128)}, u32[]{:S(2)}, u32[]{:S(2)}) collective-permute-start(f32[2,256,2048]{1,2,0:T(8,128)} %constant_dynamic-slice_fusion.2), channel_id=1, source_target_pairs={{0,16},{16,0},{1,17},{17,1},{2,18},{18,2},{3,19},{19,3},{4,20},{20... | collective-permute-start | bytes 12582920 | tf_op jit(solution)/shard_map/ppermute | solution.py:237
  809.5 11.3 %copy-start.1 = (f32[4,2]{0,1:T(2,128)S(1)}, f32[4,2]{0,1:T(2,128)}, u32[]{:S(2)}) copy-start(f32[4,2]{0,1:T(2,128)} %param.23) | copy-start | bytes 100
  (8 other events, 21.3 us)

commit v3 on v2

--- a/solution.py
+++ b/solution.py
@@ -225,17 +225,27 @@
         combined_imag = combined_imag + resp_real * mixed_imag + resp_imag * mixed_real
 
     back = inverse_cols(jnp.stack([combined_real, combined_imag]))
-    back = back.reshape((2, row_count, rows_here, width))
-    returned = lax.all_to_all(back, "row", split_axis=1, concat_axis=1, tiled=True)
+    if wl_count != 2 or own_rows * wl_count != rows_here:
+        back = back.reshape((2, row_count, rows_here, width))
+        returned = lax.all_to_all(back, "row", split_axis=1, concat_axis=1, tiled=True)
+        returned = groups_to_canon(returned, mcount, 1)
+        result_image = inverse_rows(returned, length, norm_factor)
+        return lax.psum_scatter(result_image, "wl", scatter_dimension=2, tiled=True)
+    back = back.reshape((2, row_count, 2, own_rows, width))
+    kept = lax.dynamic_index_in_dim(back, wl_index, 2, keepdims=False)
+    given = lax.dynamic_index_in_dim(back, 1 - wl_index, 2, keepdims=False)
+    summed = kept + lax.ppermute(given, "wl", perm=[(0, 1), (1, 0)])
+    returned = lax.all_to_all(summed, "row", split_axis=1, concat_axis=1, tiled=True)
     returned = groups_to_canon(returned, mcount, 1)
     result_image = inverse_rows(returned, length, norm_factor)
-    if wl_count != 2:
-        return lax.psum_scatter(result_image, "wl", scatter_dimension=2, tiled=True)
     half = length // 2
-    kept = lax.dynamic_slice_in_dim(result_image, wl_index * half, half, 2)
-    given = lax.dynamic_slice_in_dim(result_image, (1 - wl_index) * half, half, 2)
-    taken = lax.ppermute(given, "wl", perm=[(0, 1), (1, 0)])
-    return kept + taken
+    result_image = result_image.reshape((2, own_rows, 2, half))
+    mine = lax.dynamic_index_in_dim(result_image, wl_index, 2, keepdims=False)
+    theirs = lax.dynamic_index_in_dim(result_image, 1 - wl_index, 2, keepdims=False)
+    taken = lax.ppermute(theirs, "wl", perm=[(0, 1), (1, 0)])
+    upper = jnp.where(wl_index == 0, mine, taken)
+    lower = jnp.where(wl_index == 0, taken, mine)
+    return jnp.concatenate([upper, lower], 1)
 
 
 def solution(mesh):

time: 832 us -> 743 us (0.89)
  waiting for transfers between devices: 385 us -> 343 us
  matrix products: 154 us -> 118 us
  other arithmetic: 82.9 us -> 70.8 us
    all_to_all x1, waiting for transfers between devices: 182 us -> 91.8 us  [local(): lax.all_to_all(summed, 'row', split_axis=1, concat_axis=1, tiled=True)]
    ppermute x1 -> x2, waiting for transfers between devices: 91.6 us -> 135 us  [the longest x1 90.6 us: local(): summed = kept + lax.ppermute(given, 'wl', perm=[(0, 1), (1, 0)])]
    dot_general x1, matrix products: 35.8 us -> 15.4 us  [inverse_rows(): first = jnp.einsum('oafem,emRj->oafRj', first_tab, canon, precision=PRECISE)]
    another operation x10, other arithmetic: 32.9 us -> 20.5 us  [twist(): jnp.stack([real * cos_part - imag * sin_part, real * sin_part + imag * co...]
    dot_general x1, matrix products: 17 us -> 6.86 us  [inverse_rows(): out = jnp.einsum('aeRu,eufk->aRfk', lower, tabs[0], precision=PRECISE)]
    unnamed x114 -> x106, local copies, waits for them, and re-layouts: 54.1 us -> 56.9 us
  transfers between devices with their start and end apart: 5 -> 6, of which waited for: 4 -> 5; matrix products, arithmetic and copies ran while one was open for 23% -> 26% of each run, Pallas kernels for 0% -> 0%
where the time goes in v3:
time: 743 us; the launch traced here: 732 us
  waiting for transfers between devices  343 us (46%)
  local copies, waits for them, and re-layouts  174 us (23%)
  matrix products  118 us (16%)
  other arithmetic  70.8 us (10%)
  starting transfers between devices  22.3 us (3%)
    all_to_all x1, waiting for transfers between devices, local(): lax.all_to_all(summed, 'row', split_axis=1, concat_axis=1, tiled=True)  91.8 us
    ppermute x1, waiting for transfers between devices, local(): summed = kept + lax.ppermute(given, 'wl', perm=[(0, 1), (1, 0)])  90.6 us
    ppermute x1, waiting for transfers between devices, local(): other = lax.ppermute(got, 'wl', perm=[(0, 1), (1, 0)])  83.1 us
    unnamed x106, local copies, waits for them, and re-layouts  56.9 us
    ppermute x1, waiting for transfers between devices, local(): taken = lax.ppermute(theirs, 'wl', perm=[(0, 1), (1, 0)])  44.8 us
    all_to_all x1, waiting for transfers between devices, local(): lax.all_to_all(sent, 'row', split_axis=0, concat_axis=2, tiled=True)[0]  32.9 us
    dot_general x1, matrix products, forward_cols(): jnp.einsum('ofekn,oaenj->ofkaj', second_tab, turned, precision=PRECISE)  25 us
    another operation x10, other arithmetic, twist(): jnp.stack([real * cos_part - imag * sin_part, real * sin_part + imag * co...  20.5 us
  transfers between devices with their start and end apart: 6, of which 5 were waited for; matrix products, arithmetic and copies ran while one was open for 26% of the time, Pallas kernels for 0%

profile of v3, /device:TPU:10, one launch (start us, length us, event | category | flops | bytes accessed | tf_op | source)
XLA Modules:
  0.0 731.5 jit_solution(17698418947574659744)
XLA Ops:
  5.1 6.8 fusion.34
  15.0 13.9 %fusion.9 = f32[2,32,128,2,64,1]{2,4,5,3,1,0:T(8,128)S(1)} fusion(f32[2,32,2,128,128,1]{4,1,3,0,2,5:T(8,128)S(1)} %maximum_bitcast_fusion.1, f32[1,2,2,64,128]{4,3,2,1,0:T(8,128)S(1)} %maximum_bitcast_fusion.19, f32[1,2,2,64,128]{4,3,2,1,0:T(8,128)S(1)} %maximum_bitcast_fusion.18), kind=kOutput, calls=%fused_computation.18 | convolution fusion | flops 3221291008 | bytes 12845056 | tf_op jit(solution)/shard_map/oaern,oenfk->oarfk/dot_general | solution.py:81
  39.3 6.2 all-to-all-start.1
  92.3 4.8 convolution_convert_fusion
  97.1 7.8 %pad_maximum_fusion = bf16[16,2,2,256,256]{3,4,2,1,0:T(8,128)(2,1)} fusion(bf16[16,2,2,256,128]{3,4,2,1,0:T(8,128)(2,1)} %convolution_convert_fusion, bf16[16,2,2,256,128]{3,4,2,1,0:T(8,128)(2,1)} %bitcast_dynamic-update-slice_fusion.15), kind=kLoop, calls=%fused_computation.5 | loop fusion | flops 16777216 | bytes 16777216 | tf_op jit(solution)/shard_map/concatenate | solution.py:164
  104.9 32.9 %all-to-all-done.1 = f32[16,2,128,256]{2,3,1,0:T(8,128)} async-done(((f32[16,2,128,256]{2,3,1,0:T(8,128)}), f32[16,2,128,256]{2,3,1,0:T(8,128)}, u32[]{:S(2)}, u32[]{:S(2)}) %all-to-all-start.1) | async-done | bytes 4194336 | tf_op jit(solution)/shard_map/all_to_all | solution.py:185
  137.8 5.4 all-to-all-start
  143.2 5.3 copy.250
  158.4 83.1 %collective-permute-done = f32[2,2048,256]{2,1,0:T(8,128)} collective-permute-done((f32[2,2048,256]{2,1,0:T(8,128)}, f32[2,2048,256]{2,1,0:T(8,128)}, u32[]{:S(2)}, u32[]{:S(2)}) %collective-permute-start) | collective-permute-done | bytes 4194336 | tf_op jit(solution)/shard_map/ppermute | solution.py:186
  241.5 5.3 copy.251
  254.8 13.3 %copy.253 = f32[2,16,2,128,256]{4,2,1,0,3:T(2,128)} copy(f32[2,16,2,128,256]{3,4,0,1,2:T(8,128)} %pad_maximum_fusion.1) | data formatting | bytes 16777216 | tf_op jit(solution)/shard_map/stack | solution.py:191
  268.0 11.0 %reshape.1092 = f32[2,32,128,256,1,1]{3,1,0,2,4,5:T(8,128)} reshape(f32[2,16,2,128,256]{4,2,1,0,3:T(2,128)} %copy.253) | data formatting | bytes 16777216 | tf_op jit(solution)/shard_map/reshape;reshape | solution.py:95
  279.0 16.7 %fusion.12 = f32[2,32,2,128,256]{4,1,3,2,0:T(8,128)S(1)} fusion(f32[2,32,128,256,1,1]{3,1,0,2,4,5:T(8,128)} %reshape.1092, f32[1,2,2,32,32]{4,3,2,1,0:T(8,128)S(1)} %copy-done.14, f32[1,2,2,32,32]{4,3,2,1,0:T(8,128)S(1)} %copy-done.16), kind=kOutput, calls=%fused_computation.23 | convolution fusion | flops 3221233664 | bytes 25198592 | tf_op jit(solution)/shard_map/oafeb,ebnj->oafnj/dot_general | solution.py:97
  295.7 6.0 subtract_bitcast_fusion
  301.7 5.1 maximum_bitcast_fusion
  306.8 25.0 %fusion.15 = f32[2,2,128,32,256]{4,2,3,1,0:T(8,128)S(1)} fusion(f32[2,32,2,128,256,1]{4,1,3,0,2,5:T(8,128)S(1)} %maximum_bitcast_fusion, f32[1,2,2,128,128]{4,3,2,1,0:T(8,128)} %fusion.46, f32[1,2,2,128,128]{4,3,2,1,0:T(8,128)} %maximum_bitcast_fusion.11), kind=kOutput, calls=%fused_computation.24 | convolution fusion | flops 12885032960 | bytes 34078720 | tf_op jit(solution)/shard_map/ofekn,oaenj->ofkaj/dot_general | solution.py:107
  331.8 5.8 copy-done.2
  341.9 8.2 %copy.259 = f32[1,2,128,32,256]{4,3,2,1,0:T(8,128)S(1)} copy(f32[1,2,128,32,256]{4,2,3,1,0:T(8,128)} %slice.358) | data formatting | bytes 16777216 | tf_op jit(solution)/shard_map/slice | solution.py:208
  367.4 11.4 %copy.244 = bf16[1,2,2,16,256,256]{5,4,3,2,1,0:T(8,128)(2,1)} copy(bf16[1,2,2,16,256,256]{4,5,2,1,3,0:T(8,128)(2,1)} %bitcast.54) | data formatting | bytes 16777216 | tf_op jit(solution)/shard_map/all_to_all | solution.py:201
  378.7 11.1 %fusion.20 = (f32[1,4096,256]{2,1,0:T(8,128)S(1)}, f32[1,4096,256]{2,1,0:T(8,128)S(1)}) fusion(bf16[2,2,4096,256]{3,2,1,0:T(8,128)(2,1)} %bitcast.459, f32[]{:T(128)} %bitcast.123, f32[]{:T(128)} %bitcast.122, f32[2,4096,256]{2,1,0:T(8,128)} %maximum_select_fusion, f32[1,1,128,32,256]{4,3,2,1,0:T(8,128)} %copy.258, f32[]{:T(128)} %bitcast.128, f32[]{:T(128)} %bitcast.127, ...), kind=kLoop, calls=%fused_computation.37 | loop fusion | flops 36700160 | bytes 33554448 | tf_op jit(solution)/shard_map/sub | solution.py:224
  394.7 7.7 %fusion.35 = f32[32,2,128,256]{3,0,2,1:T(8,128)S(1)} fusion(f32[1,32,128,256]{3,1,0,2:T(8,128)S(1)} %copy.262, f32[1,32,128,256]{3,1,0,2:T(8,128)S(1)} %copy.261, f32[1,2,32,32]{3,2,1,0:T(8,128)S(1)} %copy-done.20, f32[1,2,32,32]{3,2,1,0:T(8,128)S(1)} %copy-done.18), kind=kOutput, calls=%fused_computation.78 | convolution fusion | flops 1612713984 | bytes 16793600 | tf_op jit(solution)/shard_map/afeb,ebnj->afnj/dot_general | solution.py:116
  405.6 12.1 %fusion.31 = f32[2,128,32,256]{3,1,2,0:T(8,128)S(1)} fusion(f32[32,2,128,256]{3,0,2,1:T(8,128)S(1)} %pad_maximum_fusion.2, f32[1,2,128,128]{3,2,1,0:T(8,128)S(1)} %copy-done.10, f32[1,2,128,128]{3,2,1,0:T(8,128)S(1)} %get-tuple-element.155), kind=kOutput, calls=%fused_computation.76 | convolution fusion | flops 6442516480 | bytes 17039360 | tf_op jit(solution)/shard_map/fken,aenj->fkaj/dot_general | solution.py:120
  417.7 4.9 copy.266
  428.6 90.6 %collective-permute-done.1 = f32[2,16,128,256]{3,2,1,0:T(8,128)} collective-permute-done((f32[2,16,128,256]{3,2,1,0:T(8,128)}, f32[2,16,128,256]{3,2,1,0:T(8,128)}, u32[]{:S(2)}, u32[]{:S(2)}) %collective-permute-start.1) | collective-permute-done | bytes 4194336 | tf_op jit(solution)/shard_map/ppermute | solution.py:237
  523.2 5.3 copy.267
  528.5 6.1 all-to-all-start.2
  535.1 91.8 %all-to-all-done.2 = f32[2,16,128,256]{3,0,2,1:T(2,128)} async-done(((f32[2,16,128,256]{3,0,2,1:T(2,128)}), f32[2,16,128,256]{3,0,2,1:T(2,128)}, u32[]{:S(2)}, u32[]{:S(2)}) %all-to-all-start.2) | async-done | bytes 4194336 | tf_op jit(solution)/shard_map/all_to_all | solution.py:238
  627.0 15.4 %convolution_bitcast_fusion = f32[2,32,2,128,256]{4,1,3,2,0:T(8,128)S(1)} fusion(f32[2,16,128,256,1,1]{3,0,2,1,5,4:T(2,128)} %bitcast.149, f32[1,2,2,32,16]{3,4,2,1,0:T(8,128)S(1)} %maximum_bitcast_fusion.28, f32[1,2,2,32,16]{3,4,2,1,0:T(8,128)S(1)} %maximum_bitcast_fusion.27), kind=kOutput, calls=%fused_computation.25 | convolution fusion | flops 1610616832 | bytes 20987904 | tf_op jit(solution)/shard_map/oafem,emRj->oafRj/dot_general | solution.py:128
  642.3 5.8 copy-done.3
  657.6 6.6 fusion.26
  664.1 6.9 fusion.25
  681.3 44.8 %collective-permute-done.2 = f32[2,128,2048]{2,1,0:T(8,128)} collective-permute-done((f32[2,128,2048]{2,1,0:T(8,128)}, f32[2,128,2048]{2,1,0:T(8,128)}, u32[]{:S(2)}, u32[]{:S(2)}) %collective-permute-start.2) | collective-permute-done | bytes 2097184 | tf_op jit(solution)/shard_map/ppermute | solution.py:245
  (201 shorter events, 144.9 us)
Async XLA Ops:
  0.0 150.3 %copy-start = (f32[4,2]{0,1:T(2,128)S(1)}, f32[4,2]{0,1:T(2,128)}, u32[]{:S(2)}) copy-start(f32[4,2]{0,1:T(2,128)} %param.23) | copy-start | bytes 100
  4.5 7.4 %copy-start.13 = (f32[1,2,2,32,32]{4,3,2,1,0:T(8,128)}, f32[1,2,2,32,32]{4,3,2,1,0:T(8,128)S(1)}, u32[]{:S(2)}) copy-start(f32[1,2,2,32,32]{4,3,2,1,0:T(8,128)S(1)} %fusion.66) | copy-start | bytes 49156
  5.1 6.8 copy-start.15
  29.0 3.6 copy-start.29
  31.8 2.8 copy-start.5
  39.3 98.6 %all-to-all-start.1 = ((f32[16,2,128,256]{2,3,1,0:T(8,128)}), f32[16,2,128,256]{2,3,1,0:T(8,128)}, u32[]{:S(2)}, u32[]{:S(2)}) async-start(f32[16,2,128,256]{2,3,1,0:T(8,128)} %scatter.4), calls=%async_computation.1 | async-start | bytes 8388608 | tf_op jit(solution)/shard_map/all_to_all | solution.py:185
  45.5 46.8 %copy-start.27 = (pred[128]{0:T(512)(128)(4,1)}, pred[128]{0:T(512)(128)(4,1)S(1)}, u32[]{:S(2)}) copy-start(pred[128]{0:T(512)(128)(4,1)S(1)} %get-tuple-element.175) | copy-start | bytes 388
  57.0 8.3 %copy-start.11 = (bf16[2,2,256,128]{3,2,1,0:T(8,128)(2,1)S(1)}, bf16[2,2,256,128]{3,2,1,0:T(8,128)(2,1)}, u32[]{:S(2)}) copy-start(bf16[2,2,256,128]{3,2,1,0:T(8,128)(2,1)} %get-tuple-element.143) | copy-start | bytes 786436
  62.9 2.4 copy-start.12
  137.8 229.5 %all-to-all-start = ((bf16[16,2,2,256,256]{3,4,2,1,0:T(8,128)(2,1)}), bf16[16,2,2,256,256]{3,4,2,1,0:T(8,128)(2,1)}, u32[]{:S(2)}, u32[]{:S(2)}) async-start(bf16[16,2,2,256,256]{3,4,2,1,0:T(8,128)(2,1)} %pad_maximum_fusion), calls=%async_computation | async-start | bytes 16777216 | tf_op jit(solution)/shard_map/all_to_all | solution.py:201
  148.6 92.9 %collective-permute-start = (f32[2,2048,256]{2,1,0:T(8,128)}, f32[2,2048,256]{2,1,0:T(8,128)}, u32[]{:S(2)}, u32[]{:S(2)}) collective-permute-start(f32[2,2048,256]{2,1,0:T(8,128)} %bitcast.468), channel_id=1, source_target_pairs={{0,16},{16,0},{1,17},{17,1},{2,18},{18,2},{3,19},{19,3},{4,20},{20... | collective-permute-start | bytes 12582920 | tf_op jit(solution)/shard_map/ppermute | solution.py:186
  153.7 93.1 %copy-start.23 = (f32[32,128]{1,0:T(8,128)}, f32[32,128]{1,0:T(8,128)S(1)}, u32[]{:S(2)}) copy-start(f32[32,128]{1,0:T(8,128)S(1)} %get-tuple-element.199) | copy-start | bytes 49156
  153.7 93.1 %copy-start.25 = (f32[32,128]{1,0:T(8,128)}, f32[32,128]{1,0:T(8,128)S(1)}, u32[]{:S(2)}) copy-start(f32[32,128]{1,0:T(8,128)S(1)} %get-tuple-element.200) | copy-start | bytes 49156
  268.0 11.0 %copy-start.14 = (f32[1,2,2,32,32]{4,3,2,1,0:T(8,128)S(1)}, f32[1,2,2,32,32]{4,3,2,1,0:T(8,128)}, u32[]{:S(2)}) copy-start(f32[1,2,2,32,32]{4,3,2,1,0:T(8,128)} %copy-done.13) | copy-start | bytes 49156
  268.0 11.0 %copy-start.16 = (f32[1,2,2,32,32]{4,3,2,1,0:T(8,128)S(1)}, f32[1,2,2,32,32]{4,3,2,1,0:T(8,128)}, u32[]{:S(2)}) copy-start(f32[1,2,2,32,32]{4,3,2,1,0:T(8,128)} %copy-done.15) | copy-start | bytes 49156
  331.8 5.8 copy-start.2
  392.2 2.5 copy-start.18
  392.3 2.5 copy-start.20
  394.7 7.7 %copy-start.21 = (f32[32,128]{0,1:T(8,128)S(1)}, f32[32,128]{0,1:T(8,128)}, u32[]{:S(2)}) copy-start(f32[32,128]{0,1:T(8,128)} %copy.263) | copy-start | bytes 49156
  394.7 7.7 %copy-start.22 = (f32[32,128]{0,1:T(8,128)S(1)}, f32[32,128]{0,1:T(8,128)}, u32[]{:S(2)}) copy-start(f32[32,128]{0,1:T(8,128)} %copy.264) | copy-start | bytes 49156
  403.9 1.7 copy-start.10
  422.5 4.6 copy-start.4
  427.1 92.1 %collective-permute-start.1 = (f32[2,16,128,256]{3,2,1,0:T(8,128)}, f32[2,16,128,256]{3,2,1,0:T(8,128)}, u32[]{:S(2)}, u32[]{:S(2)}) collective-permute-start(f32[2,16,128,256]{3,2,1,0:T(8,128)} %dynamic-slice_bitcast_fusion), channel_id=1, source_target_pairs={{0,16},{16,0},{1,17},{17,1},{2,18},{18,2},{3,19},{19,3},{4,20},{20... | collective-permute-start | bytes 12582920 | tf_op jit(solution)/shard_map/ppermute | solution.py:237
  528.5 6.6 copy-start.7
  528.5 6.6 copy-start.8
  528.5 98.5 %all-to-all-start.2 = ((f32[2,16,128,256]{3,0,2,1:T(2,128)}), f32[2,16,128,256]{3,0,2,1:T(2,128)}, u32[]{:S(2)}, u32[]{:S(2)}) async-start(f32[2,16,128,256]{3,0,2,1:T(2,128)} %copy.267), calls=%async_computation.2 | async-start | bytes 8388608 | tf_op jit(solution)/shard_map/all_to_all | solution.py:238
  642.3 5.8 copy-start.3
  648.1 0.7 copy-start.26
  648.9 3.1 copy-start.28
  652.0 4.1 copy-start.6
  677.9 48.1 %collective-permute-start.2 = (f32[2,128,2048]{2,1,0:T(8,128)}, f32[2,128,2048]{2,1,0:T(8,128)}, u32[]{:S(2)}, u32[]{:S(2)}) collective-permute-start(f32[2,128,2048]{2,1,0:T(8,128)} %bitcast.469), channel_id=1, source_target_pairs={{0,16},{16,0},{1,17},{17,1},{2,18},{18,2},{3,19},{19,3},{4,20},{20... | collective-permute-start | bytes 6291464 | tf_op jit(solution)/shard_map/ppermute | solution.py:245
  728.8 2.5 copy-start.1
  (4 other events, 2.6 us)

commit v4 on v0

--- a/solution.py
+++ b/solution.py
@@ -121,9 +121,10 @@
     return second.reshape((2, length, width))
 
 
-def inverse_rows(canon, length, scale):
+def inverse_rows(canon, length, scale, k_count=None, k_start=0):
     mcount, rows_here, width = canon.shape[1], canon.shape[2], canon.shape[3]
     across = width // 2
+    k_count = across if k_count is None else k_count
     first_tab = jnp.transpose(small_tables(NARROW, mcount, NARROW, (1.0, -1.0)), (0, 3, 1, 2, 4))
     first = jnp.einsum("oafem,emRj->oafRj", first_tab, canon, precision=PRECISE)
     lower = first[0, :, :, :, :across]
@@ -136,11 +137,15 @@
     cos_dn, sin_dn = phase(ids(NARROW)[:, None], ids(across)[None, :], length, -1.0)
     lower = twist(lower, 1, cos_up[:, None, :], sin_up[:, None, :])
     upper = twist(upper, 1, cos_dn[:, None, :], sin_dn[:, None, :])
-    tabs = small_tables(across, across, across, (1.0, -1.0)) * scale
-    tabs = jnp.transpose(tabs, (0, 2, 4, 1, 3))
+    tabs = []
+    for orient in (1.0, -1.0):
+        k_ids = ids(k_count)[:, None] + k_start
+        cos_part, sin_part = phase(k_ids, ids(across)[None, :], across, orient)
+        tabs.append(cblock(cos_part, sin_part))
+    tabs = jnp.transpose(jnp.stack(tabs) * scale, (0, 2, 4, 1, 3))
     out = jnp.einsum("aeRu,eufk->aRfk", lower, tabs[0], precision=PRECISE)
     out = out + jnp.einsum("aeRu,eufk->aRfk", upper, tabs[1], precision=PRECISE)
-    return jnp.transpose(out, (2, 1, 3, 0)).reshape((2, rows_here, length))
+    return jnp.transpose(out, (2, 1, 3, 0)).reshape((2, rows_here, k_count * NARROW))
 
 
 def pair_optics(optics):
@@ -164,30 +169,27 @@
     return jnp.concatenate([lower, mirrored.astype(optics.dtype)], -1)
 
 
-def local(scenes, optics, weights):
-    row_count = lax.axis_size("row")
-    length = scenes.shape[2]
-    across = length // NARROW
-    norm_factor = 1.0 / (float(length) * float(length))
-    wl_index = lax.axis_index("wl")
-    local_waves = optics.shape[0]
-    weight_rows = lax.dynamic_slice_in_dim(weights, wl_index * local_waves, local_waves, 0)
-    first_row = lax.axis_index("row") == 0
-
-    canon = forward_rows(scenes)
-    mcount = canon.shape[0]
-    sent = canon_to_groups(canon, row_count)
-    got = lax.all_to_all(sent, "row", split_axis=0, concat_axis=2, tiled=True)[0]
-    spec = forward_cols(got)
-
-    optic_canon = pair_optics(optics)
-    optic_sent = canon_to_groups(optic_canon, row_count)
-    optic_got = lax.all_to_all(optic_sent, "row", split_axis=0, concat_axis=3, tiled=True)[0]
-
+def split_lanes(grouped, half_index):
+    span = grouped.shape[-1] // 2
+    lead = grouped.shape[:-1]
+    parts = grouped.reshape(lead + (2, 2, span // 2))
+    picked = lax.dynamic_index_in_dim(parts, half_index, len(lead) + 1, keepdims=False)
+    return picked.reshape(lead + (span,))
+
+
+def join_lanes(mine, theirs, half_index):
+    lead = mine.shape[:-1]
+    quarter = mine.shape[-1] // 2
+    mine = mine.reshape(lead + (2, quarter))
+    theirs = theirs.reshape(lead + (2, quarter))
+    low = jnp.where(half_index == 0, mine, theirs)
+    high = jnp.where(half_index == 0, theirs, mine)
+    return jnp.stack([low, high], -2).reshape(lead + (4 * quarter,))
+
+
+def combine(spec, optic_got, weight_rows, itself):
     width = spec.shape[-1]
     span = width // 2
-    lane_ids = ids(width)
-    itself = jnp.logical_and(first_row, lane_ids % span == 0)
     direct = spec[0]
     flipped = spec[1]
     swapped = jnp.concatenate([flipped[..., span:], flipped[..., :span]], -1)
@@ -200,16 +202,79 @@
     odd_imag = 0.5 * (direct[1] - mirror_imag)
     combined_real = jnp.zeros_like(even_real)
     combined_imag = jnp.zeros_like(even_imag)
-    for colour in range(local_waves):
+    for colour in range(optic_got.shape[0]):
         mixed_real = weight_rows[colour, 0] * even_real + weight_rows[colour, 1] * odd_real
         mixed_imag = weight_rows[colour, 0] * even_imag + weight_rows[colour, 1] * odd_imag
         resp_real = optic_got[colour, 0].astype(jnp.float32)
         resp_imag = optic_got[colour, 1].astype(jnp.float32)
         combined_real = combined_real + resp_real * mixed_real - resp_imag * mixed_imag
         combined_imag = combined_imag + resp_real * mixed_imag + resp_imag * mixed_real
-
-    back = inverse_cols(jnp.stack([combined_real, combined_imag]))
-    rows_here = length // row_count
+    return jnp.stack([combined_real, combined_imag])
+
+
+def local_split(scenes, optics, weights):
+    row_count = lax.axis_size("row")
+    rows_here, length = scenes.shape[1], scenes.shape[2]
+    across = length // NARROW
+    norm_factor = 1.0 / (float(length) * float(length))
+    wl_index = lax.axis_index("wl")
+    first_row = lax.axis_index("row") == 0
+    swap = [(0, 1), (1, 0)]
+
+    optic_canon = pair_optics(optics)
+    optic_grouped = canon_to_groups(optic_canon, row_count)
+    optic_mine = split_lanes(optic_grouped, wl_index)
+    optic_theirs = lax.ppermute(split_lanes(optic_grouped, 1 - wl_index), "wl", perm=swap)
+    optic_low = jnp.where(wl_index == 0, optic_mine, optic_theirs)
+    optic_high = jnp.where(wl_index == 0, optic_theirs, optic_mine)
+    optic_all = jnp.concatenate([optic_low, optic_high], 1)
+    optic_got = lax.all_to_all(optic_all, "row", split_axis=0, concat_axis=3, tiled=True)[0]
+
+    canon = forward_rows(scenes)
+    mcount = canon.shape[0]
+    sent = split_lanes(canon_to_groups(canon, row_count), wl_index)
+    got = lax.all_to_all(sent, "row", split_axis=0, concat_axis=2, tiled=True)[0]
+    spec = forward_cols(got)
+
+    width = spec.shape[-1]
+    lane_ids = ids(width)
+    itself = jnp.logical_and(first_row, wl_index == 0)
+    itself = jnp.logical_and(itself, lane_ids % (width // 2) == 0)
+    combined = combine(spec, optic_got, weights, itself)
+
+    back = inverse_cols(combined)
+    back = back.reshape((2, row_count, rows_here, width))
+    returned = lax.all_to_all(back, "row", split_axis=1, concat_axis=1, tiled=True)
+    other = lax.ppermute(returned, "wl", perm=swap)
+    returned = join_lanes(returned, other, wl_index)
+    returned = groups_to_canon(returned, mcount, 1)
+    k_half = across // 2
+    return inverse_rows(returned, length, norm_factor, k_half, wl_index * k_half)
+
+
+def local(scenes, optics, weights):
+    row_count = lax.axis_size("row")
+    length = scenes.shape[2]
+    span = length // 2 // row_count
+    if lax.axis_size("wl") == 2 and span % 2 == 0:
+        return local_split(scenes, optics, weights)
+    norm_factor = 1.0 / (float(length) * float(length))
+    wl_index = lax.axis_index("wl")
+    local_waves = optics.shape[0]
+    weight_rows = lax.dynamic_slice_in_dim(weights, wl_index * local_waves, local_waves, 0)
+    first_row = lax.axis_index("row") == 0
+    canon = forward_rows(scenes)
+    mcount = canon.shape[0]
+    sent = canon_to_groups(canon, row_count)
+    got = lax.all_to_all(sent, "row", split_axis=0, concat_axis=2, tiled=True)[0]
+    spec = forward_cols(got)
+    optic_grouped = canon_to_groups(pair_optics(optics), row_count)
+    optic_got = lax.all_to_all(optic_grouped, "row", split_axis=0, concat_axis=3, tiled=True)[0]
+    width = spec.shape[-1]
+    itself = jnp.logical_and(first_row, ids(width) % (width // 2) == 0)
+    combined = combine(spec, optic_got, weight_rows, itself)
+    back = inverse_cols(combined)
+    rows_here = scenes.shape[1]
     back = back.reshape((2, row_count, rows_here, width))
     returned = lax.all_to_all(back, "row", split_axis=1, concat_axis=1, tiled=True)
     returned = groups_to_canon(returned, mcount, 1)

time: 981 us -> 836 us (0.85)
  waiting for transfers between devices: 515 us -> 308 us
  blocking collectives: 0 us -> 97.5 us
  matrix products: 179 us -> 144 us
  local copies, waits for them, and re-layouts: 154 us -> 166 us
  between operations: 17.5 us -> 6.39 us
    all_to_all x3 -> x2, waiting for transfers between devices: 416 us -> 126 us  [the longest x1 126 us: local_split(): lax.all_to_all(optic_all, 'row', split_axis=0, concat_axis=3, tiled=True)[0]]
    ppermute x0 -> x2, waiting for transfers between devices: none -> 182 us  [the longest x1 91.4 us: local_split(): lax.ppermute(split_lanes(optic_grouped, 1 - wl_index), 'wl', perm=swap)]
    reduce_scatter x1 -> x0, waiting for transfers between devices: 99.4 us -> none  [local(): return lax.psum_scatter(result_image, 'wl', scatter_dimension=2, tiled=True)]
    all_to_all x0 -> x1, blocking collectives: none -> 97.5 us  [local_split(): lax.all_to_all(back, 'row', split_axis=1, concat_axis=1, tiled=True)]
    unnamed x120 -> x99, local copies, waits for them, and re-layouts: 39.3 us -> 59.8 us
    another operation x10, other arithmetic: 47.6 us -> 29.9 us  [twist(): jnp.stack([real * cos_part - imag * sin_part, real * sin_part + imag * co...]
    slice x8, local copies, waits for them, and re-layouts: 25.5 us -> 9.63 us  [the longest x3 3.39 us: combine(): flipped = spec[1]]
    reshape x0 -> x2, local copies, waits for them, and re-layouts: none -> 15.7 us  [the longest x1 10.3 us: join_lanes(): return jnp.stack([low, high], -2).reshape(lead + (4 * quarter,))]
  transfers between devices with their start and end apart: 4 -> 4, of which waited for: 4 -> 3; matrix products, arithmetic and copies ran while one was open for 12% -> 17% of each run, Pallas kernels for 0% -> 0%
where the time goes in v4:
time: 836 us; the launch traced here: 825 us
  waiting for transfers between devices  308 us (37%)
  local copies, waits for them, and re-layouts  166 us (20%)
  matrix products  144 us (17%)
  blocking collectives  97.5 us (12%)
  other arithmetic  87.3 us (10%)
  starting transfers between devices  16.4 us (2%)
    all_to_all x1, waiting for transfers between devices, local_split(): lax.all_to_all(optic_all, 'row', split_axis=0, concat_axis=3, tiled=True)[0]  126 us
    all_to_all x1, blocking collectives, local_split(): lax.all_to_all(back, 'row', split_axis=1, concat_axis=1, tiled=True)  97.5 us
    ppermute x1, waiting for transfers between devices, local_split(): lax.ppermute(split_lanes(optic_grouped, 1 - wl_index), 'wl', perm=swap)  91.4 us
    ppermute x1, waiting for transfers between devices, local_split(): other = lax.ppermute(returned, 'wl', perm=swap)  90.7 us
    unnamed x99, local copies, waits for them, and re-layouts  59.8 us
    dot_general x1, matrix products, inverse_rows(): first = jnp.einsum('oafem,emRj->oafRj', first_tab, canon, precision=PRECISE)  31.9 us
    another operation x10, other arithmetic, twist(): jnp.stack([real * cos_part - imag * sin_part, real * sin_part + imag * co...  29.9 us
    dot_general x1, matrix products, forward_rows(): jnp.einsum('oaern,oenfk->oarfk', turned, second_tab, precision=PRECISE)  26 us
  transfers between devices with their start and end apart: 4, of which 3 were waited for; matrix products, arithmetic and copies ran while one was open for 17% of the time, Pallas kernels for 0%

profile of v4, /device:TPU:10, one launch (start us, length us, event | category | flops | bytes accessed | tf_op | source)
XLA Modules:
  0.0 825.1 jit_solution(16449381243977008973)
XLA Ops:
  1.8 5.2 copy.291
  7.1 16.3 %fusion.9 = f32[2,32,2,256,128]{4,1,3,2,0:T(8,128)} fusion(f32[1,2,2,32,32]{4,3,2,1,0:T(8,128)S(1)} %fusion.75, f32[1,2,2,32,32]{4,3,2,1,0:T(8,128)S(1)} %maximum_bitcast_fusion.24, f32[2,256,32,128]{3,2,1,0:T(8,128)S(1)} %bitcast.488), kind=kOutput, calls=%fused_computation.25 | convolution fusion | flops 3221233664 | bytes 25198592 | tf_op jit(solution)/shard_map/oaedb,drbn->oaern/dot_general | solution.py:71
  25.3 10.6 %subtract_bitcast_fusion = (f32[2,32,1,256,128]{4,1,3,0,2:T(8,128)}, f32[2,32,1,256,128]{4,1,3,0,2:T(8,128)}) fusion(f32[2,32,2,256,128]{4,1,3,2,0:T(8,128)} %fusion.9, f32[2,32,128]{2,1,0:T(8,128)S(1)} %pad_maximum_fusion.12, f32[2,32,128]{2,1,0:T(8,128)S(1)} %pad_maximum_fusion.11), kind=kLoop, calls=%fused_computation.24 | loop fusion | flops 12582912 | bytes 33619968 | tf_op jit(solution)/shard_map/stack | solution.py:37
  35.9 6.9 maximum_bitcast_fusion
  42.8 26.0 %fusion.25 = f32[2,32,256,2,64]{2,4,3,1,0:T(8,128)} fusion(f32[2,32,2,256,128,1]{4,1,3,0,2,5:T(8,128)S(1)} %maximum_bitcast_fusion, f32[1,2,2,64,128]{4,3,2,1,0:T(8,128)S(1)} %maximum_bitcast_fusion.19, f32[1,2,2,64,128]{4,3,2,1,0:T(8,128)S(1)} %maximum_bitcast_fusion.18), kind=kOutput, calls=%fused_computation.55 | convolution fusion | flops 6442516480 | bytes 25427968 | tf_op jit(solution)/shard_map/oaern,oenfk->oarfk/dot_general | solution.py:81
  68.7 10.0 %reshape.1144 = f32[2,32,256,2,16,4]{2,5,4,3,1,0:T(4,128)} reshape(f32[2,32,256,2,64]{2,4,3,1,0:T(8,128)} %fusion.25) | data formatting | bytes 16777216 | tf_op jit(solution)/shard_map/reshape | solution.py:86
  78.7 8.2 copy.205
  94.7 4.8 constant_dynamic-slice_fusion
  99.5 6.9 all-to-all-start.1
  159.8 8.2 convolution_convert_fusion
  168.1 7.8 pad_maximum_fusion
  175.8 8.5 %constant_dynamic-slice_fusion.2 = (bf16[16,2,2,256,2,1,64]{3,6,5,4,2,1,0:T(8,128)(2,1)}, bf16[16,2,2,256,2,1,64]{3,6,5,4,2,1,0:T(8,128)(2,1)}) fusion(bf16[16,2,2,256,2,2,64]{3,6,5,4,2,1,0:T(8,128)(2,1)} %bitcast.495, s32[]{:T(128)S(6)} %select_n.428, s32[]{:T(128)S(6)} %select_n.429), kind=kLoop, calls=%fused_computation.316 | loop fusion | bytes 16777224 | tf_op jit(solution)/shard_map/jit(dynamic_index_in_dim)/dynamic_slice | solution.py:176
  185.9 91.4 %collective-permute-done = bf16[16,2,2,256,128]{3,4,2,1,0:T(8,128)(2,1)} collective-permute-done((bf16[16,2,2,256,128]{3,4,2,1,0:T(8,128)(2,1)}, bf16[16,2,2,256,128]{3,4,2,1,0:T(8,128)(2,1)}, u32[]{:S(2)}, u32[]{:S(2)}) %collective-permute-start) | collective-permute-done | bytes 4194336 | tf_op jit(solution)/shard_map/ppermute | solution.py:227
  277.3 5.8 bitcast_select_fusion.1
  283.1 7.5 pad_maximum_fusion.1
  290.6 6.5 all-to-all-start
  305.1 5.3 copy.207
  310.4 11.5 %fusion.22 = f32[2,32,2,128,128]{4,1,3,2,0:T(8,128)S(1)} fusion(f32[2,32,128,128,1,1]{3,2,1,0,5,4:T(8,128)} %bitcast.499, f32[1,2,2,32,32]{4,3,2,1,0:T(8,128)S(1)} %fusion.75, f32[1,2,2,32,32]{4,3,2,1,0:T(8,128)S(1)} %maximum_bitcast_fusion.24), kind=kOutput, calls=%fused_computation.54 | convolution fusion | flops 1610620928 | bytes 12615680 | tf_op jit(solution)/shard_map/oafeb,ebnj->oafnj/dot_general | solution.py:97
  325.9 12.2 %fusion.19 = f32[2,2,128,32,128]{4,2,3,1,0:T(8,128)S(1)} fusion(f32[2,32,2,128,128,1]{4,1,3,0,2,5:T(8,128)S(1)} %maximum_bitcast_fusion.1, f32[1,2,2,128,128]{4,3,2,1,0:T(8,128)S(1)} %fusion.55, f32[1,2,2,128,128]{4,3,2,1,0:T(8,128)S(1)} %maximum_bitcast_fusion.11), kind=kOutput, calls=%fused_computation.53 | convolution fusion | flops 6442582016 | bytes 17301504 | tf_op jit(solution)/shard_map/ofekn,oaenj->ofkaj/dot_general | solution.py:107
  353.7 125.5 %all-to-all-done = bf16[16,4,2,256,128]{3,4,2,1,0:T(8,128)(2,1)} async-done(((bf16[16,4,2,256,128]{3,4,2,1,0:T(8,128)(2,1)}), bf16[16,4,2,256,128]{3,4,2,1,0:T(8,128)(2,1)}, u32[]{:S(2)}, u32[]{:S(2)}) %all-to-all-start) | async-done | bytes 8388640 | tf_op jit(solution)/shard_map/all_to_all | solution.py:231
  479.2 11.4 %copy.201 = bf16[1,4,2,16,256,128]{5,4,3,2,1,0:T(8,128)(2,1)} copy(bf16[1,4,2,16,256,128]{4,5,2,1,3,0:T(8,128)(2,1)} %bitcast.57) | data formatting | bytes 16777216 | tf_op jit(solution)/shard_map/all_to_all | solution.py:231
  490.6 7.1 fusion.47
  512.5 5.9 fusion.28
  521.2 97.5 %all_to_all.35 = f32[2,16,256,128]{3,2,0,1:T(8,128)} all-to-all(f32[2,16,256,128]{3,2,0,1:T(8,128)S(1)} %copy.222), channel_id=1, replica_groups=mesh['wl'=2,'row'=16] {'row'}, dimensions={1} | all-to-all | bytes 8388608 | tf_op jit(solution)/shard_map/all_to_all | solution.py:247
  618.7 5.3 copy.224
  626.4 90.7 %collective-permute-done.1 = f32[2,16,256,128]{2,3,1,0:T(8,128)} collective-permute-done((f32[2,16,256,128]{2,3,1,0:T(8,128)}, f32[2,16,256,128]{2,3,1,0:T(8,128)}, u32[]{:S(2)}, u32[]{:S(2)}) %collective-permute-start.1) | collective-permute-done | bytes 4194336 | tf_op jit(solution)/shard_map/ppermute | solution.py:248
  726.8 10.3 %copy.250 = f32[2,16,256,256,1,1]{3,1,0,2,5,4:T(8,128)} copy(f32[2,16,256,256,1,1]{2,3,1,0,5,4:T(8,128)} %bitcast.494) | data formatting | bytes 16777216 | tf_op jit(solution)/shard_map/reshape | solution.py:187
  737.2 31.9 %convolution_bitcast_fusion = f32[2,32,2,256,256]{4,1,3,2,0:T(8,128)} fusion(f32[2,16,256,256,1,1]{3,1,0,2,5,4:T(8,128)} %copy.250, f32[2,32,2,2,16,1]{1,4,3,5,2,0:T(8,128)S(1)} %maximum_bitcast_fusion.45), kind=kOutput, calls=%fused_computation.3 | convolution fusion | flops 3221225472 | bytes 41959424 | tf_op jit(solution)/shard_map/oafem,emRj->oafRj/dot_general | solution.py:129
  773.7 6.8 add_select_fusion
  786.0 13.9 %fusion.3 = f32[32,256,2,64,1]{1,3,4,2,0:T(8,128)S(1)} fusion(f32[32,2,256,128,1]{3,0,2,1,4:T(8,128)S(1)} %maximum_bitcast_fusion.3, f32[2,2,128,2,64]{2,4,1,3,0:T(8,128)S(1)} %fusion.53), kind=kOutput, calls=%fused_computation.17 | convolution fusion | flops 3221225472 | bytes 12713984 | tf_op jit(solution)/shard_map/aeRu,eufk->aRfk/dot_general | solution.py:147
  800.8 14.1 %fusion.13 = f32[2,256,64,32]{1,2,0,3:T(8,128)S(1)} fusion(f32[32,256,2,64,1]{1,3,4,2,0:T(8,128)S(1)} %fusion.3, f32[32,2,256,128,1]{3,0,2,1,4:T(8,128)S(1)} %maximum_bitcast_fusion.2, f32[2,2,128,2,64]{2,4,1,3,0:T(8,128)S(1)} %fusion.53), kind=kOutput, calls=%fused_computation.41 | convolution fusion | flops 3222274048 | bytes 16908288 | tf_op jit(solution)/shard_map/aeRu,eufk->aRfk/dot_general | solution.py:146
  819.4 5.3 copy.231
  (197 shorter events, 133.3 us)
Async XLA Ops:
  7.1 16.4 %copy-start.11 = (f32[1,2,32,32]{3,2,1,0:T(8,128)}, f32[1,2,32,32]{3,2,1,0:T(8,128)S(1)}, u32[]{:S(2)}) copy-start(f32[1,2,32,32]{3,2,1,0:T(8,128)S(1)} %get-tuple-element.165) | copy-start | bytes 24580
  7.1 16.4 %copy-start.13 = (f32[1,2,32,32]{3,2,1,0:T(8,128)}, f32[1,2,32,32]{3,2,1,0:T(8,128)S(1)}, u32[]{:S(2)}) copy-start(f32[1,2,32,32]{3,2,1,0:T(8,128)S(1)} %get-tuple-element.166) | copy-start | bytes 24580
  25.2 10.7 %copy-start.15 = (f32[2,32,128]{2,1,0:T(8,128)}, f32[2,32,128]{2,1,0:T(8,128)S(1)}, u32[]{:S(2)}) copy-start(f32[2,32,128]{2,1,0:T(8,128)S(1)} %pad_maximum_fusion.11) | copy-start | bytes 98308
  25.2 10.7 %copy-start.17 = (f32[2,32,128]{2,1,0:T(8,128)}, f32[2,32,128]{2,1,0:T(8,128)S(1)}, u32[]{:S(2)}) copy-start(f32[2,32,128]{2,1,0:T(8,128)S(1)} %pad_maximum_fusion.12) | copy-start | bytes 98308
  78.7 8.6 %copy-start.25 = (s32[4]{0:T(128)S(1)}, s32[4]{0:T(128)}, u32[]{:S(2)}) copy-start(s32[4]{0:T(128)} %constant.342.clone.1) | copy-start | bytes 52
  87.0 3.3 copy-start.4
  99.5 191.2 %all-to-all-start.1 = ((f32[16,2,256,128]{2,3,1,0:T(8,128)}), f32[16,2,256,128]{2,3,1,0:T(8,128)}, u32[]{:S(2)}, u32[]{:S(2)}) async-start(f32[16,2,256,128]{2,3,1,0:T(8,128)} %bitcast.500), calls=%async_computation.1 | async-start | bytes 8388608 | tf_op jit(solution)/shard_map/all_to_all | solution.py:236
  106.4 53.5 %copy-start.22 = (pred[128]{0:T(512)(128)(4,1)}, pred[128]{0:T(512)(128)(4,1)S(1)}, u32[]{:S(2)}) copy-start(pred[128]{0:T(512)(128)(4,1)S(1)} %get-tuple-element.187) | copy-start | bytes 388
  137.6 11.8 %copy-start.10 = (bf16[2,2,256,128]{2,3,1,0:T(8,128)(2,1)S(1)}, bf16[2,2,256,128]{2,3,1,0:T(8,128)(2,1)}, u32[]{:S(2)}) copy-start(bf16[2,2,256,128]{2,3,1,0:T(8,128)(2,1)} %copy.283) | copy-start | bytes 786436
  137.6 12.5 %copy-start.9 = (bf16[2,2,256,128]{2,3,1,0:T(8,128)(2,1)S(1)}, bf16[2,2,256,128]{2,3,1,0:T(8,128)(2,1)}, u32[]{:S(2)}) copy-start(bf16[2,2,256,128]{2,3,1,0:T(8,128)(2,1)} %copy.284) | copy-start | bytes 786436
  139.5 11.3 %copy-start.8 = (bf16[2,2,256,128]{2,3,1,0:T(8,128)(2,1)S(1)}, bf16[2,2,256,128]{2,3,1,0:T(8,128)(2,1)}, u32[]{:S(2)}) copy-start(bf16[2,2,256,128]{2,3,1,0:T(8,128)(2,1)} %copy.285) | copy-start | bytes 786436
  139.5 12.0 %copy-start.7 = (bf16[2,2,256,128]{2,3,1,0:T(8,128)(2,1)S(1)}, bf16[2,2,256,128]{2,3,1,0:T(8,128)(2,1)}, u32[]{:S(2)}) copy-start(bf16[2,2,256,128]{2,3,1,0:T(8,128)(2,1)} %copy.286) | copy-start | bytes 786436
  184.4 92.9 %collective-permute-start = (bf16[16,2,2,256,128]{3,4,2,1,0:T(8,128)(2,1)}, bf16[16,2,2,256,128]{3,4,2,1,0:T(8,128)(2,1)}, u32[]{:S(2)}, u32[]{:S(2)}) collective-permute-start(bf16[16,2,2,256,128]{3,4,2,1,0:T(8,128)(2,1)} %bitcast.55), channel_id=1, source_target_pairs={{0,16},{16,0},{1,17},{17,1},{2,18},{18,2},{3,19},{19,3},{4,20},{20... | collective-permute-start | bytes 12582920 | tf_op jit(solution)/shard_map/ppermute | solution.py:227
  290.6 6.5 copy-start.18
  290.6 6.6 copy-start.16
  290.6 6.7 copy-start.21
  290.6 188.5 %all-to-all-start = ((bf16[16,4,2,256,128]{3,4,2,1,0:T(8,128)(2,1)}), bf16[16,4,2,256,128]{3,4,2,1,0:T(8,128)(2,1)}, u32[]{:S(2)}, u32[]{:S(2)}) async-start(bf16[16,4,2,256,128]{3,4,2,1,0:T(8,128)(2,1)} %pad_maximum_fusion.1), calls=%async_computation | async-start | bytes 16777216 | tf_op jit(solution)/shard_map/all_to_all | solution.py:231
  303.2 1.8 copy-start.19
  338.2 3.3 copy-start.3
  342.0 2.2 slice-start
  349.1 1.3 copy-start.24
  490.6 7.6 copy-start
  490.6 8.8 %copy-start.1 = (f32[2,4096,128]{2,1,0:T(8,128)S(1)}, f32[2,4096,128]{2,1,0:T(8,128)}, u32[]{:S(2)}) copy-start(f32[2,4096,128]{2,1,0:T(8,128)} %maximum_select_fusion) | copy-start | bytes 12582916
  490.6 9.4 %copy-start.5 = (f32[1,1,128,32,128]{4,3,2,1,0:T(8,128)S(1)}, f32[1,1,128,32,128]{4,3,2,1,0:T(8,128)}, u32[]{:S(2)}) copy-start(f32[1,1,128,32,128]{4,3,2,1,0:T(8,128)} %copy.213) | copy-start | bytes 6291460
  503.8 2.5 copy-start.12
  503.9 2.5 copy-start.14
  624.0 93.1 %collective-permute-start.1 = (f32[2,16,256,128]{2,3,1,0:T(8,128)}, f32[2,16,256,128]{2,3,1,0:T(8,128)}, u32[]{:S(2)}, u32[]{:S(2)}) collective-permute-start(f32[2,16,256,128]{2,3,1,0:T(8,128)} %copy.224), channel_id=1, source_target_pairs={{0,16},{16,0},{1,17},{17,1},{2,18},{18,2},{3,19},{19,3},{4,20},{20... | collective-permute-start | bytes 12582920 | tf_op jit(solution)/shard_map/ppermute | solution.py:248
  723.5 3.3 copy-start.2
  769.1 4.6 copy-start.23
  773.7 6.8 copy-start.20
  785.9 13.9 %copy-start.6 = (f32[32,1,256,128]{3,0,2,1:T(8,128)S(1)}, f32[32,1,256,128]{3,0,2,1:T(8,128)}, u32[]{:S(2)}) copy-start(f32[32,1,256,128]{3,0,2,1:T(8,128)} %get-tuple-element.118) | copy-start | bytes 12582916

commit v5 on v4

--- a/solution.py
+++ b/solution.py
@@ -221,19 +221,19 @@
     first_row = lax.axis_index("row") == 0
     swap = [(0, 1), (1, 0)]
 
-    optic_canon = pair_optics(optics)
-    optic_grouped = canon_to_groups(optic_canon, row_count)
-    optic_mine = split_lanes(optic_grouped, wl_index)
-    optic_theirs = lax.ppermute(split_lanes(optic_grouped, 1 - wl_index), "wl", perm=swap)
-    optic_low = jnp.where(wl_index == 0, optic_mine, optic_theirs)
-    optic_high = jnp.where(wl_index == 0, optic_theirs, optic_mine)
-    optic_all = jnp.concatenate([optic_low, optic_high], 1)
-    optic_got = lax.all_to_all(optic_all, "row", split_axis=0, concat_axis=3, tiled=True)[0]
+    optic_grouped = canon_to_groups(pair_optics(optics), row_count)
+    optic_own = lax.all_to_all(optic_grouped, "row", split_axis=0, concat_axis=3, tiled=True)[0]
 
     canon = forward_rows(scenes)
     mcount = canon.shape[0]
     sent = split_lanes(canon_to_groups(canon, row_count), wl_index)
+    optic_own, sent = lax.optimization_barrier((optic_own, sent))
     got = lax.all_to_all(sent, "row", split_axis=0, concat_axis=2, tiled=True)[0]
+    optic_mine = split_lanes(optic_own, wl_index)
+    optic_theirs = lax.ppermute(split_lanes(optic_own, 1 - wl_index), "wl", perm=swap)
+    optic_low = jnp.where(wl_index == 0, optic_mine, optic_theirs)
+    optic_high = jnp.where(wl_index == 0, optic_theirs, optic_mine)
+    optic_got = jnp.concatenate([optic_low, optic_high], 0)
     spec = forward_cols(got)
 
     width = spec.shape[-1]

time: 836 us -> 796 us (0.952)
  waiting for transfers between devices: 308 us -> 257 us
  local copies, waits for them, and re-layouts: 166 us -> 195 us
  other arithmetic: 87.3 us -> 74.2 us
    all_to_all x1, waiting for transfers between devices: 126 us -> 82.7 us  [local_split(): lax.all_to_all(optic_grouped, 'row', split_axis=0, concat_axis=3, tiled=T...]
    unnamed x99 -> x89, local copies, waits for them, and re-layouts: 59.8 us -> 46.6 us
    optimization_barrier x0 -> x1, local copies, waits for them, and re-layouts: none -> 11.5 us  [local_split(): optic_own, sent = lax.optimization_barrier((optic_own, sent))]
    squeeze x0 -> x3, local copies, waits for them, and re-layouts: none -> 10.4 us  [the longest x1 5.6 us: combine(): flipped = spec[1]]
  transfers between devices with their start and end apart: 4 -> 4, of which waited for: 3 -> 3; matrix products, arithmetic and copies ran while one was open for 17% -> 16% of each run, Pallas kernels for 0% -> 0%
where the time goes in v5:
time: 796 us; the launch traced here: 787 us
  waiting for transfers between devices  257 us (32%)
  local copies, waits for them, and re-layouts  195 us (24%)
  matrix products  141 us (18%)
  blocking collectives  98.4 us (12%)
  other arithmetic  74.2 us (9%)
  starting transfers between devices  15 us (2%)
    all_to_all x1, blocking collectives, local_split(): lax.all_to_all(back, 'row', split_axis=1, concat_axis=1, tiled=True)  98.4 us
    ppermute x1, waiting for transfers between devices, local_split(): other = lax.ppermute(returned, 'wl', perm=swap)  90.7 us
    ppermute x1, waiting for transfers between devices, local_split(): lax.ppermute(split_lanes(optic_own, 1 - wl_index), 'wl', perm=swap)  84 us
    all_to_all x1, waiting for transfers between devices, local_split(): lax.all_to_all(optic_grouped, 'row', split_axis=0, concat_axis=3, tiled=T...  82.7 us
    unnamed x89, local copies, waits for them, and re-layouts  46.6 us
    dot_general x1, matrix products, inverse_rows(): first = jnp.einsum('oafem,emRj->oafRj', first_tab, canon, precision=PRECISE)  31.9 us
    another operation x10, other arithmetic, twist(): jnp.stack([real * cos_part - imag * sin_part, real * sin_part + imag * co...  29.9 us
    dot_general x1, matrix products, forward_rows(): jnp.einsum('oaern,oenfk->oarfk', turned, second_tab, precision=PRECISE)  26 us
  transfers between devices with their start and end apart: 4, of which 3 were waited for; matrix products, arithmetic and copies ran while one was open for 16% of the time, Pallas kernels for 0%

profile of v5, /device:TPU:10, one launch (start us, length us, event | category | flops | bytes accessed | tf_op | source)
XLA Modules:
  0.0 786.9 jit_solution(283396220708309108)
XLA Ops:
  40.9 4.8 convolution_convert_fusion
  45.8 7.7 pad_maximum_fusion
  53.5 6.6 all-to-all-start
  60.1 5.2 copy.265
  65.8 16.3 %fusion.9 = f32[2,32,2,256,128]{4,1,3,2,0:T(8,128)} fusion(f32[1,2,2,32,32]{4,3,2,1,0:T(8,128)S(1)} %fusion.77, f32[1,2,2,32,32]{4,3,2,1,0:T(8,128)S(1)} %maximum_bitcast_fusion.24, f32[2,256,32,128]{3,2,1,0:T(8,128)S(1)} %bitcast.464), kind=kOutput, calls=%fused_computation.24 | convolution fusion | flops 3221233664 | bytes 25198592 | tf_op jit(solution)/shard_map/oaedb,drbn->oaern/dot_general | solution.py:71
  84.8 10.5 %subtract_bitcast_fusion = (f32[2,32,1,256,128]{4,1,3,0,2:T(8,128)}, f32[2,32,1,256,128]{4,1,3,0,2:T(8,128)}) fusion(f32[2,32,2,256,128]{4,1,3,2,0:T(8,128)} %fusion.9, f32[2,32,128]{2,1,0:T(8,128)S(1)} %pad_maximum_fusion.11, f32[2,32,128]{2,1,0:T(8,128)S(1)} %pad_maximum_fusion.10), kind=kLoop, calls=%fused_computation.23 | loop fusion | flops 12582912 | bytes 33619968 | tf_op jit(solution)/shard_map/stack | solution.py:37
  95.3 6.8 maximum_bitcast_fusion
  102.2 26.0 %fusion.25 = f32[2,32,256,2,64]{2,4,3,1,0:T(8,128)} fusion(f32[2,32,2,256,128,1]{4,1,3,0,2,5:T(8,128)S(1)} %maximum_bitcast_fusion, f32[1,2,2,64,128]{4,3,2,1,0:T(8,128)S(1)} %maximum_bitcast_fusion.17, f32[1,2,2,64,128]{4,3,2,1,0:T(8,128)S(1)} %maximum_bitcast_fusion.16), kind=kOutput, calls=%fused_computation.54 | convolution fusion | flops 6442516480 | bytes 25427968 | tf_op jit(solution)/shard_map/oaern,oenfk->oarfk/dot_general | solution.py:81
  128.2 10.2 %reshape.1141 = f32[2,32,256,2,16,4]{2,5,4,3,1,0:T(4,128)} reshape(f32[2,32,256,2,64]{2,4,3,1,0:T(8,128)} %fusion.25) | data formatting | bytes 16777216 | tf_op jit(solution)/shard_map/reshape | solution.py:86
  138.4 8.2 %copy.171 = f32[2,32,256,2,16,4]{2,1,5,0,3,4:T(8,128)S(1)} copy(f32[2,32,256,2,16,4]{2,5,4,3,1,0:T(4,128)} %reshape.1141) | data formatting | bytes 16777216 | tf_op jit(solution)/shard_map/reshape | solution.py:86
  159.5 82.7 %all-to-all-done = bf16[16,2,2,256,256]{3,4,2,1,0:T(8,128)(2,1)} async-done(((bf16[16,2,2,256,256]{3,4,2,1,0:T(8,128)(2,1)}), bf16[16,2,2,256,256]{3,4,2,1,0:T(8,128)(2,1)}, u32[]{:S(2)}, u32[]{:S(2)}) %all-to-all-start) | async-done | bytes 8388640 | tf_op jit(solution)/shard_map/all_to_all | solution.py:225
  242.2 11.5 %copy.167 = bf16[1,2,2,16,256,256]{5,4,3,2,1,0:T(8,128)(2,1)} copy(bf16[1,2,2,16,256,256]{4,5,2,1,3,0:T(8,128)(2,1)} %bitcast.54) | data formatting | bytes 16777216 | tf_op jit(solution)/shard_map/all_to_all | solution.py:225
  253.6 5.4 all-to-all-start.1
  259.0 11.5 %copy.173 = bf16[2,2,4096,256]{2,3,1,0:T(8,128)(2,1)} copy(bf16[2,2,4096,256]{3,2,1,0:T(8,128)(2,1)} %bitcast.467) | data formatting | bytes 16777216 | tf_op jit(solution)/shard_map/optimization_barrier | solution.py:230
  270.5 8.0 %constant_dynamic-slice_fusion.1 = (bf16[2,2,4096,2,1,64]{2,5,4,3,1,0:T(8,128)(2,1)}, bf16[2,2,4096,2,1,64]{2,5,4,3,1,0:T(8,128)(2,1)}) fusion(bf16[2,2,4096,2,2,64]{2,5,4,3,1,0:T(8,128)(2,1)} %bitcast.468, s32[]{:T(128)S(6)} %select_n.431, s32[]{:T(128)S(6)} %select_n.432), kind=kLoop, calls=%fused_computation.314 | loop fusion | bytes 16777224 | tf_op jit(solution)/shard_map/jit(dynamic_index_in_dim)/dynamic_slice | solution.py:176
  287.4 84.0 %collective-permute-done = bf16[2,2,4096,128]{2,3,1,0:T(8,128)(2,1)} collective-permute-done((bf16[2,2,4096,128]{2,3,1,0:T(8,128)(2,1)}, bf16[2,2,4096,128]{2,3,1,0:T(8,128)(2,1)}, u32[]{:S(2)}, u32[]{:S(2)}) %collective-permute-start) | collective-permute-done | bytes 4194336 | tf_op jit(solution)/shard_map/ppermute | solution.py:233
  371.4 5.8 bitcast_select_fusion
  377.2 5.3 copy.174
  382.5 11.5 %fusion.22 = f32[2,32,2,128,128]{4,1,3,2,0:T(8,128)S(1)} fusion(f32[2,32,128,128,1,1]{3,2,1,0,5,4:T(8,128)} %bitcast.472, f32[1,2,2,32,32]{4,3,2,1,0:T(8,128)S(1)} %fusion.77, f32[1,2,2,32,32]{4,3,2,1,0:T(8,128)S(1)} %maximum_bitcast_fusion.24), kind=kOutput, calls=%fused_computation.53 | convolution fusion | flops 1610620928 | bytes 12615680 | tf_op jit(solution)/shard_map/oafeb,ebnj->oafnj/dot_general | solution.py:97
  398.1 12.2 %fusion.19 = f32[2,2,128,32,128]{4,2,3,1,0:T(8,128)S(1)} fusion(f32[2,32,2,128,128,1]{4,1,3,0,2,5:T(8,128)S(1)} %maximum_bitcast_fusion.1, f32[1,2,2,128,128]{4,3,2,1,0:T(8,128)S(1)} %fusion.57, f32[1,2,2,128,128]{4,3,2,1,0:T(8,128)S(1)} %maximum_bitcast_fusion.13), kind=kOutput, calls=%fused_computation.52 | convolution fusion | flops 6442582016 | bytes 17301504 | tf_op jit(solution)/shard_map/ofekn,oaenj->ofkaj/dot_general | solution.py:107
  418.8 6.6 copy.181
  425.5 5.6 copy.184
  473.3 5.9 fusion.28
  482.1 98.4 %all_to_all.35 = f32[2,16,256,128]{3,2,0,1:T(8,128)} all-to-all(f32[2,16,256,128]{3,2,0,1:T(8,128)S(1)} %copy.198), channel_id=1, replica_groups=mesh['wl'=2,'row'=16] {'row'}, dimensions={1} | all-to-all | bytes 8388608 | tf_op jit(solution)/shard_map/all_to_all | solution.py:247
  580.5 5.3 copy.200
  588.2 90.7 %collective-permute-done.1 = f32[2,16,256,128]{2,3,1,0:T(8,128)} collective-permute-done((f32[2,16,256,128]{2,3,1,0:T(8,128)}, f32[2,16,256,128]{2,3,1,0:T(8,128)}, u32[]{:S(2)}, u32[]{:S(2)}) %collective-permute-start.1) | collective-permute-done | bytes 4194336 | tf_op jit(solution)/shard_map/ppermute | solution.py:248
  688.6 10.3 %copy.226 = f32[2,16,256,256,1,1]{3,1,0,2,5,4:T(8,128)} copy(f32[2,16,256,256,1,1]{2,3,1,0,5,4:T(8,128)} %bitcast.466) | data formatting | bytes 16777216 | tf_op jit(solution)/shard_map/reshape | solution.py:187
  698.9 31.9 %convolution_bitcast_fusion = f32[2,32,2,256,256]{4,1,3,2,0:T(8,128)} fusion(f32[2,16,256,256,1,1]{3,1,0,2,5,4:T(8,128)} %copy.226, f32[2,32,2,2,16,1]{1,4,3,5,2,0:T(8,128)S(1)} %maximum_bitcast_fusion.45), kind=kOutput, calls=%fused_computation.3 | convolution fusion | flops 3221225472 | bytes 41959424 | tf_op jit(solution)/shard_map/oafem,emRj->oafRj/dot_general | solution.py:129
  735.4 6.8 add_select_fusion
  747.7 13.9 %fusion.3 = f32[32,256,2,64,1]{1,3,4,2,0:T(8,128)S(1)} fusion(f32[32,2,256,128,1]{3,0,2,1,4:T(8,128)S(1)} %maximum_bitcast_fusion.3, f32[2,2,128,2,64]{2,4,1,3,0:T(8,128)S(1)} %fusion.55), kind=kOutput, calls=%fused_computation.16 | convolution fusion | flops 3221225472 | bytes 12713984 | tf_op jit(solution)/shard_map/aeRu,eufk->aRfk/dot_general | solution.py:147
  762.5 14.1 %fusion.13 = f32[2,256,64,32]{1,2,0,3:T(8,128)S(1)} fusion(f32[32,256,2,64,1]{1,3,4,2,0:T(8,128)S(1)} %fusion.3, f32[32,2,256,128,1]{3,0,2,1,4:T(8,128)S(1)} %maximum_bitcast_fusion.2, f32[2,2,128,2,64]{2,4,1,3,0:T(8,128)S(1)} %fusion.55), kind=kOutput, calls=%fused_computation.38 | convolution fusion | flops 3222274048 | bytes 16908288 | tf_op jit(solution)/shard_map/aeRu,eufk->aRfk/dot_general | solution.py:146
  781.1 5.3 copy.207
  (191 shorter events, 145.2 us)
Async XLA Ops:
  0.0 40.9 %copy-start.18 = (pred[128]{0:T(512)(128)(4,1)}, pred[128]{0:T(512)(128)(4,1)S(1)}, u32[]{:S(2)}) copy-start(pred[128]{0:T(512)(128)(4,1)S(1)} %get-tuple-element.191) | copy-start | bytes 388
  27.7 10.4 %copy-start.12 = (bf16[2,2,256,128]{2,3,1,0:T(8,128)(2,1)S(1)}, bf16[2,2,256,128]{2,3,1,0:T(8,128)(2,1)}, u32[]{:S(2)}) copy-start(bf16[2,2,256,128]{2,3,1,0:T(8,128)(2,1)} %copy.259) | copy-start | bytes 786436
  27.7 11.0 %copy-start.11 = (bf16[2,2,256,128]{2,3,1,0:T(8,128)(2,1)S(1)}, bf16[2,2,256,128]{2,3,1,0:T(8,128)(2,1)}, u32[]{:S(2)}) copy-start(bf16[2,2,256,128]{2,3,1,0:T(8,128)(2,1)} %copy.260) | copy-start | bytes 786436
  28.8 10.6 %copy-start.10 = (bf16[2,2,256,128]{2,3,1,0:T(8,128)(2,1)S(1)}, bf16[2,2,256,128]{2,3,1,0:T(8,128)(2,1)}, u32[]{:S(2)}) copy-start(bf16[2,2,256,128]{2,3,1,0:T(8,128)(2,1)} %copy.261) | copy-start | bytes 786436
  28.9 11.3 %copy-start.9 = (bf16[2,2,256,128]{2,3,1,0:T(8,128)(2,1)S(1)}, bf16[2,2,256,128]{2,3,1,0:T(8,128)(2,1)}, u32[]{:S(2)}) copy-start(bf16[2,2,256,128]{2,3,1,0:T(8,128)(2,1)} %copy.262) | copy-start | bytes 786436
  53.5 188.7 %all-to-all-start = ((bf16[16,2,2,256,256]{3,4,2,1,0:T(8,128)(2,1)}), bf16[16,2,2,256,256]{3,4,2,1,0:T(8,128)(2,1)}, u32[]{:S(2)}, u32[]{:S(2)}) async-start(bf16[16,2,2,256,256]{3,4,2,1,0:T(8,128)(2,1)} %pad_maximum_fusion), calls=%async_computation | async-start | bytes 16777216 | tf_op jit(solution)/shard_map/all_to_all | solution.py:225
  65.8 16.3 %copy-start.13 = (f32[1,2,32,32]{3,2,1,0:T(8,128)}, f32[1,2,32,32]{3,2,1,0:T(8,128)S(1)}, u32[]{:S(2)}) copy-start(f32[1,2,32,32]{3,2,1,0:T(8,128)S(1)} %get-tuple-element.169) | copy-start | bytes 24580
  65.8 16.3 %copy-start.15 = (f32[1,2,32,32]{3,2,1,0:T(8,128)}, f32[1,2,32,32]{3,2,1,0:T(8,128)S(1)}, u32[]{:S(2)}) copy-start(f32[1,2,32,32]{3,2,1,0:T(8,128)S(1)} %get-tuple-element.170) | copy-start | bytes 24580
  138.4 9.5 %copy-start.20 = (s32[4]{0:T(128)S(1)}, s32[4]{0:T(128)}, u32[]{:S(2)}) copy-start(s32[4]{0:T(128)} %constant.340.clone.1) | copy-start | bytes 52
  146.6 3.4 copy-start.4
  253.6 123.6 %all-to-all-start.1 = ((f32[16,2,256,128]{2,3,1,0:T(8,128)}), f32[16,2,256,128]{2,3,1,0:T(8,128)}, u32[]{:S(2)}, u32[]{:S(2)}) async-start(f32[16,2,256,128]{2,3,1,0:T(8,128)} %bitcast.473), calls=%async_computation.1 | async-start | bytes 8388608 | tf_op jit(solution)/shard_map/all_to_all | solution.py:231
  270.5 9.7 %copy-start.17 = (f32[4,2]{0,1:T(2,128)S(1)}, f32[4,2]{0,1:T(2,128)}, u32[]{:S(2)}) copy-start(f32[4,2]{0,1:T(2,128)} %param.23) | copy-start | bytes 100
  278.5 92.9 %collective-permute-start = (bf16[2,2,4096,128]{2,3,1,0:T(8,128)(2,1)}, bf16[2,2,4096,128]{2,3,1,0:T(8,128)(2,1)}, u32[]{:S(2)}, u32[]{:S(2)}) collective-permute-start(bf16[2,2,4096,128]{2,3,1,0:T(8,128)(2,1)} %bitcast.95), channel_id=1, source_target_pairs={{0,16},{16,0},{1,17},{17,1},{2,18},{18,2},{3,19},{19,3},{4,20},{20... | collective-permute-start | bytes 12582920 | tf_op jit(solution)/shard_map/ppermute | solution.py:233
  438.1 3.5 copy-start.2
  441.6 2.2 copy-start
  441.6 3.5 copy-start.1
  441.6 4.1 copy-start.5
  454.9 7.4 copy-start.7
  462.3 4.8 copy-start.14
  462.3 4.8 copy-start.16
  464.1 3.0 copy-start.8
  585.8 93.1 %collective-permute-start.1 = (f32[2,16,256,128]{2,3,1,0:T(8,128)}, f32[2,16,256,128]{2,3,1,0:T(8,128)}, u32[]{:S(2)}, u32[]{:S(2)}) collective-permute-start(f32[2,16,256,128]{2,3,1,0:T(8,128)} %copy.200), channel_id=1, source_target_pairs={{0,16},{16,0},{1,17},{17,1},{2,18},{18,2},{3,19},{19,3},{4,20},{20... | collective-permute-start | bytes 12582920 | tf_op jit(solution)/shard_map/ppermute | solution.py:248
  685.3 3.3 copy-start.3
  730.8 4.5 copy-start.19
  747.6 13.9 %copy-start.6 = (f32[32,1,256,128]{3,0,2,1:T(8,128)S(1)}, f32[32,1,256,128]{3,0,2,1:T(8,128)}, u32[]{:S(2)}) copy-start(f32[32,1,256,128]{3,0,2,1:T(8,128)} %get-tuple-element.122) | copy-start | bytes 12582916

commit v6 on v3

--- a/solution.py
+++ b/solution.py
@@ -121,9 +121,10 @@
     return second.reshape((2, length, width))
 
 
-def inverse_rows(canon, length, scale):
+def inverse_rows(canon, length, scale, k_count=None, k_start=0):
     mcount, rows_here, width = canon.shape[1], canon.shape[2], canon.shape[3]
     across = width // 2
+    k_count = across if k_count is None else k_count
     first_tab = jnp.transpose(small_tables(NARROW, mcount, NARROW, (1.0, -1.0)), (0, 3, 1, 2, 4))
     first = jnp.einsum("oafem,emRj->oafRj", first_tab, canon, precision=PRECISE)
     lower = first[0, :, :, :, :across]
@@ -136,11 +137,15 @@
     cos_dn, sin_dn = phase(ids(NARROW)[:, None], ids(across)[None, :], length, -1.0)
     lower = twist(lower, 1, cos_up[:, None, :], sin_up[:, None, :])
     upper = twist(upper, 1, cos_dn[:, None, :], sin_dn[:, None, :])
-    tabs = small_tables(across, across, across, (1.0, -1.0)) * scale
-    tabs = jnp.transpose(tabs, (0, 2, 4, 1, 3))
+    tabs = []
+    for orient in (1.0, -1.0):
+        k_ids = ids(k_count)[:, None] + k_start
+        cos_part, sin_part = phase(k_ids, ids(across)[None, :], across, orient)
+        tabs.append(cblock(cos_part, sin_part))
+    tabs = jnp.transpose(jnp.stack(tabs) * scale, (0, 2, 4, 1, 3))
     out = jnp.einsum("aeRu,eufk->aRfk", lower, tabs[0], precision=PRECISE)
     out = out + jnp.einsum("aeRu,eufk->aRfk", upper, tabs[1], precision=PRECISE)
-    return jnp.transpose(out, (2, 1, 3, 0)).reshape((2, rows_here, length))
+    return jnp.transpose(out, (2, 1, 3, 0)).reshape((2, rows_here, k_count * NARROW))
 
 
 def pair_optics(optics):
@@ -237,12 +242,10 @@
     summed = kept + lax.ppermute(given, "wl", perm=[(0, 1), (1, 0)])
     returned = lax.all_to_all(summed, "row", split_axis=1, concat_axis=1, tiled=True)
     returned = groups_to_canon(returned, mcount, 1)
-    result_image = inverse_rows(returned, length, norm_factor)
-    half = length // 2
-    result_image = result_image.reshape((2, own_rows, 2, half))
-    mine = lax.dynamic_index_in_dim(result_image, wl_index, 2, keepdims=False)
-    theirs = lax.dynamic_index_in_dim(result_image, 1 - wl_index, 2, keepdims=False)
+    k_half = across // 2
+    theirs = inverse_rows(returned, length, norm_factor, k_half, (1 - wl_index) * k_half)
     taken = lax.ppermute(theirs, "wl", perm=[(0, 1), (1, 0)])
+    mine = inverse_rows(returned, length, norm_factor, k_half, wl_index * k_half)
     upper = jnp.where(wl_index == 0, mine, taken)
     lower = jnp.where(wl_index == 0, taken, mine)
     return jnp.concatenate([upper, lower], 1)

time: 743 us -> 742 us (level)
  matrix products: 118 us -> 133 us
  waiting for transfers between devices: 343 us -> 328 us
    ppermute x1, waiting for transfers between devices: 44.8 us -> 29.8 us  [local(): taken = lax.ppermute(theirs, 'wl', perm=[(0, 1), (1, 0)])]
    dot_general x1 -> x2, matrix products: 6.56 us -> 15 us  [inverse_rows(): out = out + jnp.einsum('aeRu,eufk->aRfk', upper, tabs[1], precision=PRECISE)]
    unnamed x106 -> x108, local copies, waits for them, and re-layouts: 56.9 us -> 57.1 us
  transfers between devices with their start and end apart: 6 -> 6, of which waited for: 5 -> 5; matrix products, arithmetic and copies ran while one was open for 26% -> 28% of each run, Pallas kernels for 0% -> 0%
where the time goes in v6:
time: 742 us; the launch traced here: 731 us
  waiting for transfers between devices  328 us (44%)
  local copies, waits for them, and re-layouts  173 us (23%)
  matrix products  133 us (18%)
  other arithmetic  70.7 us (10%)
  starting transfers between devices  22.3 us (3%)
    all_to_all x1, waiting for transfers between devices, local(): lax.all_to_all(summed, 'row', split_axis=1, concat_axis=1, tiled=True)  91.5 us
    ppermute x1, waiting for transfers between devices, local(): summed = kept + lax.ppermute(given, 'wl', perm=[(0, 1), (1, 0)])  90.6 us
    ppermute x1, waiting for transfers between devices, local(): other = lax.ppermute(got, 'wl', perm=[(0, 1), (1, 0)])  83.3 us
    unnamed x108, local copies, waits for them, and re-layouts  57.1 us
    all_to_all x1, waiting for transfers between devices, local(): lax.all_to_all(sent, 'row', split_axis=0, concat_axis=2, tiled=True)[0]  32.8 us
    ppermute x1, waiting for transfers between devices, local(): taken = lax.ppermute(theirs, 'wl', perm=[(0, 1), (1, 0)])  29.8 us
    dot_general x1, matrix products, forward_cols(): jnp.einsum('ofekn,oaenj->ofkaj', second_tab, turned, precision=PRECISE)  25 us
    another operation x10, other arithmetic, twist(): jnp.stack([real * cos_part - imag * sin_part, real * sin_part + imag * co...  20.6 us
  transfers between devices with their start and end apart: 6, of which 5 were waited for; matrix products, arithmetic and copies ran while one was open for 28% of the time, Pallas kernels for 0%

profile of v6, /device:TPU:10, one launch (start us, length us, event | category | flops | bytes accessed | tf_op | source)
XLA Modules:
  0.0 731.1 jit_solution(4578621857928437978)
XLA Ops:
  5.1 6.8 fusion.37
  15.0 13.9 %fusion.9 = f32[2,32,128,2,64,1]{2,4,5,3,1,0:T(8,128)S(1)} fusion(f32[2,32,2,128,128,1]{4,1,3,0,2,5:T(8,128)S(1)} %maximum_bitcast_fusion.1, f32[1,2,2,64,128]{4,3,2,1,0:T(8,128)S(1)} %maximum_bitcast_fusion.19, f32[1,2,2,64,128]{4,3,2,1,0:T(8,128)S(1)} %maximum_bitcast_fusion.18), kind=kOutput, calls=%fused_computation.18 | convolution fusion | flops 3221291008 | bytes 12845056 | tf_op jit(solution)/shard_map/oaern,oenfk->oarfk/dot_general | solution.py:81
  39.6 6.2 all-to-all-start.1
  97.6 7.8 %pad_maximum_fusion = bf16[16,2,2,256,256]{3,4,2,1,0:T(8,128)(2,1)} fusion(bf16[16,2,2,256,128]{3,4,2,1,0:T(8,128)(2,1)} %convolution_convert_fusion, bf16[16,2,2,256,128]{3,4,2,1,0:T(8,128)(2,1)} %bitcast_dynamic-update-slice_fusion.15), kind=kLoop, calls=%fused_computation.5 | loop fusion | flops 16777216 | bytes 16777216 | tf_op jit(solution)/shard_map/concatenate | solution.py:169
  105.4 32.8 %all-to-all-done.1 = f32[16,2,128,256]{2,3,1,0:T(8,128)} async-done(((f32[16,2,128,256]{2,3,1,0:T(8,128)}), f32[16,2,128,256]{2,3,1,0:T(8,128)}, u32[]{:S(2)}, u32[]{:S(2)}) %all-to-all-start.1) | async-done | bytes 4194336 | tf_op jit(solution)/shard_map/all_to_all | solution.py:190
  138.1 5.4 all-to-all-start
  143.5 5.3 copy.211
  158.5 83.3 %collective-permute-done = f32[2,2048,256]{2,1,0:T(8,128)} collective-permute-done((f32[2,2048,256]{2,1,0:T(8,128)}, f32[2,2048,256]{2,1,0:T(8,128)}, u32[]{:S(2)}, u32[]{:S(2)}) %collective-permute-start) | collective-permute-done | bytes 4194336 | tf_op jit(solution)/shard_map/ppermute | solution.py:191
  241.8 5.3 copy.212
  255.1 13.3 %copy.214 = f32[2,16,2,128,256]{4,2,1,0,3:T(2,128)} copy(f32[2,16,2,128,256]{3,4,0,1,2:T(8,128)} %pad_maximum_fusion.1) | data formatting | bytes 16777216 | tf_op jit(solution)/shard_map/stack | solution.py:196
  268.4 11.0 %reshape.1518 = f32[2,32,128,256,1,1]{3,1,0,2,4,5:T(8,128)} reshape(f32[2,16,2,128,256]{4,2,1,0,3:T(2,128)} %copy.214) | data formatting | bytes 16777216 | tf_op jit(solution)/shard_map/reshape;reshape | solution.py:95
  279.4 16.7 %fusion.12 = f32[2,32,2,128,256]{4,1,3,2,0:T(8,128)S(1)} fusion(f32[2,32,128,256,1,1]{3,1,0,2,4,5:T(8,128)} %reshape.1518, f32[1,2,2,32,32]{4,3,2,1,0:T(8,128)S(1)} %copy-done.15, f32[1,2,2,32,32]{4,3,2,1,0:T(8,128)S(1)} %copy-done.17), kind=kOutput, calls=%fused_computation.23 | convolution fusion | flops 3221233664 | bytes 25198592 | tf_op jit(solution)/shard_map/oafeb,ebnj->oafnj/dot_general | solution.py:97
  296.1 6.0 subtract_bitcast_fusion
  307.2 25.0 %fusion.15 = f32[2,2,128,32,256]{4,2,3,1,0:T(8,128)S(1)} fusion(f32[2,32,2,128,256,1]{4,1,3,0,2,5:T(8,128)S(1)} %maximum_bitcast_fusion, f32[1,2,2,128,128]{4,3,2,1,0:T(8,128)} %fusion.54, f32[1,2,2,128,128]{4,3,2,1,0:T(8,128)} %maximum_bitcast_fusion.11), kind=kOutput, calls=%fused_computation.24 | convolution fusion | flops 12885032960 | bytes 34078720 | tf_op jit(solution)/shard_map/ofekn,oaenj->ofkaj/dot_general | solution.py:107
  332.2 5.8 copy-done.2
  342.3 8.2 %copy.220 = f32[1,2,128,32,256]{4,3,2,1,0:T(8,128)S(1)} copy(f32[1,2,128,32,256]{4,2,3,1,0:T(8,128)} %slice.369) | data formatting | bytes 16777216 | tf_op jit(solution)/shard_map/slice | solution.py:213
  367.8 11.4 %copy.205 = bf16[1,2,2,16,256,256]{5,4,3,2,1,0:T(8,128)(2,1)} copy(bf16[1,2,2,16,256,256]{4,5,2,1,3,0:T(8,128)(2,1)} %bitcast.54) | data formatting | bytes 16777216 | tf_op jit(solution)/shard_map/all_to_all | solution.py:206
  379.2 11.1 %fusion.20 = (f32[1,4096,256]{2,1,0:T(8,128)S(1)}, f32[1,4096,256]{2,1,0:T(8,128)S(1)}) fusion(bf16[2,2,4096,256]{3,2,1,0:T(8,128)(2,1)} %bitcast.504, f32[]{:T(128)} %bitcast.123, f32[]{:T(128)} %bitcast.122, f32[2,4096,256]{2,1,0:T(8,128)} %maximum_select_fusion, f32[1,1,128,32,256]{4,3,2,1,0:T(8,128)} %copy.219, f32[]{:T(128)} %bitcast.128, f32[]{:T(128)} %bitcast.127, ...), kind=kLoop, calls=%fused_computation.37 | loop fusion | flops 36700160 | bytes 33554448 | tf_op jit(solution)/shard_map/sub | solution.py:229
  395.2 7.7 %fusion.38 = f32[32,2,128,256]{3,0,2,1:T(8,128)S(1)} fusion(f32[1,32,128,256]{3,1,0,2:T(8,128)S(1)} %copy.223, f32[1,32,128,256]{3,1,0,2:T(8,128)S(1)} %copy.222, f32[1,2,32,32]{3,2,1,0:T(8,128)S(1)} %copy-done.21, f32[1,2,32,32]{3,2,1,0:T(8,128)S(1)} %copy-done.19), kind=kOutput, calls=%fused_computation.80 | convolution fusion | flops 1612713984 | bytes 16793600 | tf_op jit(solution)/shard_map/afeb,ebnj->afnj/dot_general | solution.py:116
  406.0 12.1 %fusion.34 = f32[2,128,32,256]{3,1,2,0:T(8,128)S(1)} fusion(f32[32,2,128,256]{3,0,2,1:T(8,128)S(1)} %pad_maximum_fusion.2, f32[1,2,128,128]{3,2,1,0:T(8,128)S(1)} %copy-done.11, f32[1,2,128,128]{3,2,1,0:T(8,128)S(1)} %get-tuple-element.153), kind=kOutput, calls=%fused_computation.78 | convolution fusion | flops 6442516480 | bytes 17039360 | tf_op jit(solution)/shard_map/fken,aenj->fkaj/dot_general | solution.py:120
  429.1 90.6 %collective-permute-done.1 = f32[2,16,128,256]{3,2,1,0:T(8,128)} collective-permute-done((f32[2,16,128,256]{3,2,1,0:T(8,128)}, f32[2,16,128,256]{3,2,1,0:T(8,128)}, u32[]{:S(2)}, u32[]{:S(2)}) %collective-permute-start.1) | collective-permute-done | bytes 4194336 | tf_op jit(solution)/shard_map/ppermute | solution.py:242
  523.7 5.3 copy.228
  528.9 6.0 all-to-all-start.2
  535.8 91.5 %all-to-all-done.2 = f32[2,16,128,256]{3,0,2,1:T(2,128)} async-done(((f32[2,16,128,256]{3,0,2,1:T(2,128)}), f32[2,16,128,256]{3,0,2,1:T(2,128)}, u32[]{:S(2)}, u32[]{:S(2)}) %all-to-all-start.2) | async-done | bytes 4194336 | tf_op jit(solution)/shard_map/all_to_all | solution.py:243
  627.3 15.4 %convolution_bitcast_fusion = f32[2,32,2,128,256]{4,1,3,2,0:T(8,128)S(1)} fusion(f32[2,16,128,256,1,1]{3,0,2,1,5,4:T(2,128)} %bitcast.149, f32[1,2,2,32,16]{3,4,2,1,0:T(8,128)S(1)} %maximum_bitcast_fusion.40, f32[1,2,2,32,16]{3,4,2,1,0:T(8,128)S(1)} %maximum_bitcast_fusion.39), kind=kOutput, calls=%fused_computation.25 | convolution fusion | flops 1610616832 | bytes 20987904 | tf_op jit(solution)/shard_map/oafem,emRj->oafRj/dot_general | solution.py:129
  642.6 5.8 copy-done.3
  658.0 6.9 fusion.26
  664.9 7.1 fusion.39
  675.3 8.1 %fusion.28 = f32[32,128,2,64,1]{1,3,4,2,0:T(8,128)S(1)} fusion(f32[32,2,128,128,1]{3,0,2,1,4:T(8,128)} %copy-done.6, f32[2,2,128,2,64]{2,4,1,3,0:T(8,128)S(1)} %fusion.51), kind=kOutput, calls=%fused_computation.72 | convolution fusion | flops 1610612736 | bytes 6422528 | tf_op jit(solution)/shard_map/aeRu,eufk->aRfk/dot_general | solution.py:147
  683.4 6.9 fusion.40
  691.4 29.8 %collective-permute-done.2 = f32[2,128,2048]{1,2,0:T(8,128)} collective-permute-done((f32[2,128,2048]{1,2,0:T(8,128)S(1)}, f32[2,128,2048]{1,2,0:T(8,128)}, u32[]{:S(2)}, u32[]{:S(2)}) %collective-permute-start.2) | collective-permute-done | bytes 2097184 | tf_op jit(solution)/shard_map/ppermute | solution.py:247
  725.4 5.3 copy.237
  (215 shorter events, 153.6 us)
Async XLA Ops:
  0.0 150.6 %copy-start = (f32[4,2]{0,1:T(2,128)S(1)}, f32[4,2]{0,1:T(2,128)}, u32[]{:S(2)}) copy-start(f32[4,2]{0,1:T(2,128)} %param.23) | copy-start | bytes 100
  4.5 7.4 %copy-start.14 = (f32[1,2,2,32,32]{4,3,2,1,0:T(8,128)}, f32[1,2,2,32,32]{4,3,2,1,0:T(8,128)S(1)}, u32[]{:S(2)}) copy-start(f32[1,2,2,32,32]{4,3,2,1,0:T(8,128)S(1)} %fusion.74) | copy-start | bytes 49156
  5.1 6.8 copy-start.16
  29.0 3.7 copy-start.30
  31.8 2.9 copy-start.8
  39.6 98.6 %all-to-all-start.1 = ((f32[16,2,128,256]{2,3,1,0:T(8,128)}), f32[16,2,128,256]{2,3,1,0:T(8,128)}, u32[]{:S(2)}, u32[]{:S(2)}) async-start(f32[16,2,128,256]{2,3,1,0:T(8,128)} %scatter.4), calls=%async_computation.1 | async-start | bytes 8388608 | tf_op jit(solution)/shard_map/all_to_all | solution.py:190
  45.8 46.9 %copy-start.28 = (pred[128]{0:T(512)(128)(4,1)}, pred[128]{0:T(512)(128)(4,1)S(1)}, u32[]{:S(2)}) copy-start(pred[128]{0:T(512)(128)(4,1)S(1)} %get-tuple-element.193) | copy-start | bytes 388
  57.4 8.3 %copy-start.12 = (bf16[2,2,256,128]{3,2,1,0:T(8,128)(2,1)S(1)}, bf16[2,2,256,128]{3,2,1,0:T(8,128)(2,1)}, u32[]{:S(2)}) copy-start(bf16[2,2,256,128]{3,2,1,0:T(8,128)(2,1)} %get-tuple-element.143) | copy-start | bytes 786436
  63.3 2.4 copy-start.13
  138.1 229.7 %all-to-all-start = ((bf16[16,2,2,256,256]{3,4,2,1,0:T(8,128)(2,1)}), bf16[16,2,2,256,256]{3,4,2,1,0:T(8,128)(2,1)}, u32[]{:S(2)}, u32[]{:S(2)}) async-start(bf16[16,2,2,256,256]{3,4,2,1,0:T(8,128)(2,1)} %pad_maximum_fusion), calls=%async_computation | async-start | bytes 16777216 | tf_op jit(solution)/shard_map/all_to_all | solution.py:206
  148.9 92.9 %collective-permute-start = (f32[2,2048,256]{2,1,0:T(8,128)}, f32[2,2048,256]{2,1,0:T(8,128)}, u32[]{:S(2)}, u32[]{:S(2)}) collective-permute-start(f32[2,2048,256]{2,1,0:T(8,128)} %bitcast.512), channel_id=1, source_target_pairs={{0,16},{16,0},{1,17},{17,1},{2,18},{18,2},{3,19},{19,3},{4,20},{20... | collective-permute-start | bytes 12582920 | tf_op jit(solution)/shard_map/ppermute | solution.py:191
  153.8 93.3 %copy-start.24 = (f32[32,128]{1,0:T(8,128)}, f32[32,128]{1,0:T(8,128)S(1)}, u32[]{:S(2)}) copy-start(f32[32,128]{1,0:T(8,128)S(1)} %get-tuple-element.219) | copy-start | bytes 49156
  153.8 93.3 %copy-start.26 = (f32[32,128]{1,0:T(8,128)}, f32[32,128]{1,0:T(8,128)S(1)}, u32[]{:S(2)}) copy-start(f32[32,128]{1,0:T(8,128)S(1)} %get-tuple-element.220) | copy-start | bytes 49156
  268.4 11.0 %copy-start.15 = (f32[1,2,2,32,32]{4,3,2,1,0:T(8,128)S(1)}, f32[1,2,2,32,32]{4,3,2,1,0:T(8,128)}, u32[]{:S(2)}) copy-start(f32[1,2,2,32,32]{4,3,2,1,0:T(8,128)} %copy-done.14) | copy-start | bytes 49156
  268.4 11.0 %copy-start.17 = (f32[1,2,2,32,32]{4,3,2,1,0:T(8,128)S(1)}, f32[1,2,2,32,32]{4,3,2,1,0:T(8,128)}, u32[]{:S(2)}) copy-start(f32[1,2,2,32,32]{4,3,2,1,0:T(8,128)} %copy-done.16) | copy-start | bytes 49156
  332.2 5.8 copy-start.2
  392.7 2.5 copy-start.19
  392.7 2.5 copy-start.21
  395.1 7.7 %copy-start.22 = (f32[32,128]{0,1:T(8,128)S(1)}, f32[32,128]{0,1:T(8,128)}, u32[]{:S(2)}) copy-start(f32[32,128]{0,1:T(8,128)} %copy.224) | copy-start | bytes 49156
  395.2 7.7 %copy-start.23 = (f32[32,128]{0,1:T(8,128)S(1)}, f32[32,128]{0,1:T(8,128)}, u32[]{:S(2)}) copy-start(f32[32,128]{0,1:T(8,128)} %copy.225) | copy-start | bytes 49156
  404.3 1.7 copy-start.11
  422.9 4.6 copy-start.7
  427.5 92.1 %collective-permute-start.1 = (f32[2,16,128,256]{3,2,1,0:T(8,128)}, f32[2,16,128,256]{3,2,1,0:T(8,128)}, u32[]{:S(2)}, u32[]{:S(2)}) collective-permute-start(f32[2,16,128,256]{3,2,1,0:T(8,128)} %dynamic-slice_bitcast_fusion), channel_id=1, source_target_pairs={{0,16},{16,0},{1,17},{17,1},{2,18},{18,2},{3,19},{19,3},{4,20},{20... | collective-permute-start | bytes 12582920 | tf_op jit(solution)/shard_map/ppermute | solution.py:242
  528.9 98.3 %all-to-all-start.2 = ((f32[2,16,128,256]{3,0,2,1:T(2,128)}), f32[2,16,128,256]{3,0,2,1:T(2,128)}, u32[]{:S(2)}, u32[]{:S(2)}) async-start(f32[2,16,128,256]{3,0,2,1:T(2,128)} %copy.228), calls=%async_computation.2 | async-start | bytes 8388608 | tf_op jit(solution)/shard_map/all_to_all | solution.py:243
  642.6 5.8 copy-start.3
  649.2 3.1 copy-start.29
  652.3 4.1 copy-start.9
  656.8 8.1 %copy-start.4 = (f32[32,2,128,128,1]{3,0,2,1,4:T(8,128)}, f32[32,2,128,128,1]{3,0,2,1,4:T(8,128)S(1)}, u32[]{:S(2)}) copy-start(f32[32,2,128,128,1]{3,0,2,1,4:T(8,128)S(1)} %maximum_bitcast_fusion.4) | copy-start | bytes 12582916
  658.0 14.0 %copy-start.6 = (f32[32,2,128,128,1]{3,0,2,1,4:T(8,128)}, f32[32,2,128,128,1]{3,0,2,1,4:T(8,128)S(1)}, u32[]{:S(2)}) copy-start(f32[32,2,128,128,1]{3,0,2,1,4:T(8,128)S(1)} %maximum_bitcast_fusion.5) | copy-start | bytes 12582916
  673.2 48.0 %collective-permute-start.2 = (f32[2,128,2048]{1,2,0:T(8,128)S(1)}, f32[2,128,2048]{1,2,0:T(8,128)}, u32[]{:S(2)}, u32[]{:S(2)}) collective-permute-start(f32[2,128,2048]{1,2,0:T(8,128)S(1)} %bitcast.513), channel_id=1, source_target_pairs={{0,16},{16,0},{1,17},{17,1},{2,18},{18,2},{3,19},{19,3},{4,20},{20... | collective-permute-start | bytes 6291464 | tf_op jit(solution)/shard_map/ppermute | solution.py:247
  674.8 8.5 %copy-start.5 = (f32[32,2,128,128,1]{3,0,2,1,4:T(8,128)S(1)}, f32[32,2,128,128,1]{3,0,2,1,4:T(8,128)}, u32[]{:S(2)}) copy-start(f32[32,2,128,128,1]{3,0,2,1,4:T(8,128)} %copy-done.4) | copy-start | bytes 12582916
  723.1 7.6 %copy-start.1 = (f32[4,2]{0,1:T(2,128)S(1)}, f32[4,2]{0,1:T(2,128)}, u32[]{:S(2)}) copy-start(f32[4,2]{0,1:T(2,128)} %param.23) | copy-start | bytes 100
  (5 other events, 3.3 us)

commit v7 on v6

--- a/solution.py
+++ b/solution.py
@@ -106,6 +106,23 @@
     second_tab = small_tables(across, across, across, (-1.0, 1.0))
     second = jnp.einsum("ofekn,oaenj->ofkaj", second_tab, turned, precision=PRECISE)
     return second.reshape((2, 2, length, width))
+
+
+def inverse_cols_half(combined, group_count, half_index):
+    length, width = combined.shape[1], combined.shape[2]
+    across = length // NARROW
+    grid = combined.reshape((2, NARROW, across, width))
+    first_tab = jnp.transpose(small_tables(NARROW, NARROW, NARROW, (1.0,))[0], (2, 0, 1, 3))
+    first = jnp.einsum("afeb,ebnj->afnj", first_tab, grid, precision=PRECISE)
+    cos_part, sin_part = phase(ids(NARROW)[:, None], ids(across)[None, :], length, 1.0)
+    turned = twist(first, 1, cos_part[:, :, None], sin_part[:, :, None])
+    per_group = across // group_count
+    per_half = per_group // 2
+    k_ids = ids(group_count)[:, None] * per_group + half_index * per_half + ids(per_half)[None, :]
+    cos_k, sin_k = phase(k_ids.reshape((-1, 1)), ids(across)[None, :], across, 1.0)
+    second_tab = jnp.transpose(cblock(cos_k, sin_k), (0, 2, 1, 3))
+    second = jnp.einsum("fken,aenj->fkaj", second_tab, turned, precision=PRECISE)
+    return second.reshape((2, group_count, per_half * NARROW, width))
 
 
 def inverse_cols(combined):
@@ -229,17 +246,25 @@
         combined_real = combined_real + resp_real * mixed_real - resp_imag * mixed_imag
         combined_imag = combined_imag + resp_real * mixed_imag + resp_imag * mixed_real
 
-    back = inverse_cols(jnp.stack([combined_real, combined_imag]))
+    stacked = jnp.stack([combined_real, combined_imag])
+    back = inverse_cols(stacked)
     if wl_count != 2 or own_rows * wl_count != rows_here:
         back = back.reshape((2, row_count, rows_here, width))
         returned = lax.all_to_all(back, "row", split_axis=1, concat_axis=1, tiled=True)
         returned = groups_to_canon(returned, mcount, 1)
         result_image = inverse_rows(returned, length, norm_factor)
         return lax.psum_scatter(result_image, "wl", scatter_dimension=2, tiled=True)
-    back = back.reshape((2, row_count, 2, own_rows, width))
-    kept = lax.dynamic_index_in_dim(back, wl_index, 2, keepdims=False)
-    given = lax.dynamic_index_in_dim(back, 1 - wl_index, 2, keepdims=False)
-    summed = kept + lax.ppermute(given, "wl", perm=[(0, 1), (1, 0)])
+    per_group = across // row_count
+    if per_group % 2 == 0 and per_group * row_count == across:
+        given = inverse_cols_half(stacked, row_count, 1 - wl_index)
+        incoming = lax.ppermute(given, "wl", perm=[(0, 1), (1, 0)])
+        kept = inverse_cols_half(stacked, row_count, wl_index)
+    else:
+        back = back.reshape((2, row_count, 2, own_rows, width))
+        kept = lax.dynamic_index_in_dim(back, wl_index, 2, keepdims=False)
+        given = lax.dynamic_index_in_dim(back, 1 - wl_index, 2, keepdims=False)
+        incoming = lax.ppermute(given, "wl", perm=[(0, 1), (1, 0)])
+    summed = kept + incoming
     returned = lax.all_to_all(summed, "row", split_axis=1, concat_axis=1, tiled=True)
     returned = groups_to_canon(returned, mcount, 1)
     k_half = across // 2

time: 742 us -> 734 us (0.989)
  waiting for transfers between devices: 328 us -> 310 us
  matrix products: 133 us -> 145 us
    ppermute x1, waiting for transfers between devices: 90.6 us -> 74.5 us  [local(): incoming = lax.ppermute(given, 'wl', perm=[(0, 1), (1, 0)])]
    dot_general x2 -> x3, matrix products: 19.8 us -> 31 us  [the longest x2 23.3 us: inverse_cols_half(): jnp.einsum('fken,aenj->fkaj', second_tab, turned, precision=PRECISE)]
    unnamed x108 -> x110, local copies, waits for them, and re-layouts: 57.1 us -> 54.5 us
  transfers between devices with their start and end apart: 6 -> 6, of which waited for: 5 -> 5; matrix products, arithmetic and copies ran while one was open for 28% -> 31% of each run, Pallas kernels for 0% -> 0%
where the time goes in v7:
time: 734 us; the launch traced here: 723 us
  waiting for transfers between devices  310 us (42%)
  local copies, waits for them, and re-layouts  170 us (23%)
  matrix products  145 us (20%)
  other arithmetic  71.3 us (10%)
  starting transfers between devices  22.9 us (3%)
    all_to_all x1, waiting for transfers between devices, local(): lax.all_to_all(summed, 'row', split_axis=1, concat_axis=1, tiled=True)  91.3 us
    ppermute x1, waiting for transfers between devices, local(): other = lax.ppermute(got, 'wl', perm=[(0, 1), (1, 0)])  82.8 us
    ppermute x1, waiting for transfers between devices, local(): incoming = lax.ppermute(given, 'wl', perm=[(0, 1), (1, 0)])  74.5 us
    unnamed x110, local copies, waits for them, and re-layouts  54.5 us
    all_to_all x1, waiting for transfers between devices, local(): lax.all_to_all(sent, 'row', split_axis=0, concat_axis=2, tiled=True)[0]  32.1 us
    ppermute x1, waiting for transfers between devices, local(): taken = lax.ppermute(theirs, 'wl', perm=[(0, 1), (1, 0)])  29.8 us
    dot_general x1, matrix products, forward_cols(): jnp.einsum('ofekn,oaenj->ofkaj', second_tab, turned, precision=PRECISE)  25 us
    dot_general x2, matrix products, inverse_cols_half(): jnp.einsum('fken,aenj->fkaj', second_tab, turned, precision=PRECISE)  23.3 us
  transfers between devices with their start and end apart: 6, of which 5 were waited for; matrix products, arithmetic and copies ran while one was open for 31% of the time, Pallas kernels for 0%

profile of v7, /device:TPU:10, one launch (start us, length us, event | category | flops | bytes accessed | tf_op | source)
XLA Modules:
  0.0 723.1 jit_solution(9386707406404592005)
XLA Ops:
  5.1 6.8 fusion.37
  15.1 13.9 %fusion.11 = f32[2,32,128,2,64,1]{2,4,5,3,1,0:T(8,128)S(1)} fusion(f32[2,32,2,128,128,1]{4,1,3,0,2,5:T(8,128)S(1)} %maximum_bitcast_fusion.1, f32[1,2,2,64,128]{4,3,2,1,0:T(8,128)S(1)} %maximum_bitcast_fusion.22, f32[1,2,2,64,128]{4,3,2,1,0:T(8,128)S(1)} %maximum_bitcast_fusion.21), kind=kOutput, calls=%fused_computation.20 | convolution fusion | flops 3221291008 | bytes 12845056 | tf_op jit(solution)/shard_map/oaern,oenfk->oarfk/dot_general | solution.py:81
  39.1 6.2 all-to-all-start.1
  97.7 7.8 %pad_maximum_fusion = bf16[16,2,2,256,256]{3,4,2,1,0:T(8,128)(2,1)} fusion(bf16[16,2,2,256,128]{3,4,2,1,0:T(8,128)(2,1)} %convolution_convert_fusion, bf16[16,2,2,256,128]{3,4,2,1,0:T(8,128)(2,1)} %bitcast_dynamic-update-slice_fusion.15), kind=kLoop, calls=%fused_computation.5 | loop fusion | flops 16777216 | bytes 16777216 | tf_op jit(solution)/shard_map/concatenate | solution.py:186
  105.5 32.1 %all-to-all-done.1 = f32[16,2,128,256]{2,3,1,0:T(8,128)} async-done(((f32[16,2,128,256]{2,3,1,0:T(8,128)}), f32[16,2,128,256]{2,3,1,0:T(8,128)}, u32[]{:S(2)}, u32[]{:S(2)}) %all-to-all-start.1) | async-done | bytes 4194336 | tf_op jit(solution)/shard_map/all_to_all | solution.py:207
  137.6 5.4 all-to-all-start
  143.0 5.4 copy.166
  158.5 82.8 %collective-permute-done = f32[2,2048,256]{2,1,0:T(8,128)} collective-permute-done((f32[2,2048,256]{2,1,0:T(8,128)}, f32[2,2048,256]{2,1,0:T(8,128)}, u32[]{:S(2)}, u32[]{:S(2)}) %collective-permute-start) | collective-permute-done | bytes 4194336 | tf_op jit(solution)/shard_map/ppermute | solution.py:208
  241.3 5.3 copy.167
  254.6 13.3 %copy.169 = f32[2,16,2,128,256]{4,2,1,0,3:T(2,128)} copy(f32[2,16,2,128,256]{3,4,0,1,2:T(8,128)} %pad_maximum_fusion.1) | data formatting | bytes 16777216 | tf_op jit(solution)/shard_map/stack | solution.py:213
  267.9 10.9 %reshape.1813 = f32[2,32,128,256,1,1]{3,1,0,2,4,5:T(8,128)} reshape(f32[2,16,2,128,256]{4,2,1,0,3:T(2,128)} %copy.169) | data formatting | bytes 16777216 | tf_op jit(solution)/shard_map/reshape;reshape | solution.py:95
  278.8 16.7 %fusion.15 = f32[2,32,2,128,256]{4,1,3,2,0:T(8,128)S(1)} fusion(f32[2,32,128,256,1,1]{3,1,0,2,4,5:T(8,128)} %reshape.1813, f32[1,2,2,32,32]{4,3,2,1,0:T(8,128)S(1)} %fusion.82, f32[1,2,2,32,32]{4,3,2,1,0:T(8,128)S(1)} %maximum_bitcast_fusion.33), kind=kOutput, calls=%fused_computation.26 | convolution fusion | flops 3221233664 | bytes 25198592 | tf_op jit(solution)/shard_map/oafeb,ebnj->oafnj/dot_general | solution.py:97
  295.5 6.0 subtract_bitcast_fusion
  306.6 25.0 %fusion.18 = f32[2,2,128,32,256]{4,2,3,1,0:T(8,128)S(1)} fusion(f32[2,32,2,128,256,1]{4,1,3,0,2,5:T(8,128)S(1)} %maximum_bitcast_fusion, f32[1,2,2,128,128]{4,3,2,1,0:T(8,128)} %maximum_bitcast_fusion.12, f32[1,2,2,128,128]{4,3,2,1,0:T(8,128)} %maximum_bitcast_fusion.11), kind=kOutput, calls=%fused_computation.27 | convolution fusion | flops 12885032960 | bytes 34078720 | tf_op jit(solution)/shard_map/ofekn,oaenj->ofkaj/dot_general | solution.py:107
  331.6 5.8 copy-done.3
  341.7 8.2 %copy.175 = f32[1,2,128,32,256]{4,3,2,1,0:T(8,128)S(1)} copy(f32[1,2,128,32,256]{4,2,3,1,0:T(8,128)} %slice.369) | data formatting | bytes 16777216 | tf_op jit(solution)/shard_map/slice | solution.py:230
  367.2 11.4 %copy.160 = bf16[1,2,2,16,256,256]{5,4,3,2,1,0:T(8,128)(2,1)} copy(bf16[1,2,2,16,256,256]{4,5,2,1,3,0:T(8,128)(2,1)} %bitcast.54) | data formatting | bytes 16777216 | tf_op jit(solution)/shard_map/all_to_all | solution.py:223
  378.6 11.1 %fusion.23 = (f32[1,4096,256]{2,1,0:T(8,128)S(1)}, f32[1,4096,256]{2,1,0:T(8,128)S(1)}) fusion(bf16[2,2,4096,256]{3,2,1,0:T(8,128)(2,1)} %bitcast.524, f32[]{:T(128)} %bitcast.125, f32[]{:T(128)} %bitcast.124, f32[2,4096,256]{2,1,0:T(8,128)} %maximum_select_fusion, f32[1,1,128,32,256]{4,3,2,1,0:T(8,128)} %copy.174, f32[]{:T(128)} %bitcast.130, f32[]{:T(128)} %bitcast.129, ...), kind=kLoop, calls=%fused_computation.40 | loop fusion | flops 36700160 | bytes 33554448 | tf_op jit(solution)/shard_map/sub | solution.py:246
  394.6 7.7 %fusion.38 = f32[32,2,128,256]{3,0,2,1:T(8,128)S(1)} fusion(f32[1,32,128,256]{3,1,0,2:T(8,128)S(1)} %copy.178, f32[1,32,128,256]{3,1,0,2:T(8,128)S(1)} %copy.177, f32[1,2,32,32]{3,2,1,0:T(8,128)S(1)} %copy-done.19, f32[1,2,32,32]{3,2,1,0:T(8,128)S(1)} %copy-done.17), kind=kOutput, calls=%fused_computation.81 | convolution fusion | flops 1612713984 | bytes 16793600 | tf_op jit(solution)/shard_map/afeb,ebnj->afnj/dot_general | solution.py:116
  405.5 10.0 %fusion.42 = f32[2,64,32,256]{3,1,2,0:T(8,128)S(1)} fusion(f32[32,2,128,256]{3,0,2,1:T(8,128)S(1)} %pad_maximum_fusion.2, f32[1,2,64,128]{3,2,1,0:T(8,128)S(1)} %copy-done.21, f32[1,2,64,128]{3,2,1,0:T(8,128)S(1)} %copy-done.20), kind=kOutput, calls=%fused_computation.84 | convolution fusion | flops 3221258240 | bytes 12713984 | tf_op jit(solution)/shard_map/fken,aenj->fkaj/dot_general | solution.py:124
  422.1 13.3 %fusion.39 = f32[2,64,32,256]{3,1,2,0:T(8,128)S(1)} fusion(f32[32,2,128,256]{3,0,2,1:T(8,128)} %copy-done.2, f32[1,2,64,128]{3,2,1,0:T(8,128)S(1)} %get-tuple-element.164, f32[1,2,64,128]{3,2,1,0:T(8,128)S(1)} %get-tuple-element.163), kind=kOutput, calls=%fused_computation.83 | convolution fusion | flops 3221258240 | bytes 12713984 | tf_op jit(solution)/shard_map/fken,aenj->fkaj/dot_general | solution.py:124
  437.8 74.5 %collective-permute-done.1 = f32[2,16,128,256]{3,2,1,0:T(8,128)} collective-permute-done((f32[2,16,128,256]{3,2,1,0:T(8,128)}, f32[2,16,128,256]{3,2,1,0:T(8,128)}, u32[]{:S(2)}, u32[]{:S(2)}) %collective-permute-start.1) | collective-permute-done | bytes 4194336 | tf_op jit(solution)/shard_map/ppermute | solution.py:260
  520.4 6.6 all-to-all-start.2
  527.9 91.3 %all-to-all-done.2 = f32[2,16,128,256]{3,0,2,1:T(2,128)} async-done(((f32[2,16,128,256]{3,0,2,1:T(2,128)}), f32[2,16,128,256]{3,0,2,1:T(2,128)}, u32[]{:S(2)}, u32[]{:S(2)}) %all-to-all-start.2) | async-done | bytes 4194336 | tf_op jit(solution)/shard_map/all_to_all | solution.py:268
  619.2 15.4 %convolution_bitcast_fusion = f32[2,32,2,128,256]{4,1,3,2,0:T(8,128)S(1)} fusion(f32[2,16,128,256,1,1]{3,0,2,1,5,4:T(2,128)} %bitcast.158, f32[1,2,2,32,16]{3,4,2,1,0:T(8,128)S(1)} %maximum_bitcast_fusion.49, f32[1,2,2,32,16]{3,4,2,1,0:T(8,128)S(1)} %maximum_bitcast_fusion.48), kind=kOutput, calls=%fused_computation.28 | convolution fusion | flops 1610616832 | bytes 20987904 | tf_op jit(solution)/shard_map/oafem,emRj->oafRj/dot_general | solution.py:146
  634.6 5.8 copy-done.4
  649.9 6.9 fusion.29
  656.8 7.1 fusion.45
  667.2 8.1 %fusion.31 = f32[32,128,2,64,1]{1,3,4,2,0:T(8,128)S(1)} fusion(f32[32,2,128,128,1]{3,0,2,1,4:T(8,128)} %copy-done.7, f32[2,2,128,2,64]{2,4,1,3,0:T(8,128)S(1)} %fusion.57), kind=kOutput, calls=%fused_computation.74 | convolution fusion | flops 1610612736 | bytes 6422528 | tf_op jit(solution)/shard_map/aeRu,eufk->aRfk/dot_general | solution.py:164
  675.3 6.9 fusion.46
  683.4 29.8 %collective-permute-done.2 = f32[2,128,2048]{1,2,0:T(8,128)} collective-permute-done((f32[2,128,2048]{1,2,0:T(8,128)S(1)}, f32[2,128,2048]{1,2,0:T(8,128)}, u32[]{:S(2)}, u32[]{:S(2)}) %collective-permute-start.2) | collective-permute-done | bytes 2097184 | tf_op jit(solution)/shard_map/ppermute | solution.py:272
  717.3 5.3 copy.194
  (228 shorter events, 156.4 us)
Async XLA Ops:
  0.0 150.1 %copy-start = (f32[4,2]{0,1:T(2,128)S(1)}, f32[4,2]{0,1:T(2,128)}, u32[]{:S(2)}) copy-start(f32[4,2]{0,1:T(2,128)} %param.23) | copy-start | bytes 100
  12.1 1.9 copy-start.12
  12.1 1.9 copy-start.14
  29.0 3.5 copy-start.31
  31.9 2.7 copy-start.8
  39.1 98.6 %all-to-all-start.1 = ((f32[16,2,128,256]{2,3,1,0:T(8,128)}), f32[16,2,128,256]{2,3,1,0:T(8,128)}, u32[]{:S(2)}, u32[]{:S(2)}) async-start(f32[16,2,128,256]{2,3,1,0:T(8,128)} %scatter.4), calls=%async_computation.1 | async-start | bytes 8388608 | tf_op jit(solution)/shard_map/all_to_all | solution.py:207
  45.3 47.5 %copy-start.28 = (pred[128]{0:T(512)(128)(4,1)}, pred[128]{0:T(512)(128)(4,1)S(1)}, u32[]{:S(2)}) copy-start(pred[128]{0:T(512)(128)(4,1)S(1)} %get-tuple-element.203) | copy-start | bytes 388
  56.9 8.9 %copy-start.10 = (bf16[2,2,256,128]{3,2,1,0:T(8,128)(2,1)S(1)}, bf16[2,2,256,128]{3,2,1,0:T(8,128)(2,1)}, u32[]{:S(2)}) copy-start(bf16[2,2,256,128]{3,2,1,0:T(8,128)(2,1)} %get-tuple-element.143) | copy-start | bytes 786436
  63.4 2.4 copy-start.11
  84.2 8.7 %copy-start.30 = (s32[128]{0:T(128)S(1)}, s32[128]{0:T(128)}, u32[]{:S(2)}) copy-start(s32[128]{0:T(128)} %iota_subtract_fusion) | copy-start | bytes 1540
  137.6 229.6 %all-to-all-start = ((bf16[16,2,2,256,256]{3,4,2,1,0:T(8,128)(2,1)}), bf16[16,2,2,256,256]{3,4,2,1,0:T(8,128)(2,1)}, u32[]{:S(2)}, u32[]{:S(2)}) async-start(bf16[16,2,2,256,256]{3,4,2,1,0:T(8,128)(2,1)} %pad_maximum_fusion), calls=%async_computation | async-start | bytes 16777216 | tf_op jit(solution)/shard_map/all_to_all | solution.py:223
  143.0 6.9 copy-start.15
  143.0 7.0 copy-start.13
  148.4 92.9 %collective-permute-start = (f32[2,2048,256]{2,1,0:T(8,128)}, f32[2,2048,256]{2,1,0:T(8,128)}, u32[]{:S(2)}, u32[]{:S(2)}) collective-permute-start(f32[2,2048,256]{2,1,0:T(8,128)} %bitcast.533), channel_id=1, source_target_pairs={{0,16},{16,0},{1,17},{17,1},{2,18},{18,2},{3,19},{19,3},{4,20},{20... | collective-permute-start | bytes 12582920 | tf_op jit(solution)/shard_map/ppermute | solution.py:208
  153.3 3.7 copy-start.24
  153.3 3.6 copy-start.26
  331.6 5.8 copy-start.3
  392.1 2.5 copy-start.17
  392.2 2.5 copy-start.19
  394.6 7.7 %copy-start.22 = (f32[32,128]{0,1:T(8,128)S(1)}, f32[32,128]{0,1:T(8,128)}, u32[]{:S(2)}) copy-start(f32[32,128]{0,1:T(8,128)} %copy.179) | copy-start | bytes 49156
  394.6 7.7 %copy-start.23 = (f32[32,128]{0,1:T(8,128)S(1)}, f32[32,128]{0,1:T(8,128)}, u32[]{:S(2)}) copy-start(f32[32,128]{0,1:T(8,128)} %copy.180) | copy-start | bytes 49156
  405.5 10.0 %copy-start.2 = (f32[32,2,128,256]{3,0,2,1:T(8,128)}, f32[32,2,128,256]{3,0,2,1:T(8,128)S(1)}, u32[]{:S(2)}) copy-start(f32[32,2,128,256]{3,0,2,1:T(8,128)S(1)} %pad_maximum_fusion.2) | copy-start | bytes 25165828
  420.2 92.1 %collective-permute-start.1 = (f32[2,16,128,256]{3,2,1,0:T(8,128)}, f32[2,16,128,256]{3,2,1,0:T(8,128)}, u32[]{:S(2)}, u32[]{:S(2)}) collective-permute-start(f32[2,16,128,256]{3,2,1,0:T(8,128)} %bitcast.157), channel_id=1, source_target_pairs={{0,16},{16,0},{1,17},{17,1},{2,18},{18,2},{3,19},{19,3},{4,20},{20... | collective-permute-start | bytes 12582920 | tf_op jit(solution)/shard_map/ppermute | solution.py:260
  520.4 98.8 %all-to-all-start.2 = ((f32[2,16,128,256]{3,0,2,1:T(2,128)}), f32[2,16,128,256]{3,0,2,1:T(2,128)}, u32[]{:S(2)}, u32[]{:S(2)}) async-start(f32[2,16,128,256]{3,0,2,1:T(2,128)} %copy.185), calls=%async_computation.2 | async-start | bytes 8388608 | tf_op jit(solution)/shard_map/all_to_all | solution.py:268
  634.6 5.8 copy-start.4
  641.1 3.1 copy-start.29
  644.2 4.1 copy-start.9
  648.8 8.1 %copy-start.5 = (f32[32,2,128,128,1]{3,0,2,1,4:T(8,128)}, f32[32,2,128,128,1]{3,0,2,1,4:T(8,128)S(1)}, u32[]{:S(2)}) copy-start(f32[32,2,128,128,1]{3,0,2,1,4:T(8,128)S(1)} %maximum_bitcast_fusion.4) | copy-start | bytes 12582916
  649.9 14.0 %copy-start.7 = (f32[32,2,128,128,1]{3,0,2,1,4:T(8,128)}, f32[32,2,128,128,1]{3,0,2,1,4:T(8,128)S(1)}, u32[]{:S(2)}) copy-start(f32[32,2,128,128,1]{3,0,2,1,4:T(8,128)S(1)} %maximum_bitcast_fusion.5) | copy-start | bytes 12582916
  665.2 48.0 %collective-permute-start.2 = (f32[2,128,2048]{1,2,0:T(8,128)S(1)}, f32[2,128,2048]{1,2,0:T(8,128)}, u32[]{:S(2)}, u32[]{:S(2)}) collective-permute-start(f32[2,128,2048]{1,2,0:T(8,128)S(1)} %bitcast.534), channel_id=1, source_target_pairs={{0,16},{16,0},{1,17},{17,1},{2,18},{18,2},{3,19},{19,3},{4,20},{20... | collective-permute-start | bytes 6291464 | tf_op jit(solution)/shard_map/ppermute | solution.py:272
  666.8 8.5 %copy-start.6 = (f32[32,2,128,128,1]{3,0,2,1,4:T(8,128)S(1)}, f32[32,2,128,128,1]{3,0,2,1,4:T(8,128)}, u32[]{:S(2)}) copy-start(f32[32,2,128,128,1]{3,0,2,1,4:T(8,128)} %copy-done.5) | copy-start | bytes 12582916
  715.1 7.6 %copy-start.1 = (f32[4,2]{0,1:T(2,128)S(1)}, f32[4,2]{0,1:T(2,128)}, u32[]{:S(2)}) copy-start(f32[4,2]{0,1:T(2,128)} %param.23) | copy-start | bytes 100
  (6 other events, 6.1 us)

commit v8 on v7

--- a/solution.py
+++ b/solution.py
@@ -108,7 +108,7 @@
     return second.reshape((2, 2, length, width))
 
 
-def inverse_cols_half(combined, group_count, half_index):
+def inverse_cols_half(combined, group_count, half_index, part=0, parts=1):
     length, width = combined.shape[1], combined.shape[2]
     across = length // NARROW
     grid = combined.reshape((2, NARROW, across, width))
@@ -118,11 +118,13 @@
     turned = twist(first, 1, cos_part[:, :, None], sin_part[:, :, None])
     per_group = across // group_count
     per_half = per_group // 2
-    k_ids = ids(group_count)[:, None] * per_group + half_index * per_half + ids(per_half)[None, :]
+    per_part = per_half // parts
+    k_ids = ids(per_part)[None, :] + part * per_part
+    k_ids = ids(group_count)[:, None] * per_group + half_index * per_half + k_ids
     cos_k, sin_k = phase(k_ids.reshape((-1, 1)), ids(across)[None, :], across, 1.0)
     second_tab = jnp.transpose(cblock(cos_k, sin_k), (0, 2, 1, 3))
     second = jnp.einsum("fken,aenj->fkaj", second_tab, turned, precision=PRECISE)
-    return second.reshape((2, group_count, per_half * NARROW, width))
+    return second.reshape((2, group_count, per_part * NARROW, width))
 
 
 def inverse_cols(combined):
@@ -256,8 +258,12 @@
         return lax.psum_scatter(result_image, "wl", scatter_dimension=2, tiled=True)
     per_group = across // row_count
     if per_group % 2 == 0 and per_group * row_count == across:
-        given = inverse_cols_half(stacked, row_count, 1 - wl_index)
-        incoming = lax.ppermute(given, "wl", perm=[(0, 1), (1, 0)])
+        parts = 2 if per_group % 4 == 0 else 1
+        incoming = []
+        for part in range(parts):
+            given = inverse_cols_half(stacked, row_count, 1 - wl_index, part, parts)
+            incoming.append(lax.ppermute(given, "wl", perm=[(0, 1), (1, 0)]))
+        incoming = jnp.concatenate(incoming, 2)
         kept = inverse_cols_half(stacked, row_count, wl_index)
     else:
         back = back.reshape((2, row_count, 2, own_rows, width))

time: 734 us -> 731 us (level)
  waiting for transfers between devices: 310 us -> 297 us
  matrix products: 145 us -> 155 us
    ppermute x1 -> x2, waiting for transfers between devices: 74.5 us -> 61.1 us  [local(): incoming.append(lax.ppermute(given, 'wl', perm=[(0, 1), (1, 0)]))]
    dot_general x2 -> x3, matrix products: 23.3 us -> 33.1 us  [inverse_cols_half(): jnp.einsum('fken,aenj->fkaj', second_tab, turned, precision=PRECISE)]
    unnamed x110 -> x114, local copies, waits for them, and re-layouts: 54.5 us -> 54.5 us
  transfers between devices with their start and end apart: 6 -> 7, of which waited for: 5 -> 6; matrix products, arithmetic and copies ran while one was open for 31% -> 33% of each run, Pallas kernels for 0% -> 0%
where the time goes in v8:
time: 731 us; the launch traced here: 720 us
  waiting for transfers between devices  297 us (41%)
  local copies, waits for them, and re-layouts  169 us (23%)
  matrix products  155 us (21%)
  other arithmetic  72.3 us (10%)
  starting transfers between devices  22.8 us (3%)
    all_to_all x1, waiting for transfers between devices, local(): lax.all_to_all(summed, 'row', split_axis=1, concat_axis=1, tiled=True)  91.5 us
    ppermute x1, waiting for transfers between devices, local(): other = lax.ppermute(got, 'wl', perm=[(0, 1), (1, 0)])  81.9 us
    ppermute x2, waiting for transfers between devices, local(): incoming.append(lax.ppermute(given, 'wl', perm=[(0, 1), (1, 0)]))  61.1 us
    unnamed x114, local copies, waits for them, and re-layouts  54.5 us
    dot_general x3, matrix products, inverse_cols_half(): jnp.einsum('fken,aenj->fkaj', second_tab, turned, precision=PRECISE)  33.1 us
    all_to_all x1, waiting for transfers between devices, local(): lax.all_to_all(sent, 'row', split_axis=0, concat_axis=2, tiled=True)[0]  32.2 us
    ppermute x1, waiting for transfers between devices, local(): taken = lax.ppermute(theirs, 'wl', perm=[(0, 1), (1, 0)])  29.8 us
    dot_general x1, matrix products, forward_cols(): jnp.einsum('ofekn,oaenj->ofkaj', second_tab, turned, precision=PRECISE)  25 us
  transfers between devices with their start and end apart: 7, of which 6 were waited for; matrix products, arithmetic and copies ran while one was open for 33% of the time, Pallas kernels for 0%

profile of v8, /device:TPU:10, one launch (start us, length us, event | category | flops | bytes accessed | tf_op | source)
XLA Modules:
  0.0 719.6 jit_solution(16920941551246861676)
XLA Ops:
  5.1 6.8 fusion.40
  15.1 13.9 %fusion.13 = f32[2,32,128,2,64,1]{2,4,5,3,1,0:T(8,128)S(1)} fusion(f32[2,32,2,128,128,1]{4,1,3,0,2,5:T(8,128)S(1)} %maximum_bitcast_fusion.1, f32[1,2,2,64,128]{4,3,2,1,0:T(8,128)S(1)} %maximum_bitcast_fusion.22, f32[1,2,2,64,128]{4,3,2,1,0:T(8,128)S(1)} %maximum_bitcast_fusion.21), kind=kOutput, calls=%fused_computation.22 | convolution fusion | flops 3221291008 | bytes 12845056 | tf_op jit(solution)/shard_map/oaern,oenfk->oarfk/dot_general | solution.py:81
  39.6 6.2 all-to-all-start.1
  98.1 7.8 %pad_maximum_fusion = bf16[16,2,2,256,256]{3,4,2,1,0:T(8,128)(2,1)} fusion(bf16[16,2,2,256,128]{3,4,2,1,0:T(8,128)(2,1)} %convolution_convert_fusion, bf16[16,2,2,256,128]{3,4,2,1,0:T(8,128)(2,1)} %bitcast_dynamic-update-slice_fusion.15), kind=kLoop, calls=%fused_computation.5 | loop fusion | flops 16777216 | bytes 16777216 | tf_op jit(solution)/shard_map/concatenate | solution.py:188
  105.9 32.2 %all-to-all-done.1 = f32[16,2,128,256]{2,3,1,0:T(8,128)} async-done(((f32[16,2,128,256]{2,3,1,0:T(8,128)}), f32[16,2,128,256]{2,3,1,0:T(8,128)}, u32[]{:S(2)}, u32[]{:S(2)}) %all-to-all-start.1) | async-done | bytes 4194336 | tf_op jit(solution)/shard_map/all_to_all | solution.py:209
  138.1 5.4 all-to-all-start
  143.5 5.4 copy.172
  159.9 81.9 %collective-permute-done = f32[2,2048,256]{2,1,0:T(8,128)} collective-permute-done((f32[2,2048,256]{2,1,0:T(8,128)}, f32[2,2048,256]{2,1,0:T(8,128)}, u32[]{:S(2)}, u32[]{:S(2)}) %collective-permute-start) | collective-permute-done | bytes 4194336 | tf_op jit(solution)/shard_map/ppermute | solution.py:210
  255.1 13.3 %copy.175 = f32[2,16,2,128,256]{4,2,1,0,3:T(2,128)} copy(f32[2,16,2,128,256]{3,4,0,1,2:T(8,128)} %pad_maximum_fusion.1) | data formatting | bytes 16777216 | tf_op jit(solution)/shard_map/stack | solution.py:215
  268.4 10.9 %reshape.1961 = f32[2,32,128,256,1,1]{3,1,0,2,4,5:T(8,128)} reshape(f32[2,16,2,128,256]{4,2,1,0,3:T(2,128)} %copy.175) | data formatting | bytes 16777216 | tf_op jit(solution)/shard_map/reshape;reshape | solution.py:95
  279.3 16.7 %fusion.18 = f32[2,32,2,128,256]{4,1,3,2,0:T(8,128)S(1)} fusion(f32[2,32,128,256,1,1]{3,1,0,2,4,5:T(8,128)} %reshape.1961, f32[1,2,2,32,32]{4,3,2,1,0:T(8,128)S(1)} %fusion.90, f32[1,2,2,32,32]{4,3,2,1,0:T(8,128)S(1)} %maximum_bitcast_fusion.31), kind=kOutput, calls=%fused_computation.29 | convolution fusion | flops 3221233664 | bytes 25198592 | tf_op jit(solution)/shard_map/oafeb,ebnj->oafnj/dot_general | solution.py:97
  296.0 6.0 subtract_bitcast_fusion
  307.0 25.0 %fusion.21 = f32[2,2,128,32,256]{4,2,3,1,0:T(8,128)S(1)} fusion(f32[2,32,2,128,256,1]{4,1,3,0,2,5:T(8,128)S(1)} %maximum_bitcast_fusion, f32[1,2,2,128,128]{4,3,2,1,0:T(8,128)} %maximum_bitcast_fusion.12, f32[1,2,2,128,128]{4,3,2,1,0:T(8,128)} %maximum_bitcast_fusion.11), kind=kOutput, calls=%fused_computation.30 | convolution fusion | flops 12885032960 | bytes 34078720 | tf_op jit(solution)/shard_map/ofekn,oaenj->ofkaj/dot_general | solution.py:107
  332.1 5.8 copy-done.3
  342.2 8.2 %copy.181 = f32[1,2,128,32,256]{4,3,2,1,0:T(8,128)S(1)} copy(f32[1,2,128,32,256]{4,2,3,1,0:T(8,128)} %slice.369) | data formatting | bytes 16777216 | tf_op jit(solution)/shard_map/slice | solution.py:232
  367.6 11.4 %copy.166 = bf16[1,2,2,16,256,256]{5,4,3,2,1,0:T(8,128)(2,1)} copy(bf16[1,2,2,16,256,256]{4,5,2,1,3,0:T(8,128)(2,1)} %bitcast.54) | data formatting | bytes 16777216 | tf_op jit(solution)/shard_map/all_to_all | solution.py:225
  379.1 11.1 %fusion.26 = (f32[1,4096,256]{2,1,0:T(8,128)S(1)}, f32[1,4096,256]{2,1,0:T(8,128)S(1)}) fusion(bf16[2,2,4096,256]{3,2,1,0:T(8,128)(2,1)} %bitcast.544, f32[]{:T(128)} %bitcast.125, f32[]{:T(128)} %bitcast.124, f32[2,4096,256]{2,1,0:T(8,128)} %maximum_select_fusion, f32[1,1,128,32,256]{4,3,2,1,0:T(8,128)} %copy.180, f32[]{:T(128)} %bitcast.130, f32[]{:T(128)} %bitcast.129, ...), kind=kLoop, calls=%fused_computation.43 | loop fusion | flops 36700160 | bytes 33554448 | tf_op jit(solution)/shard_map/sub | solution.py:248
  395.1 7.7 %fusion.41 = f32[32,2,128,256]{3,0,2,1:T(8,128)S(1)} fusion(f32[1,32,128,256]{3,1,0,2:T(8,128)S(1)} %copy.184, f32[1,32,128,256]{3,1,0,2:T(8,128)S(1)} %copy.183, f32[1,2,32,32]{3,2,1,0:T(8,128)S(1)} %copy-done.19, f32[1,2,32,32]{3,2,1,0:T(8,128)S(1)} %copy-done.17), kind=kOutput, calls=%fused_computation.84 | convolution fusion | flops 1612713984 | bytes 16793600 | tf_op jit(solution)/shard_map/afeb,ebnj->afnj/dot_general | solution.py:116
  405.9 9.7 %fusion.47 = f32[2,32,32,256]{3,1,2,0:T(8,128)S(1)} fusion(f32[32,2,128,256]{3,0,2,1:T(8,128)S(1)} %pad_maximum_fusion.2, f32[1,2,32,128]{3,2,1,0:T(8,128)S(1)} %copy-done.27, f32[1,2,32,128]{3,2,1,0:T(8,128)S(1)} %copy-done.26), kind=kOutput, calls=%fused_computation.105 | convolution fusion | flops 1610629120 | bytes 10551296 | tf_op jit(solution)/shard_map/fken,aenj->fkaj/dot_general | solution.py:126
  418.5 9.9 %fusion.50 = f32[2,32,32,256]{3,1,2,0:T(8,128)S(1)} fusion(f32[32,2,128,256]{3,0,2,1:T(8,128)S(1)} %pad_maximum_fusion.2, f32[1,2,32,128]{3,2,1,0:T(8,128)S(1)} %copy-done.29, f32[1,2,32,128]{3,2,1,0:T(8,128)S(1)} %copy-done.28), kind=kOutput, calls=%fused_computation.106 | convolution fusion | flops 1610629120 | bytes 10551296 | tf_op jit(solution)/shard_map/fken,aenj->fkaj/dot_general | solution.py:126
  431.9 13.4 %fusion.42 = f32[2,64,32,256]{3,1,2,0:T(8,128)S(1)} fusion(f32[32,2,128,256]{3,0,2,1:T(8,128)} %copy-done.2, f32[1,2,64,128]{3,2,1,0:T(8,128)S(1)} %get-tuple-element.164, f32[1,2,64,128]{3,2,1,0:T(8,128)S(1)} %get-tuple-element.163), kind=kOutput, calls=%fused_computation.86 | convolution fusion | flops 3221258240 | bytes 12713984 | tf_op jit(solution)/shard_map/fken,aenj->fkaj/dot_general | solution.py:126
  447.8 17.9 %collective-permute-done.1 = f32[2,16,64,256]{3,2,1,0:T(8,128)} collective-permute-done((f32[2,16,64,256]{3,2,1,0:T(8,128)S(1)}, f32[2,16,64,256]{3,2,1,0:T(8,128)}, u32[]{:S(2)}, u32[]{:S(2)}) %collective-permute-start.1) | collective-permute-done | bytes 2097184 | tf_op jit(solution)/shard_map/ppermute | solution.py:265
  465.6 43.2 %collective-permute-done.2 = f32[2,16,64,256]{3,2,1,0:T(8,128)} collective-permute-done((f32[2,16,64,256]{3,2,1,0:T(8,128)}, f32[2,16,64,256]{3,2,1,0:T(8,128)}, u32[]{:S(2)}, u32[]{:S(2)}) %collective-permute-start.2) | collective-permute-done | bytes 2097184 | tf_op jit(solution)/shard_map/ppermute | solution.py:265
  517.2 6.0 all-to-all-start.2
  524.0 91.5 %all-to-all-done.2 = f32[2,16,128,256]{3,0,2,1:T(2,128)} async-done(((f32[2,16,128,256]{3,0,2,1:T(2,128)}), f32[2,16,128,256]{3,0,2,1:T(2,128)}, u32[]{:S(2)}, u32[]{:S(2)}) %all-to-all-start.2) | async-done | bytes 4194336 | tf_op jit(solution)/shard_map/all_to_all | solution.py:274
  615.5 15.4 %convolution_bitcast_fusion = f32[2,32,2,128,256]{4,1,3,2,0:T(8,128)S(1)} fusion(f32[2,16,128,256,1,1]{3,0,2,1,5,4:T(2,128)} %bitcast.167, f32[1,2,2,32,16]{3,4,2,1,0:T(8,128)S(1)} %maximum_bitcast_fusion.49, f32[1,2,2,32,16]{3,4,2,1,0:T(8,128)S(1)} %maximum_bitcast_fusion.48), kind=kOutput, calls=%fused_computation.31 | convolution fusion | flops 1610616832 | bytes 20987904 | tf_op jit(solution)/shard_map/oafem,emRj->oafRj/dot_general | solution.py:148
  630.9 5.8 copy-done.4
  646.3 6.9 fusion.32
  653.2 7.1 fusion.45
  663.6 8.1 %fusion.34 = f32[32,128,2,64,1]{1,3,4,2,0:T(8,128)S(1)} fusion(f32[32,2,128,128,1]{3,0,2,1,4:T(8,128)} %copy-done.7, f32[2,2,128,2,64]{2,4,1,3,0:T(8,128)S(1)} %fusion.63), kind=kOutput, calls=%fused_computation.77 | convolution fusion | flops 1610612736 | bytes 6422528 | tf_op jit(solution)/shard_map/aeRu,eufk->aRfk/dot_general | solution.py:166
  671.7 6.9 fusion.46
  679.8 29.8 %collective-permute-done.3 = f32[2,128,2048]{1,2,0:T(8,128)} collective-permute-done((f32[2,128,2048]{1,2,0:T(8,128)S(1)}, f32[2,128,2048]{1,2,0:T(8,128)}, u32[]{:S(2)}, u32[]{:S(2)}) %collective-permute-start.3) | collective-permute-done | bytes 2097184 | tf_op jit(solution)/shard_map/ppermute | solution.py:278
  (240 shorter events, 168.1 us)
Async XLA Ops:
  0.0 150.6 %copy-start = (f32[4,2]{0,1:T(2,128)S(1)}, f32[4,2]{0,1:T(2,128)}, u32[]{:S(2)}) copy-start(f32[4,2]{0,1:T(2,128)} %param.23) | copy-start | bytes 100
  29.0 3.6 copy-start.33
  31.9 2.9 copy-start.8
  39.6 98.6 %all-to-all-start.1 = ((f32[16,2,128,256]{2,3,1,0:T(8,128)}), f32[16,2,128,256]{2,3,1,0:T(8,128)}, u32[]{:S(2)}, u32[]{:S(2)}) async-start(f32[16,2,128,256]{2,3,1,0:T(8,128)} %scatter.4), calls=%async_computation.1 | async-start | bytes 8388608 | tf_op jit(solution)/shard_map/all_to_all | solution.py:209
  45.8 47.4 %copy-start.30 = (pred[128]{0:T(512)(128)(4,1)}, pred[128]{0:T(512)(128)(4,1)S(1)}, u32[]{:S(2)}) copy-start(pred[128]{0:T(512)(128)(4,1)S(1)} %get-tuple-element.210) | copy-start | bytes 388
  57.4 8.8 %copy-start.10 = (bf16[2,2,256,128]{3,2,1,0:T(8,128)(2,1)S(1)}, bf16[2,2,256,128]{3,2,1,0:T(8,128)(2,1)}, u32[]{:S(2)}) copy-start(bf16[2,2,256,128]{3,2,1,0:T(8,128)(2,1)} %get-tuple-element.143) | copy-start | bytes 786436
  84.5 8.7 %copy-start.32 = (s32[128]{0:T(128)S(1)}, s32[128]{0:T(128)}, u32[]{:S(2)}) copy-start(s32[128]{0:T(128)} %iota_subtract_fusion) | copy-start | bytes 1540
  138.1 229.5 %all-to-all-start = ((bf16[16,2,2,256,256]{3,4,2,1,0:T(8,128)(2,1)}), bf16[16,2,2,256,256]{3,4,2,1,0:T(8,128)(2,1)}, u32[]{:S(2)}, u32[]{:S(2)}) async-start(bf16[16,2,2,256,256]{3,4,2,1,0:T(8,128)(2,1)} %pad_maximum_fusion), calls=%async_computation | async-start | bytes 16777216 | tf_op jit(solution)/shard_map/all_to_all | solution.py:225
  143.5 6.9 copy-start.15
  143.5 7.0 copy-start.13
  148.9 92.9 %collective-permute-start = (f32[2,2048,256]{2,1,0:T(8,128)}, f32[2,2048,256]{2,1,0:T(8,128)}, u32[]{:S(2)}, u32[]{:S(2)}) collective-permute-start(f32[2,2048,256]{2,1,0:T(8,128)} %bitcast.553), channel_id=1, source_target_pairs={{0,16},{16,0},{1,17},{17,1},{2,18},{18,2},{3,19},{19,3},{4,20},{20... | collective-permute-start | bytes 12582920 | tf_op jit(solution)/shard_map/ppermute | solution.py:210
  154.0 4.4 copy-start.22
  154.0 4.4 copy-start.24
  332.0 5.8 copy-start.3
  392.6 2.5 copy-start.17
  392.6 2.5 copy-start.19
  395.1 7.7 %copy-start.20 = (f32[32,128]{0,1:T(8,128)S(1)}, f32[32,128]{0,1:T(8,128)}, u32[]{:S(2)}) copy-start(f32[32,128]{0,1:T(8,128)} %copy.185) | copy-start | bytes 49156
  395.1 7.7 %copy-start.21 = (f32[32,128]{0,1:T(8,128)S(1)}, f32[32,128]{0,1:T(8,128)}, u32[]{:S(2)}) copy-start(f32[32,128]{0,1:T(8,128)} %copy.186) | copy-start | bytes 49156
  405.9 12.6 %copy-start.2 = (f32[32,2,128,256]{3,0,2,1:T(8,128)}, f32[32,2,128,256]{3,0,2,1:T(8,128)S(1)}, u32[]{:S(2)}) copy-start(f32[32,2,128,256]{3,0,2,1:T(8,128)S(1)} %pad_maximum_fusion.2) | copy-start | bytes 25165828
  415.7 2.8 copy-start.28
  415.7 2.8 copy-start.29
  416.9 48.7 %collective-permute-start.1 = (f32[2,16,64,256]{3,2,1,0:T(8,128)S(1)}, f32[2,16,64,256]{3,2,1,0:T(8,128)}, u32[]{:S(2)}, u32[]{:S(2)}) collective-permute-start(f32[2,16,64,256]{3,2,1,0:T(8,128)S(1)} %bitcast.555), channel_id=1, source_target_pairs={{0,16},{16,0},{1,17},{17,1},{2,18},{18,2},{3,19},{19,3},{4,20},{20... | collective-permute-start | bytes 6291464 | tf_op jit(solution)/shard_map/ppermute | solution.py:265
  431.0 77.9 %collective-permute-start.2 = (f32[2,16,64,256]{3,2,1,0:T(8,128)}, f32[2,16,64,256]{3,2,1,0:T(8,128)}, u32[]{:S(2)}, u32[]{:S(2)}) collective-permute-start(f32[2,16,64,256]{3,2,1,0:T(8,128)} %bitcast.166), channel_id=1, source_target_pairs={{0,16},{16,0},{1,17},{17,1},{2,18},{18,2},{3,19},{19,3},{4,20},{20... | collective-permute-start | bytes 6291464 | tf_op jit(solution)/shard_map/ppermute | solution.py:265
  517.2 98.3 %all-to-all-start.2 = ((f32[2,16,128,256]{3,0,2,1:T(2,128)}), f32[2,16,128,256]{3,0,2,1:T(2,128)}, u32[]{:S(2)}, u32[]{:S(2)}) async-start(f32[2,16,128,256]{3,0,2,1:T(2,128)} %copy.193), calls=%async_computation.2 | async-start | bytes 8388608 | tf_op jit(solution)/shard_map/all_to_all | solution.py:274
  630.9 5.8 copy-start.4
  637.4 3.1 copy-start.31
  640.6 4.1 copy-start.9
  645.1 8.1 %copy-start.5 = (f32[32,2,128,128,1]{3,0,2,1,4:T(8,128)}, f32[32,2,128,128,1]{3,0,2,1,4:T(8,128)S(1)}, u32[]{:S(2)}) copy-start(f32[32,2,128,128,1]{3,0,2,1,4:T(8,128)S(1)} %maximum_bitcast_fusion.4) | copy-start | bytes 12582916
  646.3 14.1 %copy-start.7 = (f32[32,2,128,128,1]{3,0,2,1,4:T(8,128)}, f32[32,2,128,128,1]{3,0,2,1,4:T(8,128)S(1)}, u32[]{:S(2)}) copy-start(f32[32,2,128,128,1]{3,0,2,1,4:T(8,128)S(1)} %maximum_bitcast_fusion.5) | copy-start | bytes 12582916
  661.6 48.0 %collective-permute-start.3 = (f32[2,128,2048]{1,2,0:T(8,128)S(1)}, f32[2,128,2048]{1,2,0:T(8,128)}, u32[]{:S(2)}, u32[]{:S(2)}) collective-permute-start(f32[2,128,2048]{1,2,0:T(8,128)S(1)} %bitcast.554), channel_id=1, source_target_pairs={{0,16},{16,0},{1,17},{17,1},{2,18},{18,2},{3,19},{19,3},{4,20},{20... | collective-permute-start | bytes 6291464 | tf_op jit(solution)/shard_map/ppermute | solution.py:278
  663.2 8.5 %copy-start.6 = (f32[32,2,128,128,1]{3,0,2,1,4:T(8,128)S(1)}, f32[32,2,128,128,1]{3,0,2,1,4:T(8,128)}, u32[]{:S(2)}) copy-start(f32[32,2,128,128,1]{3,0,2,1,4:T(8,128)} %copy-done.5) | copy-start | bytes 12582916
  711.5 7.6 %copy-start.1 = (f32[4,2]{0,1:T(2,128)S(1)}, f32[4,2]{0,1:T(2,128)}, u32[]{:S(2)}) copy-start(f32[4,2]{0,1:T(2,128)} %param.23) | copy-start | bytes 100
  (9 other events, 12.3 us)

commit v9 on v8

--- a/solution.py
+++ b/solution.py
@@ -274,8 +274,12 @@
     returned = lax.all_to_all(summed, "row", split_axis=1, concat_axis=1, tiled=True)
     returned = groups_to_canon(returned, mcount, 1)
     k_half = across // 2
-    theirs = inverse_rows(returned, length, norm_factor, k_half, (1 - wl_index) * k_half)
-    taken = lax.ppermute(theirs, "wl", perm=[(0, 1), (1, 0)])
+    k_part = k_half // 2 if k_half % 2 == 0 else k_half
+    taken = []
+    for k_first in range(0, k_half, k_part):
+        theirs = inverse_rows(returned, length, norm_factor, k_part, (1 - wl_index) * k_half + k_first)
+        taken.append(lax.ppermute(theirs, "wl", perm=[(0, 1), (1, 0)]))
+    taken = jnp.concatenate(taken, 2)
     mine = inverse_rows(returned, length, norm_factor, k_half, wl_index * k_half)
     upper = jnp.where(wl_index == 0, mine, taken)
     lower = jnp.where(wl_index == 0, taken, mine)

time: 731 us -> 734 us (level)
  waiting for transfers between devices: 297 us -> 284 us
  local copies, waits for them, and re-layouts: 169 us -> 179 us
    ppermute x1 -> x2, waiting for transfers between devices: 29.8 us -> 17.5 us  [local(): taken.append(lax.ppermute(theirs, 'wl', perm=[(0, 1), (1, 0)]))]
    add x2 -> x3, local copies, waits for them, and re-layouts: 2.44 us -> 10.7 us  [inverse_rows(): out = out + jnp.einsum('aeRu,eufk->aRfk', upper, tabs[1], precision=PRECISE)]
    dot_general x2 -> x3, matrix products: 14 us -> 17.2 us  [inverse_rows(): out = jnp.einsum('aeRu,eufk->aRfk', lower, tabs[0], precision=PRECISE)]
    unnamed x114 -> x117, local copies, waits for them, and re-layouts: 54.5 us -> 55.8 us
    dot_general x2 -> x3, matrix products: 15 us -> 14.2 us  [inverse_rows(): out = out + jnp.einsum('aeRu,eufk->aRfk', upper, tabs[1], precision=PRECISE)]
  transfers between devices with their start and end apart: 7 -> 8, of which waited for: 6 -> 6; matrix products, arithmetic and copies ran while one was open for 33% -> 35% of each run, Pallas kernels for 0% -> 0%
where the time goes in v9:
time: 734 us; the launch traced here: 723 us
  waiting for transfers between devices  284 us (39%)
  local copies, waits for them, and re-layouts  179 us (24%)
  matrix products  157 us (21%)
  other arithmetic  76.2 us (10%)
  starting transfers between devices  23.4 us (3%)
    all_to_all x1, waiting for transfers between devices, local(): lax.all_to_all(summed, 'row', split_axis=1, concat_axis=1, tiled=True)  90.9 us
    ppermute x1, waiting for transfers between devices, local(): other = lax.ppermute(got, 'wl', perm=[(0, 1), (1, 0)])  82.1 us
    ppermute x2, waiting for transfers between devices, local(): incoming.append(lax.ppermute(given, 'wl', perm=[(0, 1), (1, 0)]))  61.1 us
    unnamed x117, local copies, waits for them, and re-layouts  55.8 us
    dot_general x3, matrix products, inverse_cols_half(): jnp.einsum('fken,aenj->fkaj', second_tab, turned, precision=PRECISE)  33.1 us
    all_to_all x1, waiting for transfers between devices, local(): lax.all_to_all(sent, 'row', split_axis=0, concat_axis=2, tiled=True)[0]  32.1 us
    another operation x10, other arithmetic, twist(): jnp.stack([real * cos_part - imag * sin_part, real * sin_part + imag * co...  26 us
    dot_general x1, matrix products, forward_cols(): jnp.einsum('ofekn,oaenj->ofkaj', second_tab, turned, precision=PRECISE)  25 us
  transfers between devices with their start and end apart: 8, of which 6 were waited for; matrix products, arithmetic and copies ran while one was open for 35% of the time, Pallas kernels for 0%

profile of v9, /device:TPU:10, one launch (start us, length us, event | category | flops | bytes accessed | tf_op | source)
XLA Modules:
  0.0 723.0 jit_solution(5934283640502653618)
XLA Ops:
  5.1 6.8 fusion.46
  15.1 14.2 %fusion.13 = f32[2,32,128,2,64,1]{2,4,5,3,1,0:T(8,128)S(1)} fusion(f32[2,32,2,128,128,1]{4,1,3,0,2,5:T(8,128)S(1)} %maximum_bitcast_fusion.1, f32[1,2,2,64,128]{4,3,2,1,0:T(8,128)S(1)} %maximum_bitcast_fusion.22, f32[1,2,2,64,128]{4,3,2,1,0:T(8,128)S(1)} %maximum_bitcast_fusion.21), kind=kOutput, calls=%fused_computation.22 | convolution fusion | flops 3221291008 | bytes 12845056 | tf_op jit(solution)/shard_map/oaern,oenfk->oarfk/dot_general | solution.py:81
  39.5 6.2 all-to-all-start.1
  98.1 7.8 %pad_maximum_fusion = bf16[16,2,2,256,256]{3,4,2,1,0:T(8,128)(2,1)} fusion(bf16[16,2,2,256,128]{3,4,2,1,0:T(8,128)(2,1)} %convolution_convert_fusion, bf16[16,2,2,256,128]{3,4,2,1,0:T(8,128)(2,1)} %bitcast_dynamic-update-slice_fusion.15), kind=kLoop, calls=%fused_computation.5 | loop fusion | flops 16777216 | bytes 16777216 | tf_op jit(solution)/shard_map/concatenate | solution.py:188
  105.9 32.1 %all-to-all-done.1 = f32[16,2,128,256]{2,3,1,0:T(8,128)} async-done(((f32[16,2,128,256]{2,3,1,0:T(8,128)}), f32[16,2,128,256]{2,3,1,0:T(8,128)}, u32[]{:S(2)}, u32[]{:S(2)}) %all-to-all-start.1) | async-done | bytes 4194336 | tf_op jit(solution)/shard_map/all_to_all | solution.py:209
  138.0 5.4 all-to-all-start
  143.5 5.4 copy.180
  159.7 82.1 %collective-permute-done = f32[2,2048,256]{2,1,0:T(8,128)} collective-permute-done((f32[2,2048,256]{2,1,0:T(8,128)}, f32[2,2048,256]{2,1,0:T(8,128)}, u32[]{:S(2)}, u32[]{:S(2)}) %collective-permute-start) | collective-permute-done | bytes 4194336 | tf_op jit(solution)/shard_map/ppermute | solution.py:210
  255.1 13.3 %copy.183 = f32[2,16,2,128,256]{4,2,1,0,3:T(2,128)} copy(f32[2,16,2,128,256]{3,4,0,1,2:T(8,128)} %pad_maximum_fusion.1) | data formatting | bytes 16777216 | tf_op jit(solution)/shard_map/stack | solution.py:215
  268.3 10.9 %reshape.2174 = f32[2,32,128,256,1,1]{3,1,0,2,4,5:T(8,128)} reshape(f32[2,16,2,128,256]{4,2,1,0,3:T(2,128)} %copy.183) | data formatting | bytes 16777216 | tf_op jit(solution)/shard_map/reshape;reshape | solution.py:95
  279.2 16.7 %fusion.18 = f32[2,32,2,128,256]{4,1,3,2,0:T(8,128)S(1)} fusion(f32[2,32,128,256,1,1]{3,1,0,2,4,5:T(8,128)} %reshape.2174, f32[1,2,2,32,32]{4,3,2,1,0:T(8,128)S(1)} %fusion.98, f32[1,2,2,32,32]{4,3,2,1,0:T(8,128)S(1)} %maximum_bitcast_fusion.29), kind=kOutput, calls=%fused_computation.29 | convolution fusion | flops 3221233664 | bytes 25198592 | tf_op jit(solution)/shard_map/oafeb,ebnj->oafnj/dot_general | solution.py:97
  296.0 6.0 subtract_bitcast_fusion
  307.1 25.0 %fusion.21 = f32[2,2,128,32,256]{4,2,3,1,0:T(8,128)S(1)} fusion(f32[2,32,2,128,256,1]{4,1,3,0,2,5:T(8,128)S(1)} %maximum_bitcast_fusion, f32[1,2,2,128,128]{4,3,2,1,0:T(8,128)} %maximum_bitcast_fusion.12, f32[1,2,2,128,128]{4,3,2,1,0:T(8,128)} %maximum_bitcast_fusion.11), kind=kOutput, calls=%fused_computation.30 | convolution fusion | flops 12885032960 | bytes 34078720 | tf_op jit(solution)/shard_map/ofekn,oaenj->ofkaj/dot_general | solution.py:107
  332.1 5.8 copy-done.3
  342.2 8.2 %copy.189 = f32[1,2,128,32,256]{4,3,2,1,0:T(8,128)S(1)} copy(f32[1,2,128,32,256]{4,2,3,1,0:T(8,128)} %slice.380) | data formatting | bytes 16777216 | tf_op jit(solution)/shard_map/slice | solution.py:232
  367.7 11.4 %copy.174 = bf16[1,2,2,16,256,256]{5,4,3,2,1,0:T(8,128)(2,1)} copy(bf16[1,2,2,16,256,256]{4,5,2,1,3,0:T(8,128)(2,1)} %bitcast.54) | data formatting | bytes 16777216 | tf_op jit(solution)/shard_map/all_to_all | solution.py:225
  379.1 11.1 %fusion.26 = (f32[1,4096,256]{2,1,0:T(8,128)S(1)}, f32[1,4096,256]{2,1,0:T(8,128)S(1)}) fusion(bf16[2,2,4096,256]{3,2,1,0:T(8,128)(2,1)} %bitcast.587, f32[]{:T(128)} %bitcast.125, f32[]{:T(128)} %bitcast.124, f32[2,4096,256]{2,1,0:T(8,128)} %maximum_select_fusion, f32[1,1,128,32,256]{4,3,2,1,0:T(8,128)} %copy.188, f32[]{:T(128)} %bitcast.130, f32[]{:T(128)} %bitcast.129, ...), kind=kLoop, calls=%fused_computation.43 | loop fusion | flops 36700160 | bytes 33554448 | tf_op jit(solution)/shard_map/sub | solution.py:248
  395.1 7.7 %fusion.47 = f32[32,2,128,256]{3,0,2,1:T(8,128)S(1)} fusion(f32[1,32,128,256]{3,1,0,2:T(8,128)S(1)} %copy.192, f32[1,32,128,256]{3,1,0,2:T(8,128)S(1)} %copy.191, f32[1,2,32,32]{3,2,1,0:T(8,128)S(1)} %copy-done.20, f32[1,2,32,32]{3,2,1,0:T(8,128)S(1)} %copy-done.18), kind=kOutput, calls=%fused_computation.92 | convolution fusion | flops 1612713984 | bytes 16793600 | tf_op jit(solution)/shard_map/afeb,ebnj->afnj/dot_general | solution.py:116
  406.0 9.7 %fusion.56 = f32[2,32,32,256]{3,1,2,0:T(8,128)S(1)} fusion(f32[32,2,128,256]{3,0,2,1:T(8,128)S(1)} %pad_maximum_fusion.2, f32[1,2,32,128]{3,2,1,0:T(8,128)S(1)} %copy-done.28, f32[1,2,32,128]{3,2,1,0:T(8,128)S(1)} %copy-done.27), kind=kOutput, calls=%fused_computation.111 | convolution fusion | flops 1610629120 | bytes 10551296 | tf_op jit(solution)/shard_map/fken,aenj->fkaj/dot_general | solution.py:126
  418.5 9.9 %fusion.59 = f32[2,32,32,256]{3,1,2,0:T(8,128)S(1)} fusion(f32[32,2,128,256]{3,0,2,1:T(8,128)S(1)} %pad_maximum_fusion.2, f32[1,2,32,128]{3,2,1,0:T(8,128)S(1)} %copy-done.30, f32[1,2,32,128]{3,2,1,0:T(8,128)S(1)} %copy-done.29), kind=kOutput, calls=%fused_computation.112 | convolution fusion | flops 1610629120 | bytes 10551296 | tf_op jit(solution)/shard_map/fken,aenj->fkaj/dot_general | solution.py:126
  431.9 13.4 %fusion.52 = f32[2,64,32,256]{3,1,2,0:T(8,128)S(1)} fusion(f32[32,2,128,256]{3,0,2,1:T(8,128)} %copy-done.2, f32[1,2,64,128]{3,2,1,0:T(8,128)S(1)} %get-tuple-element.160, f32[1,2,64,128]{3,2,1,0:T(8,128)S(1)} %get-tuple-element.159), kind=kOutput, calls=%fused_computation.94 | convolution fusion | flops 3221258240 | bytes 12713984 | tf_op jit(solution)/shard_map/fken,aenj->fkaj/dot_general | solution.py:126
  447.8 17.9 %collective-permute-done.1 = f32[2,16,64,256]{3,2,1,0:T(8,128)} collective-permute-done((f32[2,16,64,256]{3,2,1,0:T(8,128)S(1)}, f32[2,16,64,256]{3,2,1,0:T(8,128)}, u32[]{:S(2)}, u32[]{:S(2)}) %collective-permute-start.1) | collective-permute-done | bytes 2097184 | tf_op jit(solution)/shard_map/ppermute | solution.py:265
  465.7 43.2 %collective-permute-done.2 = f32[2,16,64,256]{3,2,1,0:T(8,128)} collective-permute-done((f32[2,16,64,256]{3,2,1,0:T(8,128)}, f32[2,16,64,256]{3,2,1,0:T(8,128)}, u32[]{:S(2)}, u32[]{:S(2)}) %collective-permute-start.2) | collective-permute-done | bytes 2097184 | tf_op jit(solution)/shard_map/ppermute | solution.py:265
  517.2 6.0 all-to-all-start.2
  524.7 90.9 %all-to-all-done.2 = f32[2,16,128,256]{3,0,2,1:T(2,128)} async-done(((f32[2,16,128,256]{3,0,2,1:T(2,128)}), f32[2,16,128,256]{3,0,2,1:T(2,128)}, u32[]{:S(2)}, u32[]{:S(2)}) %all-to-all-start.2) | async-done | bytes 4194336 | tf_op jit(solution)/shard_map/all_to_all | solution.py:274
  615.5 15.4 %convolution_bitcast_fusion = f32[2,32,2,128,256]{4,1,3,2,0:T(8,128)S(1)} fusion(f32[2,16,128,256,1,1]{3,0,2,1,5,4:T(2,128)} %bitcast.167, f32[1,2,2,32,16]{3,4,2,1,0:T(8,128)S(1)} %maximum_bitcast_fusion.47, f32[1,2,2,32,16]{3,4,2,1,0:T(8,128)S(1)} %maximum_bitcast_fusion.46), kind=kOutput, calls=%fused_computation.31 | convolution fusion | flops 1610616832 | bytes 20987904 | tf_op jit(solution)/shard_map/oafem,emRj->oafRj/dot_general | solution.py:148
  630.9 5.8 copy-done.4
  672.6 5.4 copy.212
  680.7 6.9 fusion.33
  687.6 7.1 fusion.55
  697.2 17.5 %collective-permute-done.4 = f32[2,128,1024]{1,2,0:T(8,128)S(1)} collective-permute-done((f32[2,128,1024]{1,2,0:T(8,128)}, f32[2,128,1024]{1,2,0:T(8,128)S(1)}, u32[]{:S(2)}, u32[]{:S(2)}) %collective-permute-start.4) | collective-permute-done | bytes 1048608 | tf_op jit(solution)/shard_map/ppermute | solution.py:281
  717.5 5.3 copy.213
  (255 shorter events, 188.5 us)
Async XLA Ops:
  0.0 150.6 %copy-start = (f32[4,2]{0,1:T(2,128)S(1)}, f32[4,2]{0,1:T(2,128)}, u32[]{:S(2)}) copy-start(f32[4,2]{0,1:T(2,128)} %param.23) | copy-start | bytes 100
  29.3 3.3 copy-start.34
  31.9 2.8 copy-start.9
  39.5 98.6 %all-to-all-start.1 = ((f32[16,2,128,256]{2,3,1,0:T(8,128)}), f32[16,2,128,256]{2,3,1,0:T(8,128)}, u32[]{:S(2)}, u32[]{:S(2)}) async-start(f32[16,2,128,256]{2,3,1,0:T(8,128)} %scatter.4), calls=%async_computation.1 | async-start | bytes 8388608 | tf_op jit(solution)/shard_map/all_to_all | solution.py:209
  45.7 47.5 %copy-start.31 = (pred[128]{0:T(512)(128)(4,1)}, pred[128]{0:T(512)(128)(4,1)S(1)}, u32[]{:S(2)}) copy-start(pred[128]{0:T(512)(128)(4,1)S(1)} %get-tuple-element.220) | copy-start | bytes 388
  57.3 8.9 %copy-start.11 = (bf16[2,2,256,128]{3,2,1,0:T(8,128)(2,1)S(1)}, bf16[2,2,256,128]{3,2,1,0:T(8,128)(2,1)}, u32[]{:S(2)}) copy-start(bf16[2,2,256,128]{3,2,1,0:T(8,128)(2,1)} %get-tuple-element.143) | copy-start | bytes 786436
  84.5 8.7 %copy-start.33 = (s32[128]{0:T(128)S(1)}, s32[128]{0:T(128)}, u32[]{:S(2)}) copy-start(s32[128]{0:T(128)} %iota_subtract_fusion) | copy-start | bytes 1540
  138.0 229.7 %all-to-all-start = ((bf16[16,2,2,256,256]{3,4,2,1,0:T(8,128)(2,1)}), bf16[16,2,2,256,256]{3,4,2,1,0:T(8,128)(2,1)}, u32[]{:S(2)}, u32[]{:S(2)}) async-start(bf16[16,2,2,256,256]{3,4,2,1,0:T(8,128)(2,1)} %pad_maximum_fusion), calls=%async_computation | async-start | bytes 16777216 | tf_op jit(solution)/shard_map/all_to_all | solution.py:225
  143.5 6.9 copy-start.16
  143.5 7.0 copy-start.14
  148.8 92.9 %collective-permute-start = (f32[2,2048,256]{2,1,0:T(8,128)}, f32[2,2048,256]{2,1,0:T(8,128)}, u32[]{:S(2)}, u32[]{:S(2)}) collective-permute-start(f32[2,2048,256]{2,1,0:T(8,128)} %bitcast.596), channel_id=1, source_target_pairs={{0,16},{16,0},{1,17},{17,1},{2,18},{18,2},{3,19},{19,3},{4,20},{20... | collective-permute-start | bytes 12582920 | tf_op jit(solution)/shard_map/ppermute | solution.py:210
  153.8 4.4 copy-start.23
  153.8 4.4 copy-start.25
  332.1 5.8 copy-start.3
  395.1 7.7 %copy-start.21 = (f32[32,128]{0,1:T(8,128)S(1)}, f32[32,128]{0,1:T(8,128)}, u32[]{:S(2)}) copy-start(f32[32,128]{0,1:T(8,128)} %copy.193) | copy-start | bytes 49156
  395.1 7.7 %copy-start.22 = (f32[32,128]{0,1:T(8,128)S(1)}, f32[32,128]{0,1:T(8,128)}, u32[]{:S(2)}) copy-start(f32[32,128]{0,1:T(8,128)} %copy.194) | copy-start | bytes 49156
  405.9 12.6 %copy-start.2 = (f32[32,2,128,256]{3,0,2,1:T(8,128)}, f32[32,2,128,256]{3,0,2,1:T(8,128)S(1)}, u32[]{:S(2)}) copy-start(f32[32,2,128,256]{3,0,2,1:T(8,128)S(1)} %pad_maximum_fusion.2) | copy-start | bytes 25165828
  415.7 2.8 copy-start.29
  415.7 2.8 copy-start.30
  416.9 48.7 %collective-permute-start.1 = (f32[2,16,64,256]{3,2,1,0:T(8,128)S(1)}, f32[2,16,64,256]{3,2,1,0:T(8,128)}, u32[]{:S(2)}, u32[]{:S(2)}) collective-permute-start(f32[2,16,64,256]{3,2,1,0:T(8,128)S(1)} %bitcast.597), channel_id=1, source_target_pairs={{0,16},{16,0},{1,17},{17,1},{2,18},{18,2},{3,19},{19,3},{4,20},{20... | collective-permute-start | bytes 6291464 | tf_op jit(solution)/shard_map/ppermute | solution.py:265
  431.0 77.9 %collective-permute-start.2 = (f32[2,16,64,256]{3,2,1,0:T(8,128)}, f32[2,16,64,256]{3,2,1,0:T(8,128)}, u32[]{:S(2)}, u32[]{:S(2)}) collective-permute-start(f32[2,16,64,256]{3,2,1,0:T(8,128)} %bitcast.166), channel_id=1, source_target_pairs={{0,16},{16,0},{1,17},{17,1},{2,18},{18,2},{3,19},{19,3},{4,20},{20... | collective-permute-start | bytes 6291464 | tf_op jit(solution)/shard_map/ppermute | solution.py:265
  517.2 98.3 %all-to-all-start.2 = ((f32[2,16,128,256]{3,0,2,1:T(2,128)}), f32[2,16,128,256]{3,0,2,1:T(2,128)}, u32[]{:S(2)}, u32[]{:S(2)}) async-start(f32[2,16,128,256]{3,0,2,1:T(2,128)} %copy.201), calls=%async_computation.2 | async-start | bytes 8388608 | tf_op jit(solution)/shard_map/all_to_all | solution.py:274
  630.9 5.8 copy-start.4
  637.5 3.1 copy-start.32
  645.2 3.7 copy-start.6
  645.2 3.7 copy-start.8
  649.0 3.7 copy-start.5
  666.9 29.1 %collective-permute-start.3 = (f32[2,128,1024]{1,2,0:T(8,128)S(1)}, f32[2,128,1024]{1,2,0:T(8,128)}, u32[]{:S(2)}, u32[]{:S(2)}) collective-permute-start(f32[2,128,1024]{1,2,0:T(8,128)S(1)} %bitcast.598), channel_id=1, source_target_pairs={{0,16},{16,0},{1,17},{17,1},{2,18},{18,2},{3,19},{19,3},{4,20},{20... | collective-permute-start | bytes 3145736 | tf_op jit(solution)/shard_map/ppermute | solution.py:281
  672.6 6.0 copy-start.7
  678.0 36.8 %collective-permute-start.4 = (f32[2,128,1024]{1,2,0:T(8,128)}, f32[2,128,1024]{1,2,0:T(8,128)S(1)}, u32[]{:S(2)}, u32[]{:S(2)}) collective-permute-start(f32[2,128,1024]{1,2,0:T(8,128)} %bitcast.599), channel_id=1, source_target_pairs={{0,16},{16,0},{1,17},{17,1},{2,18},{18,2},{3,19},{19,3},{4,20},{20... | collective-permute-start | bytes 3145736 | tf_op jit(solution)/shard_map/ppermute | solution.py:281
  680.7 6.9 copy-start.10
  715.1 7.7 %copy-start.1 = (f32[4,2]{0,1:T(2,128)S(1)}, f32[4,2]{0,1:T(2,128)}, u32[]{:S(2)}) copy-start(f32[4,2]{0,1:T(2,128)} %param.23) | copy-start | bytes 100
  (11 other events, 17.3 us)

commit v10 on v8

--- a/solution.py
+++ b/solution.py
@@ -258,7 +258,7 @@
         return lax.psum_scatter(result_image, "wl", scatter_dimension=2, tiled=True)
     per_group = across // row_count
     if per_group % 2 == 0 and per_group * row_count == across:
-        parts = 2 if per_group % 4 == 0 else 1
+        parts = 4 if per_group % 8 == 0 else 1
         incoming = []
         for part in range(parts):
             given = inverse_cols_half(stacked, row_count, 1 - wl_index, part, parts)

time: 731 us -> 724 us (level)
  matrix products: 155 us -> 178 us
  waiting for transfers between devices: 297 us -> 274 us
  local copies, waits for them, and re-layouts: 169 us -> 159 us
    dot_general x3 -> x5, matrix products: 33.1 us -> 54.1 us  [inverse_cols_half(): jnp.einsum('fken,aenj->fkaj', second_tab, turned, precision=PRECISE)]
    ppermute x2 -> x4, waiting for transfers between devices: 61.1 us -> 40.1 us  [local(): incoming.append(lax.ppermute(given, 'wl', perm=[(0, 1), (1, 0)]))]
    unnamed x114 -> x118, local copies, waits for them, and re-layouts: 54.5 us -> 48.7 us
  transfers between devices with their start and end apart: 7 -> 9, of which waited for: 6 -> 6; matrix products, arithmetic and copies ran while one was open for 33% -> 36% of each run, Pallas kernels for 0% -> 0%
where the time goes in v10:
time: 724 us; the launch traced here: 713 us
  waiting for transfers between devices  274 us (38%)
  matrix products  178 us (25%)
  local copies, waits for them, and re-layouts  159 us (22%)
  other arithmetic  72.8 us (10%)
  starting transfers between devices  24.9 us (3%)
    all_to_all x1, waiting for transfers between devices, local(): lax.all_to_all(summed, 'row', split_axis=1, concat_axis=1, tiled=True)  91.5 us
    ppermute x1, waiting for transfers between devices, local(): other = lax.ppermute(got, 'wl', perm=[(0, 1), (1, 0)])  80.8 us
    dot_general x5, matrix products, inverse_cols_half(): jnp.einsum('fken,aenj->fkaj', second_tab, turned, precision=PRECISE)  54.1 us
    unnamed x118, local copies, waits for them, and re-layouts  48.7 us
    ppermute x4, waiting for transfers between devices, local(): incoming.append(lax.ppermute(given, 'wl', perm=[(0, 1), (1, 0)]))  40.1 us
    all_to_all x1, waiting for transfers between devices, local(): lax.all_to_all(sent, 'row', split_axis=0, concat_axis=2, tiled=True)[0]  32.1 us
    ppermute x1, waiting for transfers between devices, local(): taken = lax.ppermute(theirs, 'wl', perm=[(0, 1), (1, 0)])  29.8 us
    dot_general x1, matrix products, forward_cols(): jnp.einsum('ofekn,oaenj->ofkaj', second_tab, turned, precision=PRECISE)  25 us
  transfers between devices with their start and end apart: 9, of which 6 were waited for; matrix products, arithmetic and copies ran while one was open for 36% of the time, Pallas kernels for 0%

profile of v10, /device:TPU:10, one launch (start us, length us, event | category | flops | bytes accessed | tf_op | source)
XLA Modules:
  0.0 713.1 jit_solution(16438513354789603543)
XLA Ops:
  5.1 6.8 fusion.46
  15.1 13.9 %fusion.17 = f32[2,32,128,2,64,1]{2,4,5,3,1,0:T(8,128)S(1)} fusion(f32[2,32,2,128,128,1]{4,1,3,0,2,5:T(8,128)S(1)} %maximum_bitcast_fusion.1, f32[1,2,2,64,128]{4,3,2,1,0:T(8,128)S(1)} %maximum_bitcast_fusion.22, f32[1,2,2,64,128]{4,3,2,1,0:T(8,128)S(1)} %maximum_bitcast_fusion.21), kind=kOutput, calls=%fused_computation.26 | convolution fusion | flops 3221291008 | bytes 12845056 | tf_op jit(solution)/shard_map/oaern,oenfk->oarfk/dot_general | solution.py:81
  39.4 6.2 all-to-all-start.1
  98.0 7.8 %pad_maximum_fusion = bf16[16,2,2,256,256]{3,4,2,1,0:T(8,128)(2,1)} fusion(bf16[16,2,2,256,128]{3,4,2,1,0:T(8,128)(2,1)} %convolution_convert_fusion, bf16[16,2,2,256,128]{3,4,2,1,0:T(8,128)(2,1)} %bitcast_dynamic-update-slice_fusion.15), kind=kLoop, calls=%fused_computation.5 | loop fusion | flops 16777216 | bytes 16777216 | tf_op jit(solution)/shard_map/concatenate | solution.py:188
  105.9 32.1 %all-to-all-done.1 = f32[16,2,128,256]{2,3,1,0:T(8,128)} async-done(((f32[16,2,128,256]{2,3,1,0:T(8,128)}), f32[16,2,128,256]{2,3,1,0:T(8,128)}, u32[]{:S(2)}, u32[]{:S(2)}) %all-to-all-start.1) | async-done | bytes 4194336 | tf_op jit(solution)/shard_map/all_to_all | solution.py:209
  160.9 80.8 %collective-permute-done = f32[2,2048,256]{2,1,0:T(8,128)} collective-permute-done((f32[2,2048,256]{2,1,0:T(8,128)}, f32[2,2048,256]{2,1,0:T(8,128)}, u32[]{:S(2)}, u32[]{:S(2)}) %collective-permute-start) | collective-permute-done | bytes 4194336 | tf_op jit(solution)/shard_map/ppermute | solution.py:210
  255.0 13.3 %copy.175 = f32[2,16,2,128,256]{4,2,1,0,3:T(2,128)} copy(f32[2,16,2,128,256]{3,4,0,1,2:T(8,128)} %pad_maximum_fusion.1) | data formatting | bytes 16777216 | tf_op jit(solution)/shard_map/stack | solution.py:215
  268.3 10.9 %reshape.2175 = f32[2,32,128,256,1,1]{3,1,0,2,4,5:T(8,128)} reshape(f32[2,16,2,128,256]{4,2,1,0,3:T(2,128)} %copy.175) | data formatting | bytes 16777216 | tf_op jit(solution)/shard_map/reshape;reshape | solution.py:95
  279.2 16.7 %fusion.19 = f32[2,32,2,128,256]{4,1,3,2,0:T(8,128)S(1)} fusion(f32[2,32,128,256,1,1]{3,1,0,2,4,5:T(8,128)} %reshape.2175, f32[1,2,2,32,32]{4,3,2,1,0:T(8,128)S(1)} %fusion.98, f32[1,2,2,32,32]{4,3,2,1,0:T(8,128)S(1)} %maximum_bitcast_fusion.31), kind=kOutput, calls=%fused_computation.30 | convolution fusion | flops 3221233664 | bytes 25198592 | tf_op jit(solution)/shard_map/oafeb,ebnj->oafnj/dot_general | solution.py:97
  295.9 6.0 subtract_bitcast_fusion
  306.9 25.0 %fusion.22 = f32[2,2,128,32,256]{4,2,3,1,0:T(8,128)S(1)} fusion(f32[2,32,2,128,256,1]{4,1,3,0,2,5:T(8,128)S(1)} %maximum_bitcast_fusion, f32[1,2,2,128,128]{4,3,2,1,0:T(8,128)} %maximum_bitcast_fusion.12, f32[1,2,2,128,128]{4,3,2,1,0:T(8,128)} %maximum_bitcast_fusion.11), kind=kOutput, calls=%fused_computation.31 | convolution fusion | flops 12885032960 | bytes 34078720 | tf_op jit(solution)/shard_map/ofekn,oaenj->ofkaj/dot_general | solution.py:107
  331.9 5.8 copy-done.3
  342.1 8.2 %copy.181 = f32[1,2,128,32,256]{4,3,2,1,0:T(8,128)S(1)} copy(f32[1,2,128,32,256]{4,2,3,1,0:T(8,128)} %slice.369) | data formatting | bytes 16777216 | tf_op jit(solution)/shard_map/slice | solution.py:232
  367.5 11.5 %copy.166 = bf16[1,2,2,16,256,256]{5,4,3,2,1,0:T(8,128)(2,1)} copy(bf16[1,2,2,16,256,256]{4,5,2,1,3,0:T(8,128)(2,1)} %bitcast.54) | data formatting | bytes 16777216 | tf_op jit(solution)/shard_map/all_to_all | solution.py:225
  379.0 11.1 %fusion.32 = (f32[1,4096,256]{2,1,0:T(8,128)S(1)}, f32[1,4096,256]{2,1,0:T(8,128)S(1)}) fusion(bf16[2,2,4096,256]{3,2,1,0:T(8,128)(2,1)} %bitcast.577, f32[]{:T(128)} %bitcast.125, f32[]{:T(128)} %bitcast.124, f32[2,4096,256]{2,1,0:T(8,128)} %maximum_select_fusion, f32[1,1,128,32,256]{4,3,2,1,0:T(8,128)} %copy.180, f32[]{:T(128)} %bitcast.130, f32[]{:T(128)} %bitcast.129, ...), kind=kLoop, calls=%fused_computation.49 | loop fusion | flops 36700160 | bytes 33554448 | tf_op jit(solution)/shard_map/sub | solution.py:248
  395.0 7.7 %fusion.47 = f32[32,2,128,256]{3,0,2,1:T(8,128)S(1)} fusion(f32[1,32,128,256]{3,1,0,2:T(8,128)S(1)} %copy.184, f32[1,32,128,256]{3,1,0,2:T(8,128)S(1)} %copy.183, f32[1,2,32,32]{3,2,1,0:T(8,128)S(1)} %copy-done.17, f32[1,2,32,32]{3,2,1,0:T(8,128)S(1)} %copy-done.15), kind=kOutput, calls=%fused_computation.90 | convolution fusion | flops 1612713984 | bytes 16793600 | tf_op jit(solution)/shard_map/afeb,ebnj->afnj/dot_general | solution.py:116
  405.9 9.4 %fusion.57 = f32[2,16,32,256]{3,1,2,0:T(8,128)S(1)} fusion(f32[32,2,128,256]{3,0,2,1:T(8,128)S(1)} %pad_maximum_fusion.2, f32[1,2,16,128]{3,2,1,0:T(8,128)S(1)} %copy-done.25, f32[1,2,16,128]{3,2,1,0:T(8,128)S(1)} %copy-done.24), kind=kOutput, calls=%fused_computation.111 | convolution fusion | flops 805314560 | bytes 9469952 | tf_op jit(solution)/shard_map/fken,aenj->fkaj/dot_general | solution.py:126
  416.8 10.7 %fusion.60 = f32[2,16,32,256]{3,1,2,0:T(8,128)} fusion(f32[32,2,128,256]{3,0,2,1:T(8,128)S(1)} %pad_maximum_fusion.2, f32[1,2,16,128]{3,2,1,0:T(8,128)S(1)} %copy-done.27, f32[1,2,16,128]{3,2,1,0:T(8,128)S(1)} %copy-done.26), kind=kOutput, calls=%fused_computation.112 | convolution fusion | flops 805314560 | bytes 9469952 | tf_op jit(solution)/shard_map/fken,aenj->fkaj/dot_general | solution.py:126
  428.1 10.5 %fusion.63 = f32[2,16,32,256]{3,1,2,0:T(8,128)} fusion(f32[32,2,128,256]{3,0,2,1:T(8,128)S(1)} %pad_maximum_fusion.2, f32[1,2,16,128]{3,2,1,0:T(8,128)S(1)} %copy-done.29, f32[1,2,16,128]{3,2,1,0:T(8,128)S(1)} %copy-done.28), kind=kOutput, calls=%fused_computation.113 | convolution fusion | flops 805314560 | bytes 9469952 | tf_op jit(solution)/shard_map/fken,aenj->fkaj/dot_general | solution.py:126
  440.1 10.5 %fusion.66 = f32[2,16,32,256]{3,1,2,0:T(8,128)} fusion(f32[32,2,128,256]{3,0,2,1:T(8,128)S(1)} %pad_maximum_fusion.2, f32[1,2,16,128]{3,2,1,0:T(8,128)S(1)} %copy-done.31, f32[1,2,16,128]{3,2,1,0:T(8,128)S(1)} %copy-done.30), kind=kOutput, calls=%fused_computation.114 | convolution fusion | flops 805314560 | bytes 9469952 | tf_op jit(solution)/shard_map/fken,aenj->fkaj/dot_general | solution.py:126
  451.6 13.0 %fusion.48 = f32[2,64,32,256]{3,1,2,0:T(8,128)S(1)} fusion(f32[32,2,128,256]{3,0,2,1:T(8,128)} %copy-done.2, f32[1,2,64,128]{3,2,1,0:T(8,128)S(1)} %get-tuple-element.164, f32[1,2,64,128]{3,2,1,0:T(8,128)S(1)} %get-tuple-element.163), kind=kOutput, calls=%fused_computation.92 | convolution fusion | flops 3221258240 | bytes 12713984 | tf_op jit(solution)/shard_map/fken,aenj->fkaj/dot_general | solution.py:126
  467.1 19.4 %collective-permute-done.3 = f32[2,16,32,256]{3,1,2,0:T(8,128)} collective-permute-done((f32[2,16,32,256]{3,1,2,0:T(8,128)}, f32[2,16,32,256]{3,1,2,0:T(8,128)}, u32[]{:S(2)}, u32[]{:S(2)}) %collective-permute-start.3) | collective-permute-done | bytes 1048608 | tf_op jit(solution)/shard_map/ppermute | solution.py:265
  486.5 20.7 %collective-permute-done.4 = f32[2,16,32,256]{3,1,2,0:T(8,128)} collective-permute-done((f32[2,16,32,256]{3,1,2,0:T(8,128)}, f32[2,16,32,256]{3,1,2,0:T(8,128)}, u32[]{:S(2)}, u32[]{:S(2)}) %collective-permute-start.4) | collective-permute-done | bytes 1048608 | tf_op jit(solution)/shard_map/ppermute | solution.py:265
  507.2 6.0 maximum_add_fusion
  517.7 6.0 all-to-all-start.2
  524.6 91.5 %all-to-all-done.2 = f32[2,16,128,256]{3,2,0,1:T(8,128)} async-done(((f32[2,16,128,256]{3,2,0,1:T(8,128)}), f32[2,16,128,256]{3,2,0,1:T(8,128)}, u32[]{:S(2)}, u32[]{:S(2)}) %all-to-all-start.2) | async-done | bytes 4194336 | tf_op jit(solution)/shard_map/all_to_all | solution.py:274
  616.0 18.1 %convolution_bitcast_fusion = f32[2,32,2,128,256]{4,1,3,2,0:T(8,128)S(1)} fusion(f32[2,16,128,256,1,1]{3,2,0,1,5,4:T(8,128)} %bitcast.181, f32[1,2,2,32,16]{3,4,2,1,0:T(8,128)S(1)} %maximum_bitcast_fusion.45, f32[1,2,2,32,16]{3,4,2,1,0:T(8,128)S(1)} %maximum_bitcast_fusion.44), kind=kOutput, calls=%fused_computation.32 | convolution fusion | flops 1610616832 | bytes 20987904 | tf_op jit(solution)/shard_map/oafem,emRj->oafRj/dot_general | solution.py:148
  639.9 6.9 fusion.38
  646.8 7.1 fusion.51
  657.2 8.1 %fusion.40 = f32[32,128,2,64,1]{1,3,4,2,0:T(8,128)S(1)} fusion(f32[32,2,128,128,1]{3,0,2,1,4:T(8,128)} %copy-done.6, f32[2,2,128,2,64]{2,4,1,3,0:T(8,128)S(1)} %fusion.75), kind=kOutput, calls=%fused_computation.83 | convolution fusion | flops 1610612736 | bytes 6422528 | tf_op jit(solution)/shard_map/aeRu,eufk->aRfk/dot_general | solution.py:166
  665.3 6.9 fusion.52
  673.4 29.8 %collective-permute-done.5 = f32[2,128,2048]{1,2,0:T(8,128)} collective-permute-done((f32[2,128,2048]{1,2,0:T(8,128)S(1)}, f32[2,128,2048]{1,2,0:T(8,128)}, u32[]{:S(2)}, u32[]{:S(2)}) %collective-permute-start.5) | collective-permute-done | bytes 2097184 | tf_op jit(solution)/shard_map/ppermute | solution.py:278
  (248 shorter events, 170.6 us)
Async XLA Ops:
  0.0 150.5 %copy-start = (f32[4,2]{0,1:T(2,128)S(1)}, f32[4,2]{0,1:T(2,128)}, u32[]{:S(2)}) copy-start(f32[4,2]{0,1:T(2,128)} %param.23) | copy-start | bytes 100
  29.0 3.5 copy-start.35
  39.4 98.6 %all-to-all-start.1 = ((f32[16,2,128,256]{2,3,1,0:T(8,128)}), f32[16,2,128,256]{2,3,1,0:T(8,128)}, u32[]{:S(2)}, u32[]{:S(2)}) async-start(f32[16,2,128,256]{2,3,1,0:T(8,128)} %scatter.4), calls=%async_computation.1 | async-start | bytes 8388608 | tf_op jit(solution)/shard_map/all_to_all | solution.py:209
  45.7 47.5 %copy-start.32 = (pred[128]{0:T(512)(128)(4,1)}, pred[128]{0:T(512)(128)(4,1)S(1)}, u32[]{:S(2)}) copy-start(pred[128]{0:T(512)(128)(4,1)S(1)} %get-tuple-element.218) | copy-start | bytes 388
  57.3 8.8 %copy-start.8 = (bf16[2,2,256,128]{3,2,1,0:T(8,128)(2,1)S(1)}, bf16[2,2,256,128]{3,2,1,0:T(8,128)(2,1)}, u32[]{:S(2)}) copy-start(bf16[2,2,256,128]{3,2,1,0:T(8,128)(2,1)} %get-tuple-element.143) | copy-start | bytes 786436
  84.5 8.7 %copy-start.34 = (s32[128]{0:T(128)S(1)}, s32[128]{0:T(128)}, u32[]{:S(2)}) copy-start(s32[128]{0:T(128)} %iota_subtract_fusion) | copy-start | bytes 1540
  138.0 229.5 %all-to-all-start = ((bf16[16,2,2,256,256]{3,4,2,1,0:T(8,128)(2,1)}), bf16[16,2,2,256,256]{3,4,2,1,0:T(8,128)(2,1)}, u32[]{:S(2)}, u32[]{:S(2)}) async-start(bf16[16,2,2,256,256]{3,4,2,1,0:T(8,128)(2,1)} %pad_maximum_fusion), calls=%async_computation | async-start | bytes 16777216 | tf_op jit(solution)/shard_map/all_to_all | solution.py:225
  143.4 6.9 copy-start.13
  143.4 7.0 copy-start.11
  148.7 92.9 %collective-permute-start = (f32[2,2048,256]{2,1,0:T(8,128)}, f32[2,2048,256]{2,1,0:T(8,128)}, u32[]{:S(2)}, u32[]{:S(2)}) collective-permute-start(f32[2,2048,256]{2,1,0:T(8,128)} %bitcast.586), channel_id=1, source_target_pairs={{0,16},{16,0},{1,17},{17,1},{2,18},{18,2},{3,19},{19,3},{4,20},{20... | collective-permute-start | bytes 12582920 | tf_op jit(solution)/shard_map/ppermute | solution.py:210
  153.8 5.6 copy-start.20
  153.8 5.6 copy-start.22
  331.9 5.8 copy-start.3
  395.0 7.7 %copy-start.18 = (f32[32,128]{0,1:T(8,128)S(1)}, f32[32,128]{0,1:T(8,128)}, u32[]{:S(2)}) copy-start(f32[32,128]{0,1:T(8,128)} %copy.185) | copy-start | bytes 49156
  395.0 7.7 %copy-start.19 = (f32[32,128]{0,1:T(8,128)S(1)}, f32[32,128]{0,1:T(8,128)}, u32[]{:S(2)}) copy-start(f32[32,128]{0,1:T(8,128)} %copy.186) | copy-start | bytes 49156
  405.8 34.3 %copy-start.2 = (f32[32,2,128,256]{3,0,2,1:T(8,128)}, f32[32,2,128,256]{3,0,2,1:T(8,128)S(1)}, u32[]{:S(2)}) copy-start(f32[32,2,128,256]{3,0,2,1:T(8,128)S(1)} %pad_maximum_fusion.2) | copy-start | bytes 25165828
  405.9 11.0 %copy-start.26 = (f32[1,2,16,128]{3,2,1,0:T(8,128)S(1)}, f32[1,2,16,128]{3,2,1,0:T(8,128)}, u32[]{:S(2)}) copy-start(f32[1,2,16,128]{3,2,1,0:T(8,128)} %get-tuple-element.179) | copy-start | bytes 49156
  405.9 11.0 %copy-start.27 = (f32[1,2,16,128]{3,2,1,0:T(8,128)S(1)}, f32[1,2,16,128]{3,2,1,0:T(8,128)}, u32[]{:S(2)}) copy-start(f32[1,2,16,128]{3,2,1,0:T(8,128)} %get-tuple-element.180) | copy-start | bytes 49156
  415.2 51.8 %collective-permute-start.1 = (f32[2,16,32,256]{3,1,2,0:T(8,128)S(1)}, f32[2,16,32,256]{3,1,2,0:T(8,128)S(1)}, u32[]{:S(2)}, u32[]{:S(2)}) collective-permute-start(f32[2,16,32,256]{3,1,2,0:T(8,128)S(1)} %fusion.57), channel_id=1, source_target_pairs={{0,16},{16,0},{1,17},{17,1},{2,18},{18,2},{3,19},{19,3},{4,20},{20... | collective-permute-start | bytes 3145736 | tf_op jit(solution)/shard_map/ppermute | solution.py:265
  416.8 11.3 %copy-start.28 = (f32[1,2,16,128]{3,2,1,0:T(8,128)S(1)}, f32[1,2,16,128]{3,2,1,0:T(8,128)}, u32[]{:S(2)}) copy-start(f32[1,2,16,128]{3,2,1,0:T(8,128)} %get-tuple-element.181) | copy-start | bytes 49156
  416.8 11.3 %copy-start.29 = (f32[1,2,16,128]{3,2,1,0:T(8,128)S(1)}, f32[1,2,16,128]{3,2,1,0:T(8,128)}, u32[]{:S(2)}) copy-start(f32[1,2,16,128]{3,2,1,0:T(8,128)} %get-tuple-element.182) | copy-start | bytes 49156
  427.6 39.5 %collective-permute-start.2 = (f32[2,16,32,256]{3,1,2,0:T(8,128)}, f32[2,16,32,256]{3,1,2,0:T(8,128)S(1)}, u32[]{:S(2)}, u32[]{:S(2)}) collective-permute-start(f32[2,16,32,256]{3,1,2,0:T(8,128)} %fusion.60), channel_id=1, source_target_pairs={{0,16},{16,0},{1,17},{17,1},{2,18},{18,2},{3,19},{19,3},{4,20},{20... | collective-permute-start | bytes 3145736 | tf_op jit(solution)/shard_map/ppermute | solution.py:265
  428.1 12.0 %copy-start.30 = (f32[1,2,16,128]{3,2,1,0:T(8,128)S(1)}, f32[1,2,16,128]{3,2,1,0:T(8,128)}, u32[]{:S(2)}) copy-start(f32[1,2,16,128]{3,2,1,0:T(8,128)} %get-tuple-element.183) | copy-start | bytes 49156
  428.1 12.0 %copy-start.31 = (f32[1,2,16,128]{3,2,1,0:T(8,128)S(1)}, f32[1,2,16,128]{3,2,1,0:T(8,128)}, u32[]{:S(2)}) copy-start(f32[1,2,16,128]{3,2,1,0:T(8,128)} %get-tuple-element.184) | copy-start | bytes 49156
  438.6 47.9 %collective-permute-start.3 = (f32[2,16,32,256]{3,1,2,0:T(8,128)}, f32[2,16,32,256]{3,1,2,0:T(8,128)}, u32[]{:S(2)}, u32[]{:S(2)}) collective-permute-start(f32[2,16,32,256]{3,1,2,0:T(8,128)} %fusion.63), channel_id=1, source_target_pairs={{0,16},{16,0},{1,17},{17,1},{2,18},{18,2},{3,19},{19,3},{4,20},{20... | collective-permute-start | bytes 3145736 | tf_op jit(solution)/shard_map/ppermute | solution.py:265
  450.6 56.6 %collective-permute-start.4 = (f32[2,16,32,256]{3,1,2,0:T(8,128)}, f32[2,16,32,256]{3,1,2,0:T(8,128)}, u32[]{:S(2)}, u32[]{:S(2)}) collective-permute-start(f32[2,16,32,256]{3,1,2,0:T(8,128)} %fusion.66), channel_id=1, source_target_pairs={{0,16},{16,0},{1,17},{17,1},{2,18},{18,2},{3,19},{19,3},{4,20},{20... | collective-permute-start | bytes 3145736 | tf_op jit(solution)/shard_map/ppermute | solution.py:265
  517.7 98.3 %all-to-all-start.2 = ((f32[2,16,128,256]{3,2,0,1:T(8,128)}), f32[2,16,128,256]{3,2,0,1:T(8,128)}, u32[]{:S(2)}, u32[]{:S(2)}) async-start(f32[2,16,128,256]{3,2,0,1:T(8,128)} %copy.194), calls=%async_computation.2 | async-start | bytes 8388608 | tf_op jit(solution)/shard_map/all_to_all | solution.py:274
  638.8 8.1 %copy-start.4 = (f32[32,2,128,128,1]{3,0,2,1,4:T(8,128)}, f32[32,2,128,128,1]{3,0,2,1,4:T(8,128)S(1)}, u32[]{:S(2)}) copy-start(f32[32,2,128,128,1]{3,0,2,1,4:T(8,128)S(1)} %maximum_bitcast_fusion.4) | copy-start | bytes 12582916
  639.9 14.0 %copy-start.6 = (f32[32,2,128,128,1]{3,0,2,1,4:T(8,128)}, f32[32,2,128,128,1]{3,0,2,1,4:T(8,128)S(1)}, u32[]{:S(2)}) copy-start(f32[32,2,128,128,1]{3,0,2,1,4:T(8,128)S(1)} %maximum_bitcast_fusion.5) | copy-start | bytes 12582916
  655.2 48.0 %collective-permute-start.5 = (f32[2,128,2048]{1,2,0:T(8,128)S(1)}, f32[2,128,2048]{1,2,0:T(8,128)}, u32[]{:S(2)}, u32[]{:S(2)}) collective-permute-start(f32[2,128,2048]{1,2,0:T(8,128)S(1)} %bitcast.587), channel_id=1, source_target_pairs={{0,16},{16,0},{1,17},{17,1},{2,18},{18,2},{3,19},{19,3},{4,20},{20... | collective-permute-start | bytes 6291464 | tf_op jit(solution)/shard_map/ppermute | solution.py:278
  656.8 8.5 %copy-start.5 = (f32[32,2,128,128,1]{3,0,2,1,4:T(8,128)S(1)}, f32[32,2,128,128,1]{3,0,2,1,4:T(8,128)}, u32[]{:S(2)}) copy-start(f32[32,2,128,128,1]{3,0,2,1,4:T(8,128)} %copy-done.4) | copy-start | bytes 12582916
  705.1 7.7 %copy-start.1 = (f32[4,2]{0,1:T(2,128)S(1)}, f32[4,2]{0,1:T(2,128)}, u32[]{:S(2)}) copy-start(f32[4,2]{0,1:T(2,128)} %param.23) | copy-start | bytes 100
  (13 other events, 21.9 us)
